TPU v7x, 256 devices: a whole 4x4x8 slice. The times are simulated.
256 devices in a mesh: section: 16 (over z_lo, x, core), tp: 16 (over y, z_hi).
Axes of the slice: x: 4, y: 4, z: 8 (z_hi: 4, z_lo: 2; z = z_hi * 2 + z_lo), core: 2. Of those that a mesh axis runs over, the one named last changes fastest.
Arguments:
- tokens: bfloat16 [2, 512, 4096], P(None, 'tp'), may hold values from -6 to 6
- norm_gains: float32 [2, 4096], replicated, may hold values from 0.1 to 1.9
- w_gate: bfloat16 [16, 4096, 2048], P('section', None, 'tp'), may hold values from -0.09375 to 0.09375
- w_up: bfloat16 [16, 4096, 2048], P('section', None, 'tp'), may hold values from -0.09375 to 0.09375
- w_down: bfloat16 [16, 2048, 4096], P('section', 'tp'), may hold values from -0.0625 to 0.0625
Outputs:
- acts: bfloat16 [16, 2, 512, 512], P('section', None, 'tp')
All inputs are finite; a program needn't handle non-finite values.
Results may differ from a plain program's by a relative error of at most 0.022.
Values may be sent and summed in bfloat16 or wider, within the bound.
No kernel may reach another device: no remote copies, remote signals or barrier semaphores. Data moves between devices by JAX's collectives and lax.ppermute only.
A program may use at most 64 MiB of HBM per device.

v0:
```python
import jax
import jax.numpy as jnp
from jax import lax
from jax.sharding import PartitionSpec as P

LAYERS = 2
PIECES = 1


epsilon = 1e-05


def swapped(value, axis, mask):
    pairs = [(source, source ^ mask) for source in range(lax.axis_size(axis))]
    return lax.ppermute(value, axis, pairs)


def tp_ring(value, inner, outer, stage, step):
    pairs = []
    for source in range(inner * outer):
        high, low = divmod(source, inner)
        if stage == "inner":
            target = high * inner + (low + step) % inner
        else:
            target = ((high + step) % outer) * inner + low
        pairs.append((source, target))
    return lax.ppermute(value, "tp", pairs)


def ring_gather(block, ring):
    half = block.shape[1] // 2
    from_left = ring(block, 1)
    from_right = ring(block, -1)
    opposite = jnp.concatenate(
        [ring(from_left[:, :half], 1), ring(from_right[:, half:], -1)], axis=1
    )
    return jnp.concatenate([block, from_right, opposite, from_left], axis=0)


def ring_scatter(groups, ring):
    rows = groups.shape[0] // 4
    half = groups.shape[1] // 2
    own, plus, opposite, minus = (groups[i * rows:(i + 1) * rows] for i in range(4))
    early_left = ring(opposite[:, :half], 1).astype(jnp.float32)
    early_right = ring(opposite[:, half:], -1).astype(jnp.float32)
    to_right = jnp.concatenate(
        [(plus[:, :half].astype(jnp.float32) + early_left).astype(jnp.bfloat16), plus[:, half:]], axis=1
    )
    to_left = jnp.concatenate(
        [minus[:, :half], (minus[:, half:].astype(jnp.float32) + early_right).astype(jnp.bfloat16)], axis=1
    )
    return (
        own.astype(jnp.float32)
        + ring(to_right, 1).astype(jnp.float32)
        + ring(to_left, -1).astype(jnp.float32)
    )


def direct_gather(block, ring):
    return jnp.concatenate([block, ring(block, -1), ring(block, 2), ring(block, 1)], axis=0)


def direct_scatter(groups, ring):
    rows = groups.shape[0] // 4
    own, plus, opposite, minus = (groups[i * rows:(i + 1) * rows] for i in range(4))
    return (
        own.astype(jnp.float32)
        + ring(plus, 1).astype(jnp.float32)
        + ring(opposite, 2).astype(jnp.float32)
        + ring(minus, -1).astype(jnp.float32)
    )


def shifted(value, axis, steps):
    count = lax.axis_size(axis)
    return lax.ppermute(value, axis, [(source, source + steps) for source in range(count - steps)])


def body(tokens, norm_gains, w_gate, w_up, w_down):
    section_count = lax.axis_size("section")
    split = section_count // LAYERS
    bit_count = split.bit_length() - 1
    position = lax.axis_index("section")
    section_layer = position // split
    member = position % split
    core = member % 2
    xpos = member // 2
    x_count = split // 2

    tp_count = lax.axis_size("tp")
    inner = 4
    outer = tp_count // inner

    def inner_ring(value, step):
        return tp_ring(value, inner, outer, "inner", step)

    def outer_ring(value, step):
        return tp_ring(value, inner, outer, "outer", step)

    micro_count, tok_dev, model_width = tokens.shape
    piece_width = model_width // split
    half_width = model_width // 2
    row_count = tok_dev // PIECES
    piece_count = micro_count * PIECES
    tick_count = piece_count + LAYERS - 1

    def pick(value, axis, which):
        shape = value.shape
        grouped = value.reshape(shape[:axis] + (x_count, 2, piece_width) + shape[axis + 1:])
        chosen = lax.dynamic_index_in_dim(grouped, which, axis + 1, keepdims=False)
        return chosen.reshape(shape[:axis] + (half_width,) + shape[axis + 1:])

    other = 1 - core
    gate_own = pick(w_gate[0], 0, core)
    gate_other = pick(w_gate[0], 0, other)
    up_own = pick(w_up[0], 0, core)
    up_other = pick(w_up[0], 0, other)
    down_own = pick(w_down[0], 1, core)
    down_other = pick(w_down[0], 1, other)
    norm_gain = lax.dynamic_index_in_dim(norm_gains, section_layer, 0, keepdims=False)
    gain_own = pick(norm_gain, 0, core)

    def from_tokens(piece_index):
        micro_index, part = divmod(piece_index, PIECES)
        rows = tokens[micro_index, part * row_count:(part + 1) * row_count].astype(jnp.float32)
        return pick(rows, 1, core), jnp.sum(rows * rows, axis=1, keepdims=True)

    def from_received(received):
        current = received.astype(jnp.float32)
        own_sq = jnp.sum(current * current, axis=1, keepdims=True)
        return current, own_sq + swapped(own_sq, "section", 1)

    def tick(current, square_sum):
        inv_rms = lax.rsqrt(square_sum / model_width + epsilon)
        normed = (current * inv_rms * gain_own).astype(jnp.bfloat16)
        gathered = ring_gather(direct_gather(normed, inner_ring), outer_ring)
        gathered_other = swapped(gathered, "section", 1)
        gate_proj = jnp.dot(gathered, gate_own, preferred_element_type=jnp.float32) + jnp.dot(
            gathered_other, gate_other, preferred_element_type=jnp.float32
        )
        up_proj = jnp.dot(gathered, up_own, preferred_element_type=jnp.float32) + jnp.dot(
            gathered_other, up_other, preferred_element_type=jnp.float32
        )
        active = (jax.nn.silu(gate_proj) * up_proj).astype(jnp.bfloat16)
        part_other = jnp.dot(active, down_other, preferred_element_type=jnp.float32).astype(jnp.bfloat16)
        part_from_other = swapped(part_other, "section", 1)
        part_own = jnp.dot(active, down_own, preferred_element_type=jnp.float32).astype(jnp.bfloat16)
        pair = (part_own.astype(jnp.float32) + part_from_other.astype(jnp.float32)).astype(jnp.bfloat16)
        summed = direct_scatter(ring_scatter(pair, outer_ring).astype(jnp.bfloat16), inner_ring).astype(jnp.bfloat16)
        summed = summed.astype(jnp.float32) + sum(
            swapped(summed, "section", 2 * mask).astype(jnp.float32) for mask in range(1, x_count)
        )
        full_half = (current + summed.astype(jnp.float32)).astype(jnp.bfloat16)
        block = lax.dynamic_index_in_dim(
            full_half.reshape(row_count, x_count, piece_width), xpos, 1, keepdims=False
        )
        return full_half, block

    blocks = []
    received = None
    for tick_index in range(tick_count):
        if tick_index == 0:
            current, square_sum = from_tokens(0)
        elif tick_index >= piece_count:
            current, square_sum = from_received(received)
        else:
            first_current, first_sum = from_tokens(tick_index)
            later_current, later_sum = from_received(received)
            is_first = section_layer == 0
            current = jnp.where(is_first, first_current, later_current)
            square_sum = jnp.where(is_first, first_sum, later_sum)
        full_half, block = tick(current, square_sum)
        blocks.append(block)
        if tick_index < tick_count - 1:
            received = shifted(full_half, "section", split)

    stacked = jnp.stack(blocks, axis=0)
    outputs = []
    for micro_index in range(micro_count):
        parts = [
            lax.dynamic_index_in_dim(stacked, micro_index * PIECES + part + section_layer, 0, keepdims=False)
            for part in range(PIECES)
        ]
        outputs.append(jnp.concatenate(parts, axis=0))
    return jnp.stack(outputs, axis=0)[None]


def solution(mesh):
    in_specs = (
        P(None, "tp", None),
        P(),
        P("section", None, "tp"),
        P("section", None, "tp"),
        P("section", "tp", None),
    )
    out_specs = P("section", None, "tp", None)
    return jax.shard_map(body, mesh=mesh, in_specs=in_specs, out_specs=out_specs, check_vma=False)
```

profile of v0, /device:TPU:32, one launch (start us, length us, event | category | flops | bytes accessed | tf_op | source)
XLA Modules:
  0.0 351.2 jit_solution(5048350283182236129)
XLA Ops:
  6.4 5.4 %collective-permute-start = (bf16[32,2048]{1,0:T(8,128)(2,1)S(1)}, bf16[32,2048]{1,0:T(8,128)(2,1)S(1)}, u32[]{:S(2)}, u32[]{:S(2)}) collective-permute-start(bf16[32,2048]{1,0:T(8,128)(2,1)S(1)} %get-tuple-element.12), channel_id=1, source_target_pairs={{0,3},{1,0},{2,1},{3,2},{4,7},{5,4},{6,5},{7,6},{8,11},{9,8},{10,9... | collective-permute-start | bytes 393224 | tf_op jit(solution)/shard_map/ppermute | solution.py:27
  17.7 7.5 %collective-permute-done.1 = bf16[32,2048]{1,0:T(8,128)(2,1)S(1)} collective-permute-done((bf16[32,2048]{1,0:T(8,128)(2,1)S(1)}, bf16[32,2048]{1,0:T(8,128)(2,1)S(1)}, u32[]{:S(2)}, u32[]{:S(2)}) %collective-permute-start.1) | collective-permute-done | bytes 131104 | tf_op jit(solution)/shard_map/ppermute | solution.py:27
  30.1 9.5 %collective-permute-done.3 = bf16[128,2048]{1,0:T(8,128)(2,1)S(1)} collective-permute-done((bf16[128,2048]{1,0:T(8,128)(2,1)S(1)}, bf16[128,2048]{1,0:T(8,128)(2,1)S(1)}, u32[]{:S(2)}, u32[]{:S(2)}) %collective-permute-start.3) | collective-permute-done | bytes 524320 | tf_op jit(solution)/shard_map/ppermute | solution.py:27
  39.6 3.8 %collective-permute-start.6 = (bf16[128,1024]{1,0:T(8,128)(2,1)S(1)}, bf16[128,1024]{1,0:T(8,128)(2,1)S(1)}, u32[]{:S(2)}, u32[]{:S(2)}) collective-permute-start(bf16[128,1024]{1,0:T(8,128)(2,1)S(1)} %slice.192), channel_id=1, source_target_pairs={{0,12},{1,13},{2,14},{3,15},{4,0},{5,1},{6,2},{7,3},{8,4},{9,5},{1... | collective-permute-start | bytes 786440 | tf_op jit(solution)/shard_map/ppermute | solution.py:27
  65.9 3.8 %collective-permute-done.8 = bf16[512,2048]{1,0:T(8,128)(2,1)S(1)} collective-permute-done((bf16[512,2048]{1,0:T(8,128)(2,1)S(1)}, bf16[512,2048]{1,0:T(8,128)(2,1)S(1)}, u32[]{:S(2)}, u32[]{:S(2)}) %collective-permute-start.8) | collective-permute-done | bytes 2097184 | tf_op jit(solution)/shard_map/ppermute | solution.py:15
  73.8 6.6 %collective-permute-done.9 = bf16[128,1024]{1,0:T(8,128)(2,1)S(1)} collective-permute-done((bf16[128,1024]{1,0:T(8,128)(2,1)S(1)}, bf16[128,1024]{1,0:T(8,128)(2,1)S(1)}, u32[]{:S(2)}, u32[]{:S(2)}) %collective-permute-start.9) | collective-permute-done | bytes 262176 | tf_op jit(solution)/shard_map/ppermute | solution.py:27
  83.8 10.4 %collective-permute-done.12 = bf16[128,2048]{1,0:T(8,128)(2,1)S(1)} collective-permute-done((bf16[128,2048]{1,0:T(8,128)(2,1)S(1)}, bf16[128,2048]{1,0:T(8,128)(2,1)S(1)}, u32[]{:S(2)}, u32[]{:S(2)}) %collective-permute-start.12) | collective-permute-done | bytes 524320 | tf_op jit(solution)/shard_map/ppermute | solution.py:27
  94.2 3.5 %collective-permute-done.10 = bf16[128,2048]{1,0:T(8,128)(2,1)S(1)} collective-permute-done((bf16[128,2048]{1,0:T(8,128)(2,1)S(1)}, bf16[128,2048]{1,0:T(8,128)(2,1)S(1)}, u32[]{:S(2)}, u32[]{:S(2)}) %collective-permute-start.10) | collective-permute-done | bytes 524320 | tf_op jit(solution)/shard_map/ppermute | solution.py:27
  98.1 4.4 %collective-permute-start.15 = (bf16[32,2048]{1,0:T(8,128)(2,1)S(1)}, bf16[32,2048]{1,0:T(8,128)(2,1)S(1)}, u32[]{:S(2)}, u32[]{:S(2)}) collective-permute-start(bf16[32,2048]{1,0:T(8,128)(2,1)S(1)} %get-tuple-element.46), channel_id=1, source_target_pairs={{0,3},{1,0},{2,1},{3,2},{4,7},{5,4},{6,5},{7,6},{8,11},{9,8},{10,9... | collective-permute-start | bytes 393224 | tf_op jit(solution)/shard_map/ppermute | solution.py:27
  107.5 7.0 %collective-permute-done.14 = bf16[32,2048]{1,0:T(8,128)(2,1)S(1)} collective-permute-done((bf16[32,2048]{1,0:T(8,128)(2,1)S(1)}, bf16[32,2048]{1,0:T(8,128)(2,1)S(1)}, u32[]{:S(2)}, u32[]{:S(2)}) %collective-permute-start.14) | collective-permute-done | bytes 131104 | tf_op jit(solution)/shard_map/ppermute | solution.py:27
  119.1 4.1 %collective-permute-done.18 = bf16[32,2048]{1,0:T(8,128)(2,1)S(1)} collective-permute-done((bf16[32,2048]{1,0:T(8,128)(2,1)S(1)}, bf16[32,2048]{1,0:T(8,128)(2,1)S(1)}, u32[]{:S(2)}, u32[]{:S(2)}) %collective-permute-start.18) | collective-permute-done | bytes 131104 | tf_op jit(solution)/shard_map/ppermute | solution.py:15
  126.7 5.6 %collective-permute-done.19 = bf16[32,2048]{1,0:T(8,128)(2,1)S(1)} collective-permute-done((bf16[32,2048]{1,0:T(8,128)(2,1)S(1)}, bf16[32,2048]{1,0:T(8,128)(2,1)S(1)}, u32[]{:S(2)}, u32[]{:S(2)}) %collective-permute-start.19) | collective-permute-done | bytes 131104 | tf_op jit(solution)/shard_map/ppermute | solution.py:76
  143.8 4.6 %collective-permute-done.22 = bf16[32,2048]{1,0:T(8,128)(2,1)S(1)} collective-permute-done((bf16[32,2048]{1,0:T(8,128)(2,1)S(1)}, bf16[32,2048]{1,0:T(8,128)(2,1)S(1)}, u32[]{:S(2)}, u32[]{:S(2)}) %collective-permute-start.22) | collective-permute-done | bytes 131104 | tf_op jit(solution)/shard_map/ppermute | solution.py:27
  153.3 11.8 %collective-permute-done.24 = bf16[128,2048]{1,0:T(8,128)(2,1)S(1)} collective-permute-done((bf16[128,2048]{1,0:T(8,128)(2,1)S(1)}, bf16[128,2048]{1,0:T(8,128)(2,1)S(1)}, u32[]{:S(2)}, u32[]{:S(2)}) %collective-permute-start.24) | collective-permute-done | bytes 524320 | tf_op jit(solution)/shard_map/ppermute | solution.py:27
  167.4 5.2 %collective-permute-done.27 = bf16[128,1024]{1,0:T(8,128)(2,1)S(1)} collective-permute-done((bf16[128,1024]{1,0:T(8,128)(2,1)S(1)}, bf16[128,1024]{1,0:T(8,128)(2,1)S(1)}, u32[]{:S(2)}, u32[]{:S(2)}) %collective-permute-start.27) | collective-permute-done | bytes 262176 | tf_op jit(solution)/shard_map/ppermute | solution.py:27
  175.4 4.1 %collective-permute-done.28 = bf16[512,2048]{1,0:T(8,128)(2,1)S(1)} collective-permute-done((bf16[512,2048]{1,0:T(8,128)(2,1)S(1)}, bf16[512,2048]{1,0:T(8,128)(2,1)S(1)}, u32[]{:S(2)}, u32[]{:S(2)}) %collective-permute-start.28) | collective-permute-done | bytes 2097184 | tf_op jit(solution)/shard_map/ppermute | solution.py:15
  184.0 4.0 %collective-permute-done.29 = bf16[512,2048]{1,0:T(8,128)(2,1)S(1)} collective-permute-done((bf16[512,2048]{1,0:T(8,128)(2,1)S(1)}, bf16[512,2048]{1,0:T(8,128)(2,1)S(1)}, u32[]{:S(2)}, u32[]{:S(2)}) %collective-permute-start.29) | collective-permute-done | bytes 2097184 | tf_op jit(solution)/shard_map/ppermute | solution.py:15
  192.3 6.2 %collective-permute-done.30 = bf16[128,1024]{1,0:T(8,128)(2,1)S(1)} collective-permute-done((bf16[128,1024]{1,0:T(8,128)(2,1)S(1)}, bf16[128,1024]{1,0:T(8,128)(2,1)S(1)}, u32[]{:S(2)}, u32[]{:S(2)}) %collective-permute-start.30) | collective-permute-done | bytes 262176 | tf_op jit(solution)/shard_map/ppermute | solution.py:27
  202.1 10.2 %collective-permute-done.33 = bf16[128,2048]{1,0:T(8,128)(2,1)S(1)} collective-permute-done((bf16[128,2048]{1,0:T(8,128)(2,1)S(1)}, bf16[128,2048]{1,0:T(8,128)(2,1)S(1)}, u32[]{:S(2)}, u32[]{:S(2)}) %collective-permute-start.33) | collective-permute-done | bytes 524320 | tf_op jit(solution)/shard_map/ppermute | solution.py:27
  223.3 5.9 %collective-permute-done.35 = bf16[32,2048]{1,0:T(8,128)(2,1)S(1)} collective-permute-done((bf16[32,2048]{1,0:T(8,128)(2,1)S(1)}, bf16[32,2048]{1,0:T(8,128)(2,1)S(1)}, u32[]{:S(2)}, u32[]{:S(2)}) %collective-permute-start.35) | collective-permute-done | bytes 131104 | tf_op jit(solution)/shard_map/ppermute | solution.py:27
  239.5 5.6 %collective-permute-done.40 = bf16[32,2048]{1,0:T(8,128)(2,1)S(1)} collective-permute-done((bf16[32,2048]{1,0:T(8,128)(2,1)S(1)}, bf16[32,2048]{1,0:T(8,128)(2,1)S(1)}, u32[]{:S(2)}, u32[]{:S(2)}) %collective-permute-start.40) | collective-permute-done | bytes 131104 | tf_op jit(solution)/shard_map/ppermute | solution.py:76
  247.7 4.7 %collective-permute-start.43 = (bf16[32,2048]{1,0:T(8,128)(2,1)S(1)}, bf16[32,2048]{1,0:T(8,128)(2,1)S(1)}, u32[]{:S(2)}, u32[]{:S(2)}) collective-permute-start(bf16[32,2048]{1,0:T(8,128)(2,1)S(1)} %get-tuple-element.8), channel_id=1, source_target_pairs={{0,2},{1,3},{2,0},{3,1},{4,6},{5,7},{6,4},{7,5},{8,10},{9,11},{10,... | collective-permute-start | bytes 393224 | tf_op jit(solution)/shard_map/ppermute | solution.py:27
  252.9 3.8 %collective-permute-done.42 = bf16[32,2048]{1,0:T(8,128)(2,1)S(1)} collective-permute-done((bf16[32,2048]{1,0:T(8,128)(2,1)S(1)}, bf16[32,2048]{1,0:T(8,128)(2,1)S(1)}, u32[]{:S(2)}, u32[]{:S(2)}) %collective-permute-start.42) | collective-permute-done | bytes 131104 | tf_op jit(solution)/shard_map/ppermute | solution.py:27
  256.7 5.3 %collective-permute-done.43 = bf16[32,2048]{1,0:T(8,128)(2,1)S(1)} collective-permute-done((bf16[32,2048]{1,0:T(8,128)(2,1)S(1)}, bf16[32,2048]{1,0:T(8,128)(2,1)S(1)}, u32[]{:S(2)}, u32[]{:S(2)}) %collective-permute-start.43) | collective-permute-done | bytes 131104 | tf_op jit(solution)/shard_map/ppermute | solution.py:27
  266.1 11.8 %collective-permute-done.45 = bf16[128,2048]{1,0:T(8,128)(2,1)S(1)} collective-permute-done((bf16[128,2048]{1,0:T(8,128)(2,1)S(1)}, bf16[128,2048]{1,0:T(8,128)(2,1)S(1)}, u32[]{:S(2)}, u32[]{:S(2)}) %collective-permute-start.45) | collective-permute-done | bytes 524320 | tf_op jit(solution)/shard_map/ppermute | solution.py:27
  280.4 5.0 %collective-permute-done.48 = bf16[128,1024]{1,0:T(8,128)(2,1)S(1)} collective-permute-done((bf16[128,1024]{1,0:T(8,128)(2,1)S(1)}, bf16[128,1024]{1,0:T(8,128)(2,1)S(1)}, u32[]{:S(2)}, u32[]{:S(2)}) %collective-permute-start.48) | collective-permute-done | bytes 262176 | tf_op jit(solution)/shard_map/ppermute | solution.py:27
  288.4 4.1 %collective-permute-done.49 = bf16[512,2048]{1,0:T(8,128)(2,1)S(1)} collective-permute-done((bf16[512,2048]{1,0:T(8,128)(2,1)S(1)}, bf16[512,2048]{1,0:T(8,128)(2,1)S(1)}, u32[]{:S(2)}, u32[]{:S(2)}) %collective-permute-start.49) | collective-permute-done | bytes 2097184 | tf_op jit(solution)/shard_map/ppermute | solution.py:15
  296.4 4.0 %collective-permute-done.50 = bf16[512,2048]{1,0:T(8,128)(2,1)S(1)} collective-permute-done((bf16[512,2048]{1,0:T(8,128)(2,1)S(1)}, bf16[512,2048]{1,0:T(8,128)(2,1)S(1)}, u32[]{:S(2)}, u32[]{:S(2)}) %collective-permute-start.50) | collective-permute-done | bytes 2097184 | tf_op jit(solution)/shard_map/ppermute | solution.py:15
  304.6 6.3 %collective-permute-done.51 = bf16[128,1024]{1,0:T(8,128)(2,1)S(1)} collective-permute-done((bf16[128,1024]{1,0:T(8,128)(2,1)S(1)}, bf16[128,1024]{1,0:T(8,128)(2,1)S(1)}, u32[]{:S(2)}, u32[]{:S(2)}) %collective-permute-start.51) | collective-permute-done | bytes 262176 | tf_op jit(solution)/shard_map/ppermute | solution.py:27
  314.3 10.2 %collective-permute-done.54 = bf16[128,2048]{1,0:T(8,128)(2,1)S(1)} collective-permute-done((bf16[128,2048]{1,0:T(8,128)(2,1)S(1)}, bf16[128,2048]{1,0:T(8,128)(2,1)S(1)}, u32[]{:S(2)}, u32[]{:S(2)}) %collective-permute-start.54) | collective-permute-done | bytes 524320 | tf_op jit(solution)/shard_map/ppermute | solution.py:27
  329.3 4.7 %collective-permute-start.56 = (bf16[32,2048]{1,0:T(8,128)(2,1)S(1)}, bf16[32,2048]{1,0:T(8,128)(2,1)S(1)}, u32[]{:S(2)}, u32[]{:S(2)}) collective-permute-start(bf16[32,2048]{1,0:T(8,128)(2,1)S(1)} %get-tuple-element.39), channel_id=1, source_target_pairs={{0,2},{1,3},{2,0},{3,1},{4,6},{5,7},{6,4},{7,5},{8,10},{9,11},{10,... | collective-permute-start | bytes 393224 | tf_op jit(solution)/shard_map/ppermute | solution.py:27
  337.0 3.9 %collective-permute-done.56 = bf16[32,2048]{1,0:T(8,128)(2,1)S(1)} collective-permute-done((bf16[32,2048]{1,0:T(8,128)(2,1)S(1)}, bf16[32,2048]{1,0:T(8,128)(2,1)S(1)}, u32[]{:S(2)}, u32[]{:S(2)}) %collective-permute-start.56) | collective-permute-done | bytes 131104 | tf_op jit(solution)/shard_map/ppermute | solution.py:27
  (214 shorter events, 157.1 us)
Async XLA Ops:
  6.4 11.3 %collective-permute-start = (bf16[32,2048]{1,0:T(8,128)(2,1)S(1)}, bf16[32,2048]{1,0:T(8,128)(2,1)S(1)}, u32[]{:S(2)}, u32[]{:S(2)}) collective-permute-start(bf16[32,2048]{1,0:T(8,128)(2,1)S(1)} %get-tuple-element.12), channel_id=1, source_target_pairs={{0,3},{1,0},{2,1},{3,2},{4,7},{5,4},{6,5},{7,6},{8,11},{9,8},{10,9... | collective-permute-start | bytes 393224 | tf_op jit(solution)/shard_map/ppermute | solution.py:27
  11.8 13.4 %collective-permute-start.1 = (bf16[32,2048]{1,0:T(8,128)(2,1)S(1)}, bf16[32,2048]{1,0:T(8,128)(2,1)S(1)}, u32[]{:S(2)}, u32[]{:S(2)}) collective-permute-start(bf16[32,2048]{1,0:T(8,128)(2,1)S(1)} %get-tuple-element.12), channel_id=1, source_target_pairs={{0,2},{1,3},{2,0},{3,1},{4,6},{5,7},{6,4},{7,5},{8,10},{9,11},{10,... | collective-permute-start | bytes 393224 | tf_op jit(solution)/shard_map/ppermute | solution.py:27
  13.2 12.4 %collective-permute-start.2 = (bf16[32,2048]{1,0:T(8,128)(2,1)S(1)}, bf16[32,2048]{1,0:T(8,128)(2,1)S(1)}, u32[]{:S(2)}, u32[]{:S(2)}) collective-permute-start(bf16[32,2048]{1,0:T(8,128)(2,1)S(1)} %get-tuple-element.12), channel_id=1, source_target_pairs={{0,1},{1,2},{2,3},{3,0},{4,5},{5,6},{6,7},{7,4},{8,9},{9,10},{10,1... | collective-permute-start | bytes 393224 | tf_op jit(solution)/shard_map/ppermute | solution.py:27
  25.7 13.9 %collective-permute-start.3 = (bf16[128,2048]{1,0:T(8,128)(2,1)S(1)}, bf16[128,2048]{1,0:T(8,128)(2,1)S(1)}, u32[]{:S(2)}, u32[]{:S(2)}) collective-permute-start(bf16[128,2048]{1,0:T(8,128)(2,1)S(1)} %pad_maximum_fusion), channel_id=1, source_target_pairs={{0,12},{1,13},{2,14},{3,15},{4,0},{5,1},{6,2},{7,3},{8,4},{9,5},{1... | collective-permute-start | bytes 1572872 | tf_op jit(solution)/shard_map/ppermute | solution.py:27
  28.8 14.6 %collective-permute-start.4 = (bf16[128,2048]{1,0:T(8,128)(2,1)S(1)}, bf16[128,2048]{1,0:T(8,128)(2,1)S(1)}, u32[]{:S(2)}, u32[]{:S(2)}) collective-permute-start(bf16[128,2048]{1,0:T(8,128)(2,1)S(1)} %pad_maximum_fusion), channel_id=1, source_target_pairs={{0,4},{1,5},{2,6},{3,7},{4,8},{5,9},{6,10},{7,11},{8,12},{9,13},{1... | collective-permute-start | bytes 1572872 | tf_op jit(solution)/shard_map/ppermute | solution.py:27
  70.5 9.9 %collective-permute-start.9 = (bf16[128,1024]{1,0:T(8,128)(2,1)S(1)}, bf16[128,1024]{1,0:T(8,128)(2,1)S(1)}, u32[]{:S(2)}, u32[]{:S(2)}) collective-permute-start(bf16[128,1024]{1,0:T(8,128)(2,1)S(1)} %get-tuple-element.27), channel_id=1, source_target_pairs={{0,4},{1,5},{2,6},{3,7},{4,8},{5,9},{6,10},{7,11},{8,12},{9,13},{1... | collective-permute-start | bytes 786440 | tf_op jit(solution)/shard_map/ppermute | solution.py:27
  70.6 9.8 %collective-permute-start.11 = (bf16[128,1024]{1,0:T(8,128)(2,1)S(1)}, bf16[128,1024]{1,0:T(8,128)(2,1)S(1)}, u32[]{:S(2)}, u32[]{:S(2)}) collective-permute-start(bf16[128,1024]{1,0:T(8,128)(2,1)S(1)} %get-tuple-element.28), channel_id=1, source_target_pairs={{0,12},{1,13},{2,14},{3,15},{4,0},{5,1},{6,2},{7,3},{8,4},{9,5},{1... | collective-permute-start | bytes 786440 | tf_op jit(solution)/shard_map/ppermute | solution.py:27
  80.6 13.6 %collective-permute-start.12 = (bf16[128,2048]{1,0:T(8,128)(2,1)S(1)}, bf16[128,2048]{1,0:T(8,128)(2,1)S(1)}, u32[]{:S(2)}, u32[]{:S(2)}) collective-permute-start(bf16[128,2048]{1,0:T(8,128)(2,1)S(1)} %pad_maximum_fusion.2), channel_id=1, source_target_pairs={{0,12},{1,13},{2,14},{3,15},{4,0},{5,1},{6,2},{7,3},{8,4},{9,5},{1... | collective-permute-start | bytes 1572872 | tf_op jit(solution)/shard_map/ppermute | solution.py:27
  83.7 14.1 %collective-permute-start.10 = (bf16[128,2048]{1,0:T(8,128)(2,1)S(1)}, bf16[128,2048]{1,0:T(8,128)(2,1)S(1)}, u32[]{:S(2)}, u32[]{:S(2)}) collective-permute-start(bf16[128,2048]{1,0:T(8,128)(2,1)S(1)} %pad_maximum_fusion.1), channel_id=1, source_target_pairs={{0,4},{1,5},{2,6},{3,7},{4,8},{5,9},{6,10},{7,11},{8,12},{9,13},{1... | collective-permute-start | bytes 1572872 | tf_op jit(solution)/shard_map/ppermute | solution.py:27
  98.1 9.4 %collective-permute-start.15 = (bf16[32,2048]{1,0:T(8,128)(2,1)S(1)}, bf16[32,2048]{1,0:T(8,128)(2,1)S(1)}, u32[]{:S(2)}, u32[]{:S(2)}) collective-permute-start(bf16[32,2048]{1,0:T(8,128)(2,1)S(1)} %get-tuple-element.46), channel_id=1, source_target_pairs={{0,3},{1,0},{2,1},{3,2},{4,7},{5,4},{6,5},{7,6},{8,11},{9,8},{10,9... | collective-permute-start | bytes 393224 | tf_op jit(solution)/shard_map/ppermute | solution.py:27
  102.5 12.0 %collective-permute-start.14 = (bf16[32,2048]{1,0:T(8,128)(2,1)S(1)}, bf16[32,2048]{1,0:T(8,128)(2,1)S(1)}, u32[]{:S(2)}, u32[]{:S(2)}) collective-permute-start(bf16[32,2048]{1,0:T(8,128)(2,1)S(1)} %get-tuple-element.47), channel_id=1, source_target_pairs={{0,2},{1,3},{2,0},{3,1},{4,6},{5,7},{6,4},{7,5},{8,10},{9,11},{10,... | collective-permute-start | bytes 393224 | tf_op jit(solution)/shard_map/ppermute | solution.py:27
  104.6 9.9 %collective-permute-start.13 = (bf16[32,2048]{1,0:T(8,128)(2,1)S(1)}, bf16[32,2048]{1,0:T(8,128)(2,1)S(1)}, u32[]{:S(2)}, u32[]{:S(2)}) collective-permute-start(bf16[32,2048]{1,0:T(8,128)(2,1)S(1)} %get-tuple-element.45), channel_id=1, source_target_pairs={{0,1},{1,2},{2,3},{3,0},{4,5},{5,6},{6,7},{7,4},{8,9},{9,10},{10,1... | collective-permute-start | bytes 393224 | tf_op jit(solution)/shard_map/ppermute | solution.py:27
  133.7 10.1 %collective-permute-start.21 = (bf16[32,2048]{1,0:T(8,128)(2,1)S(1)}, bf16[32,2048]{1,0:T(8,128)(2,1)S(1)}, u32[]{:S(2)}, u32[]{:S(2)}) collective-permute-start(bf16[32,2048]{1,0:T(8,128)(2,1)S(1)} %get-tuple-element.10), channel_id=1, source_target_pairs={{0,3},{1,0},{2,1},{3,2},{4,7},{5,4},{6,5},{7,6},{8,11},{9,8},{10,9... | collective-permute-start | bytes 393224 | tf_op jit(solution)/shard_map/ppermute | solution.py:27
  135.8 12.6 %collective-permute-start.22 = (bf16[32,2048]{1,0:T(8,128)(2,1)S(1)}, bf16[32,2048]{1,0:T(8,128)(2,1)S(1)}, u32[]{:S(2)}, u32[]{:S(2)}) collective-permute-start(bf16[32,2048]{1,0:T(8,128)(2,1)S(1)} %get-tuple-element.10), channel_id=1, source_target_pairs={{0,2},{1,3},{2,0},{3,1},{4,6},{5,7},{6,4},{7,5},{8,10},{9,11},{10,... | collective-permute-start | bytes 393224 | tf_op jit(solution)/shard_map/ppermute | solution.py:27
  139.3 11.8 %collective-permute-start.23 = (bf16[32,2048]{1,0:T(8,128)(2,1)S(1)}, bf16[32,2048]{1,0:T(8,128)(2,1)S(1)}, u32[]{:S(2)}, u32[]{:S(2)}) collective-permute-start(bf16[32,2048]{1,0:T(8,128)(2,1)S(1)} %get-tuple-element.10), channel_id=1, source_target_pairs={{0,1},{1,2},{2,3},{3,0},{4,5},{5,6},{6,7},{7,4},{8,9},{9,10},{10,1... | collective-permute-start | bytes 393224 | tf_op jit(solution)/shard_map/ppermute | solution.py:27
  151.1 13.9 %collective-permute-start.24 = (bf16[128,2048]{1,0:T(8,128)(2,1)S(1)}, bf16[128,2048]{1,0:T(8,128)(2,1)S(1)}, u32[]{:S(2)}, u32[]{:S(2)}) collective-permute-start(bf16[128,2048]{1,0:T(8,128)(2,1)S(1)} %pad_maximum_fusion.3), channel_id=1, source_target_pairs={{0,12},{1,13},{2,14},{3,15},{4,0},{5,1},{6,2},{7,3},{8,4},{9,5},{1... | collective-permute-start | bytes 1572872 | tf_op jit(solution)/shard_map/ppermute | solution.py:27
  151.7 15.2 %collective-permute-start.25 = (bf16[128,2048]{1,0:T(8,128)(2,1)S(1)}, bf16[128,2048]{1,0:T(8,128)(2,1)S(1)}, u32[]{:S(2)}, u32[]{:S(2)}) collective-permute-start(bf16[128,2048]{1,0:T(8,128)(2,1)S(1)} %pad_maximum_fusion.3), channel_id=1, source_target_pairs={{0,4},{1,5},{2,6},{3,7},{4,8},{5,9},{6,10},{7,11},{8,12},{9,13},{1... | collective-permute-start | bytes 1572872 | tf_op jit(solution)/shard_map/ppermute | solution.py:27
  188.9 9.6 %collective-permute-start.30 = (bf16[128,1024]{1,0:T(8,128)(2,1)S(1)}, bf16[128,1024]{1,0:T(8,128)(2,1)S(1)}, u32[]{:S(2)}, u32[]{:S(2)}) collective-permute-start(bf16[128,1024]{1,0:T(8,128)(2,1)S(1)} %get-tuple-element.21), channel_id=1, source_target_pairs={{0,4},{1,5},{2,6},{3,7},{4,8},{5,9},{6,10},{7,11},{8,12},{9,13},{1... | collective-permute-start | bytes 786440 | tf_op jit(solution)/shard_map/ppermute | solution.py:27
  188.9 9.6 %collective-permute-start.32 = (bf16[128,1024]{1,0:T(8,128)(2,1)S(1)}, bf16[128,1024]{1,0:T(8,128)(2,1)S(1)}, u32[]{:S(2)}, u32[]{:S(2)}) collective-permute-start(bf16[128,1024]{1,0:T(8,128)(2,1)S(1)} %get-tuple-element.22), channel_id=1, source_target_pairs={{0,12},{1,13},{2,14},{3,15},{4,0},{5,1},{6,2},{7,3},{8,4},{9,5},{1... | collective-permute-start | bytes 786440 | tf_op jit(solution)/shard_map/ppermute | solution.py:27
  198.7 13.5 %collective-permute-start.33 = (bf16[128,2048]{1,0:T(8,128)(2,1)S(1)}, bf16[128,2048]{1,0:T(8,128)(2,1)S(1)}, u32[]{:S(2)}, u32[]{:S(2)}) collective-permute-start(bf16[128,2048]{1,0:T(8,128)(2,1)S(1)} %pad_maximum_fusion.5), channel_id=1, source_target_pairs={{0,12},{1,13},{2,14},{3,15},{4,0},{5,1},{6,2},{7,3},{8,4},{9,5},{1... | collective-permute-start | bytes 1572872 | tf_op jit(solution)/shard_map/ppermute | solution.py:27
  202.0 13.8 %collective-permute-start.31 = (bf16[128,2048]{1,0:T(8,128)(2,1)S(1)}, bf16[128,2048]{1,0:T(8,128)(2,1)S(1)}, u32[]{:S(2)}, u32[]{:S(2)}) collective-permute-start(bf16[128,2048]{1,0:T(8,128)(2,1)S(1)} %pad_maximum_fusion.4), channel_id=1, source_target_pairs={{0,4},{1,5},{2,6},{3,7},{4,8},{5,9},{6,10},{7,11},{8,12},{9,13},{1... | collective-permute-start | bytes 1572872 | tf_op jit(solution)/shard_map/ppermute | solution.py:27
  218.2 11.1 %collective-permute-start.35 = (bf16[32,2048]{1,0:T(8,128)(2,1)S(1)}, bf16[32,2048]{1,0:T(8,128)(2,1)S(1)}, u32[]{:S(2)}, u32[]{:S(2)}) collective-permute-start(bf16[32,2048]{1,0:T(8,128)(2,1)S(1)} %get-tuple-element.42), channel_id=1, source_target_pairs={{0,2},{1,3},{2,0},{3,1},{4,6},{5,7},{6,4},{7,5},{8,10},{9,11},{10,... | collective-permute-start | bytes 393224 | tf_op jit(solution)/shard_map/ppermute | solution.py:27
  246.5 10.2 %collective-permute-start.42 = (bf16[32,2048]{1,0:T(8,128)(2,1)S(1)}, bf16[32,2048]{1,0:T(8,128)(2,1)S(1)}, u32[]{:S(2)}, u32[]{:S(2)}) collective-permute-start(bf16[32,2048]{1,0:T(8,128)(2,1)S(1)} %get-tuple-element.8), channel_id=1, source_target_pairs={{0,3},{1,0},{2,1},{3,2},{4,7},{5,4},{6,5},{7,6},{8,11},{9,8},{10,9... | collective-permute-start | bytes 393224 | tf_op jit(solution)/shard_map/ppermute | solution.py:27
  247.7 14.3 %collective-permute-start.43 = (bf16[32,2048]{1,0:T(8,128)(2,1)S(1)}, bf16[32,2048]{1,0:T(8,128)(2,1)S(1)}, u32[]{:S(2)}, u32[]{:S(2)}) collective-permute-start(bf16[32,2048]{1,0:T(8,128)(2,1)S(1)} %get-tuple-element.8), channel_id=1, source_target_pairs={{0,2},{1,3},{2,0},{3,1},{4,6},{5,7},{6,4},{7,5},{8,10},{9,11},{10,... | collective-permute-start | bytes 393224 | tf_op jit(solution)/shard_map/ppermute | solution.py:27
  252.4 11.5 %collective-permute-start.44 = (bf16[32,2048]{1,0:T(8,128)(2,1)S(1)}, bf16[32,2048]{1,0:T(8,128)(2,1)S(1)}, u32[]{:S(2)}, u32[]{:S(2)}) collective-permute-start(bf16[32,2048]{1,0:T(8,128)(2,1)S(1)} %get-tuple-element.8), channel_id=1, source_target_pairs={{0,1},{1,2},{2,3},{3,0},{4,5},{5,6},{6,7},{7,4},{8,9},{9,10},{10,1... | collective-permute-start | bytes 393224 | tf_op jit(solution)/shard_map/ppermute | solution.py:27
  264.0 13.9 %collective-permute-start.45 = (bf16[128,2048]{1,0:T(8,128)(2,1)S(1)}, bf16[128,2048]{1,0:T(8,128)(2,1)S(1)}, u32[]{:S(2)}, u32[]{:S(2)}) collective-permute-start(bf16[128,2048]{1,0:T(8,128)(2,1)S(1)} %pad_maximum_fusion.6), channel_id=1, source_target_pairs={{0,12},{1,13},{2,14},{3,15},{4,0},{5,1},{6,2},{7,3},{8,4},{9,5},{1... | collective-permute-start | bytes 1572872 | tf_op jit(solution)/shard_map/ppermute | solution.py:27
  264.5 15.2 %collective-permute-start.46 = (bf16[128,2048]{1,0:T(8,128)(2,1)S(1)}, bf16[128,2048]{1,0:T(8,128)(2,1)S(1)}, u32[]{:S(2)}, u32[]{:S(2)}) collective-permute-start(bf16[128,2048]{1,0:T(8,128)(2,1)S(1)} %pad_maximum_fusion.6), channel_id=1, source_target_pairs={{0,4},{1,5},{2,6},{3,7},{4,8},{5,9},{6,10},{7,11},{8,12},{9,13},{1... | collective-permute-start | bytes 1572872 | tf_op jit(solution)/shard_map/ppermute | solution.py:27
  301.2 9.6 %collective-permute-start.51 = (bf16[128,1024]{1,0:T(8,128)(2,1)S(1)}, bf16[128,1024]{1,0:T(8,128)(2,1)S(1)}, u32[]{:S(2)}, u32[]{:S(2)}) collective-permute-start(bf16[128,1024]{1,0:T(8,128)(2,1)S(1)} %get-tuple-element.15), channel_id=1, source_target_pairs={{0,4},{1,5},{2,6},{3,7},{4,8},{5,9},{6,10},{7,11},{8,12},{9,13},{1... | collective-permute-start | bytes 786440 | tf_op jit(solution)/shard_map/ppermute | solution.py:27
  301.3 9.5 %collective-permute-start.53 = (bf16[128,1024]{1,0:T(8,128)(2,1)S(1)}, bf16[128,1024]{1,0:T(8,128)(2,1)S(1)}, u32[]{:S(2)}, u32[]{:S(2)}) collective-permute-start(bf16[128,1024]{1,0:T(8,128)(2,1)S(1)} %get-tuple-element.16), channel_id=1, source_target_pairs={{0,12},{1,13},{2,14},{3,15},{4,0},{5,1},{6,2},{7,3},{8,4},{9,5},{1... | collective-permute-start | bytes 786440 | tf_op jit(solution)/shard_map/ppermute | solution.py:27
  311.1 13.4 %collective-permute-start.54 = (bf16[128,2048]{1,0:T(8,128)(2,1)S(1)}, bf16[128,2048]{1,0:T(8,128)(2,1)S(1)}, u32[]{:S(2)}, u32[]{:S(2)}) collective-permute-start(bf16[128,2048]{1,0:T(8,128)(2,1)S(1)} %pad_maximum_fusion.8), channel_id=1, source_target_pairs={{0,12},{1,13},{2,14},{3,15},{4,0},{5,1},{6,2},{7,3},{8,4},{9,5},{1... | collective-permute-start | bytes 1572872 | tf_op jit(solution)/shard_map/ppermute | solution.py:27
  314.2 13.8 %collective-permute-start.52 = (bf16[128,2048]{1,0:T(8,128)(2,1)S(1)}, bf16[128,2048]{1,0:T(8,128)(2,1)S(1)}, u32[]{:S(2)}, u32[]{:S(2)}) collective-permute-start(bf16[128,2048]{1,0:T(8,128)(2,1)S(1)} %pad_maximum_fusion.7), channel_id=1, source_target_pairs={{0,4},{1,5},{2,6},{3,7},{4,8},{5,9},{6,10},{7,11},{8,12},{9,13},{1... | collective-permute-start | bytes 1572872 | tf_op jit(solution)/shard_map/ppermute | solution.py:27
  329.3 11.6 %collective-permute-start.56 = (bf16[32,2048]{1,0:T(8,128)(2,1)S(1)}, bf16[32,2048]{1,0:T(8,128)(2,1)S(1)}, u32[]{:S(2)}, u32[]{:S(2)}) collective-permute-start(bf16[32,2048]{1,0:T(8,128)(2,1)S(1)} %get-tuple-element.39), channel_id=1, source_target_pairs={{0,2},{1,3},{2,0},{3,1},{4,6},{5,7},{6,4},{7,5},{8,10},{9,11},{10,... | collective-permute-start | bytes 393224 | tf_op jit(solution)/shard_map/ppermute | solution.py:27
  (40 other events, 296.9 us)
where the time goes:
time: 358 us; the launch traced here: 351 us
  waiting for transfers between devices  216 us (60%)
  starting transfers between devices  97 us (27%)
  matrix products  16 us (4%)
  local copies, waits for them, and re-layouts  14.2 us (4%)
  other arithmetic  7.23 us (2%)
    ppermute x42, waiting for transfers between devices, tp_ring(): return lax.ppermute(value, 'tp', pairs)  167 us
    ppermute x42, starting transfers between devices, tp_ring(): return lax.ppermute(value, 'tp', pairs)  79.9 us
    ppermute x17, waiting for transfers between devices, swapped(): return lax.ppermute(value, axis, pairs)  37.4 us
    ppermute x17, starting transfers between devices, swapped(): return lax.ppermute(value, axis, pairs)  14.5 us
    ppermute x2, waiting for transfers between devices, shifted(): lax.ppermute(value, axis, [(source, source + steps) for source in range(c...  11.1 us
  transfers between devices with their start and end apart: 61, of which 50 were waited for; matrix products, arithmetic and copies ran while one was open for 3% of the time, Pallas kernels for 0%

commit v1 on v0

--- a/solution.py
+++ b/solution.py
@@ -4,7 +4,6 @@
 from jax.sharding import PartitionSpec as P
 
 LAYERS = 2
-PIECES = 1
 
 
 epsilon = 1e-05
@@ -100,9 +99,7 @@
     micro_count, tok_dev, model_width = tokens.shape
     piece_width = model_width // split
     half_width = model_width // 2
-    row_count = tok_dev // PIECES
-    piece_count = micro_count * PIECES
-    tick_count = piece_count + LAYERS - 1
+    row_count = micro_count * tok_dev
 
     def pick(value, axis, which):
         shape = value.shape
@@ -120,9 +117,8 @@
     norm_gain = lax.dynamic_index_in_dim(norm_gains, section_layer, 0, keepdims=False)
     gain_own = pick(norm_gain, 0, core)
 
-    def from_tokens(piece_index):
-        micro_index, part = divmod(piece_index, PIECES)
-        rows = tokens[micro_index, part * row_count:(part + 1) * row_count].astype(jnp.float32)
+    def from_tokens():
+        rows = tokens.reshape(row_count, model_width).astype(jnp.float32)
         return pick(rows, 1, core), jnp.sum(rows * rows, axis=1, keepdims=True)
 
     def from_received(received):
@@ -158,31 +154,19 @@
 
     blocks = []
     received = None
-    for tick_index in range(tick_count):
+    for tick_index in range(LAYERS):
         if tick_index == 0:
-            current, square_sum = from_tokens(0)
-        elif tick_index >= piece_count:
+            current, square_sum = from_tokens()
+        else:
             current, square_sum = from_received(received)
-        else:
-            first_current, first_sum = from_tokens(tick_index)
-            later_current, later_sum = from_received(received)
-            is_first = section_layer == 0
-            current = jnp.where(is_first, first_current, later_current)
-            square_sum = jnp.where(is_first, first_sum, later_sum)
         full_half, block = tick(current, square_sum)
         blocks.append(block)
-        if tick_index < tick_count - 1:
+        if tick_index < LAYERS - 1:
             received = shifted(full_half, "section", split)
 
     stacked = jnp.stack(blocks, axis=0)
-    outputs = []
-    for micro_index in range(micro_count):
-        parts = [
-            lax.dynamic_index_in_dim(stacked, micro_index * PIECES + part + section_layer, 0, keepdims=False)
-            for part in range(PIECES)
-        ]
-        outputs.append(jnp.concatenate(parts, axis=0))
-    return jnp.stack(outputs, axis=0)[None]
+    mine = lax.dynamic_index_in_dim(stacked, section_layer, 0, keepdims=False)
+    return mine.reshape(1, micro_count, tok_dev, piece_width)
 
 
 def solution(mesh):

time: 358 us -> 394 us (1.10)
  waiting for transfers between devices: 216 us -> 272 us
  starting transfers between devices: 97 us -> 70.4 us
  matrix products: 16 us -> 23.8 us
    ppermute x42 -> x28, waiting for transfers between devices: 167 us -> 214 us  [tp_ring(): return lax.ppermute(value, 'tp', pairs)]
    ppermute x42 -> x28, starting transfers between devices: 79.9 us -> 59.5 us  [tp_ring(): return lax.ppermute(value, 'tp', pairs)]
    ppermute x17 -> x11, waiting for transfers between devices: 37.4 us -> 49.5 us  [swapped(): return lax.ppermute(value, axis, pairs)]
    ppermute x17 -> x11, starting transfers between devices: 14.5 us -> 9.66 us  [swapped(): return lax.ppermute(value, axis, pairs)]
    ppermute x2 -> x1, waiting for transfers between devices: 11.1 us -> 7.73 us  [shifted(): lax.ppermute(value, axis, [(source, source + steps) for source in range(c...]
  transfers between devices with their start and end apart: 61 -> 40, of which waited for: 50 -> 33; matrix products, arithmetic and copies ran while one was open for 3% -> 2% of each run, Pallas kernels for 0% -> 0%
where the time goes in v1:
time: 394 us; the launch traced here: 387 us
  waiting for transfers between devices  272 us (69%)
  starting transfers between devices  70.4 us (18%)
  matrix products  23.8 us (6%)
  local copies, waits for them, and re-layouts  12.9 us (3%)
  other arithmetic  7.18 us (2%)
    ppermute x28, waiting for transfers between devices, tp_ring(): return lax.ppermute(value, 'tp', pairs)  214 us
    ppermute x28, starting transfers between devices, tp_ring(): return lax.ppermute(value, 'tp', pairs)  59.5 us
    ppermute x11, waiting for transfers between devices, swapped(): return lax.ppermute(value, axis, pairs)  49.5 us
    ppermute x11, starting transfers between devices, swapped(): return lax.ppermute(value, axis, pairs)  9.66 us
  transfers between devices with their start and end apart: 40, of which 33 were waited for; matrix products, arithmetic and copies ran while one was open for 2% of the time, Pallas kernels for 0%

profile of v1, /device:TPU:32, one launch (start us, length us, event | category | flops | bytes accessed | tf_op | source)
XLA Modules:
  0.0 386.9 jit_solution(14492415625423774898)
XLA Ops:
  6.1 5.4 %collective-permute-start = (bf16[64,2048]{1,0:T(8,128)(2,1)S(1)}, bf16[64,2048]{1,0:T(8,128)(2,1)S(1)}, u32[]{:S(2)}, u32[]{:S(2)}) collective-permute-start(bf16[64,2048]{1,0:T(8,128)(2,1)S(1)} %get-tuple-element.8), channel_id=1, source_target_pairs={{0,3},{1,0},{2,1},{3,2},{4,7},{5,4},{6,5},{7,6},{8,11},{9,8},{10,9... | collective-permute-start | bytes 786440 | tf_op jit(solution)/shard_map/ppermute | solution.py:26
  15.3 11.1 %collective-permute-done = bf16[64,2048]{1,0:T(8,128)(2,1)S(1)} collective-permute-done((bf16[64,2048]{1,0:T(8,128)(2,1)S(1)}, bf16[64,2048]{1,0:T(8,128)(2,1)S(1)}, u32[]{:S(2)}, u32[]{:S(2)}) %collective-permute-start) | collective-permute-done | bytes 262176 | tf_op jit(solution)/shard_map/ppermute | solution.py:26
  26.5 9.4 %collective-permute-done.1 = bf16[64,2048]{1,0:T(8,128)(2,1)S(1)} collective-permute-done((bf16[64,2048]{1,0:T(8,128)(2,1)S(1)}, bf16[64,2048]{1,0:T(8,128)(2,1)S(1)}, u32[]{:S(2)}, u32[]{:S(2)}) %collective-permute-start.1) | collective-permute-done | bytes 262176 | tf_op jit(solution)/shard_map/ppermute | solution.py:26
  40.2 21.5 %collective-permute-done.3 = bf16[256,2048]{1,0:T(8,128)(2,1)S(1)} collective-permute-done((bf16[256,2048]{1,0:T(8,128)(2,1)S(1)}, bf16[256,2048]{1,0:T(8,128)(2,1)S(1)}, u32[]{:S(2)}, u32[]{:S(2)}) %collective-permute-start.3) | collective-permute-done | bytes 1048608 | tf_op jit(solution)/shard_map/ppermute | solution.py:26
  61.8 3.8 collective-permute-start.6
  68.2 7.5 %collective-permute-done.6 = bf16[256,1024]{1,0:T(8,128)(2,1)S(1)} collective-permute-done((bf16[256,1024]{1,0:T(8,128)(2,1)S(1)}, bf16[256,1024]{1,0:T(8,128)(2,1)S(1)}, u32[]{:S(2)}, u32[]{:S(2)}) %collective-permute-start.6) | collective-permute-done | bytes 524320 | tf_op jit(solution)/shard_map/ppermute | solution.py:26
  75.6 3.5 collective-permute-done.5
  84.9 4.4 %collective-permute-done.7 = bf16[1024,2048]{1,0:T(8,128)(2,1)} collective-permute-done((bf16[1024,2048]{1,0:T(8,128)(2,1)}, bf16[1024,2048]{1,0:T(8,128)(2,1)}, u32[]{:S(2)}, u32[]{:S(2)}) %collective-permute-start.7) | collective-permute-done | bytes 4194336 | tf_op jit(solution)/shard_map/ppermute | solution.py:14
  92.7 3.5 convolution_add_fusion.3
  104.6 7.0 %collective-permute-done.8 = bf16[1024,2048]{1,0:T(8,128)(2,1)S(1)} collective-permute-done((bf16[1024,2048]{1,0:T(8,128)(2,1)S(1)}, bf16[1024,2048]{1,0:T(8,128)(2,1)S(1)}, u32[]{:S(2)}, u32[]{:S(2)}) %collective-permute-start.8) | collective-permute-done | bytes 4194336 | tf_op jit(solution)/shard_map/ppermute | solution.py:14
  116.4 11.9 %collective-permute-done.9 = bf16[256,1024]{1,0:T(8,128)(2,1)S(1)} collective-permute-done((bf16[256,1024]{1,0:T(8,128)(2,1)S(1)}, bf16[256,1024]{1,0:T(8,128)(2,1)S(1)}, u32[]{:S(2)}, u32[]{:S(2)}) %collective-permute-start.9) | collective-permute-done | bytes 524320 | tf_op jit(solution)/shard_map/ppermute | solution.py:26
  132.0 21.4 %collective-permute-done.12 = bf16[256,2048]{1,0:T(8,128)(2,1)S(1)} collective-permute-done((bf16[256,2048]{1,0:T(8,128)(2,1)S(1)}, bf16[256,2048]{1,0:T(8,128)(2,1)S(1)}, u32[]{:S(2)}, u32[]{:S(2)}) %collective-permute-start.12) | collective-permute-done | bytes 1048608 | tf_op jit(solution)/shard_map/ppermute | solution.py:26
  153.5 3.6 collective-permute-done.10
  157.6 4.5 %collective-permute-start.15 = (bf16[64,2048]{1,0:T(8,128)(2,1)S(1)}, bf16[64,2048]{1,0:T(8,128)(2,1)S(1)}, u32[]{:S(2)}, u32[]{:S(2)}) collective-permute-start(bf16[64,2048]{1,0:T(8,128)(2,1)S(1)} %get-tuple-element.25), channel_id=1, source_target_pairs={{0,3},{1,0},{2,1},{3,2},{4,7},{5,4},{6,5},{7,6},{8,11},{9,8},{10,9... | collective-permute-start | bytes 786440 | tf_op jit(solution)/shard_map/ppermute | solution.py:26
  167.1 3.8 collective-permute-done.15
  170.9 9.8 %collective-permute-done.14 = bf16[64,2048]{1,0:T(8,128)(2,1)S(1)} collective-permute-done((bf16[64,2048]{1,0:T(8,128)(2,1)S(1)}, bf16[64,2048]{1,0:T(8,128)(2,1)S(1)}, u32[]{:S(2)}, u32[]{:S(2)}) %collective-permute-start.14) | collective-permute-done | bytes 262176 | tf_op jit(solution)/shard_map/ppermute | solution.py:26
  185.8 11.0 %collective-permute-done.18 = bf16[64,2048]{1,0:T(8,128)(2,1)S(1)} collective-permute-done((bf16[64,2048]{1,0:T(8,128)(2,1)S(1)}, bf16[64,2048]{1,0:T(8,128)(2,1)S(1)}, u32[]{:S(2)}, u32[]{:S(2)}) %collective-permute-start.18) | collective-permute-done | bytes 262176 | tf_op jit(solution)/shard_map/ppermute | solution.py:14
  198.8 7.7 %collective-permute-done.19 = bf16[64,2048]{1,0:T(8,128)(2,1)S(1)} collective-permute-done((bf16[64,2048]{1,0:T(8,128)(2,1)S(1)}, bf16[64,2048]{1,0:T(8,128)(2,1)S(1)}, u32[]{:S(2)}, u32[]{:S(2)}) %collective-permute-start.19) | collective-permute-done | bytes 262176 | tf_op jit(solution)/shard_map/ppermute | solution.py:75
  208.1 5.5 %collective-permute-start.21 = (bf16[64,2048]{1,0:T(8,128)(2,1)S(1)}, bf16[64,2048]{1,0:T(8,128)(2,1)S(1)}, u32[]{:S(2)}, u32[]{:S(2)}) collective-permute-start(bf16[64,2048]{1,0:T(8,128)(2,1)S(1)} %get-tuple-element.6), channel_id=1, source_target_pairs={{0,3},{1,0},{2,1},{3,2},{4,7},{5,4},{6,5},{7,6},{8,11},{9,8},{10,9... | collective-permute-start | bytes 786440 | tf_op jit(solution)/shard_map/ppermute | solution.py:26
  216.5 7.3 %collective-permute-done.21 = bf16[64,2048]{1,0:T(8,128)(2,1)S(1)} collective-permute-done((bf16[64,2048]{1,0:T(8,128)(2,1)S(1)}, bf16[64,2048]{1,0:T(8,128)(2,1)S(1)}, u32[]{:S(2)}, u32[]{:S(2)}) %collective-permute-start.21) | collective-permute-done | bytes 262176 | tf_op jit(solution)/shard_map/ppermute | solution.py:26
  223.8 13.3 %collective-permute-done.22 = bf16[64,2048]{1,0:T(8,128)(2,1)S(1)} collective-permute-done((bf16[64,2048]{1,0:T(8,128)(2,1)S(1)}, bf16[64,2048]{1,0:T(8,128)(2,1)S(1)}, u32[]{:S(2)}, u32[]{:S(2)}) %collective-permute-start.22) | collective-permute-done | bytes 262176 | tf_op jit(solution)/shard_map/ppermute | solution.py:26
  239.3 22.9 %collective-permute-done.24 = bf16[256,2048]{1,0:T(8,128)(2,1)S(1)} collective-permute-done((bf16[256,2048]{1,0:T(8,128)(2,1)S(1)}, bf16[256,2048]{1,0:T(8,128)(2,1)S(1)}, u32[]{:S(2)}, u32[]{:S(2)}) %collective-permute-start.24) | collective-permute-done | bytes 1048608 | tf_op jit(solution)/shard_map/ppermute | solution.py:26
  264.7 10.5 %collective-permute-done.27 = bf16[256,1024]{1,0:T(8,128)(2,1)S(1)} collective-permute-done((bf16[256,1024]{1,0:T(8,128)(2,1)S(1)}, bf16[256,1024]{1,0:T(8,128)(2,1)S(1)}, u32[]{:S(2)}, u32[]{:S(2)}) %collective-permute-start.27) | collective-permute-done | bytes 524320 | tf_op jit(solution)/shard_map/ppermute | solution.py:26
  278.3 7.1 %collective-permute-done.28 = bf16[1024,2048]{1,0:T(8,128)(2,1)S(1)} collective-permute-done((bf16[1024,2048]{1,0:T(8,128)(2,1)S(1)}, bf16[1024,2048]{1,0:T(8,128)(2,1)S(1)}, u32[]{:S(2)}, u32[]{:S(2)}) %collective-permute-start.28) | collective-permute-done | bytes 4194336 | tf_op jit(solution)/shard_map/ppermute | solution.py:14
  292.0 7.0 %collective-permute-done.29 = bf16[1024,2048]{1,0:T(8,128)(2,1)S(1)} collective-permute-done((bf16[1024,2048]{1,0:T(8,128)(2,1)S(1)}, bf16[1024,2048]{1,0:T(8,128)(2,1)S(1)}, u32[]{:S(2)}, u32[]{:S(2)}) %collective-permute-start.29) | collective-permute-done | bytes 4194336 | tf_op jit(solution)/shard_map/ppermute | solution.py:14
  303.8 11.9 %collective-permute-done.30 = bf16[256,1024]{1,0:T(8,128)(2,1)S(1)} collective-permute-done((bf16[256,1024]{1,0:T(8,128)(2,1)S(1)}, bf16[256,1024]{1,0:T(8,128)(2,1)S(1)}, u32[]{:S(2)}, u32[]{:S(2)}) %collective-permute-start.30) | collective-permute-done | bytes 524320 | tf_op jit(solution)/shard_map/ppermute | solution.py:26
  319.5 21.4 %collective-permute-done.33 = bf16[256,2048]{1,0:T(8,128)(2,1)S(1)} collective-permute-done((bf16[256,2048]{1,0:T(8,128)(2,1)S(1)}, bf16[256,2048]{1,0:T(8,128)(2,1)S(1)}, u32[]{:S(2)}, u32[]{:S(2)}) %collective-permute-start.33) | collective-permute-done | bytes 1048608 | tf_op jit(solution)/shard_map/ppermute | solution.py:26
  340.9 3.6 collective-permute-done.31
  345.1 5.5 %collective-permute-start.36 = (bf16[64,2048]{1,0:T(8,128)(2,1)S(1)}, bf16[64,2048]{1,0:T(8,128)(2,1)S(1)}, u32[]{:S(2)}, u32[]{:S(2)}) collective-permute-start(bf16[64,2048]{1,0:T(8,128)(2,1)S(1)} %get-tuple-element.22), channel_id=1, source_target_pairs={{0,3},{1,0},{2,1},{3,2},{4,7},{5,4},{6,5},{7,6},{8,11},{9,8},{10,9... | collective-permute-start | bytes 786440 | tf_op jit(solution)/shard_map/ppermute | solution.py:26
  353.4 9.3 %collective-permute-done.36 = bf16[64,2048]{1,0:T(8,128)(2,1)S(1)} collective-permute-done((bf16[64,2048]{1,0:T(8,128)(2,1)S(1)}, bf16[64,2048]{1,0:T(8,128)(2,1)S(1)}, u32[]{:S(2)}, u32[]{:S(2)}) %collective-permute-start.36) | collective-permute-done | bytes 262176 | tf_op jit(solution)/shard_map/ppermute | solution.py:26
  362.7 6.5 %collective-permute-done.35 = bf16[64,2048]{1,0:T(8,128)(2,1)S(1)} collective-permute-done((bf16[64,2048]{1,0:T(8,128)(2,1)S(1)}, bf16[64,2048]{1,0:T(8,128)(2,1)S(1)}, u32[]{:S(2)}, u32[]{:S(2)}) %collective-permute-start.35) | collective-permute-done | bytes 262176 | tf_op jit(solution)/shard_map/ppermute | solution.py:26
  374.1 10.6 %collective-permute-done.39 = bf16[64,2048]{1,0:T(8,128)(2,1)S(1)} collective-permute-done((bf16[64,2048]{1,0:T(8,128)(2,1)S(1)}, bf16[64,2048]{1,0:T(8,128)(2,1)S(1)}, u32[]{:S(2)}, u32[]{:S(2)}) %collective-permute-start.39) | collective-permute-done | bytes 262176 | tf_op jit(solution)/shard_map/ppermute | solution.py:14
  (123 shorter events, 92.6 us)
Async XLA Ops:
  6.1 20.4 %collective-permute-start = (bf16[64,2048]{1,0:T(8,128)(2,1)S(1)}, bf16[64,2048]{1,0:T(8,128)(2,1)S(1)}, u32[]{:S(2)}, u32[]{:S(2)}) collective-permute-start(bf16[64,2048]{1,0:T(8,128)(2,1)S(1)} %get-tuple-element.8), channel_id=1, source_target_pairs={{0,3},{1,0},{2,1},{3,2},{4,7},{5,4},{6,5},{7,6},{8,11},{9,8},{10,9... | collective-permute-start | bytes 786440 | tf_op jit(solution)/shard_map/ppermute | solution.py:26
  11.5 24.4 %collective-permute-start.1 = (bf16[64,2048]{1,0:T(8,128)(2,1)S(1)}, bf16[64,2048]{1,0:T(8,128)(2,1)S(1)}, u32[]{:S(2)}, u32[]{:S(2)}) collective-permute-start(bf16[64,2048]{1,0:T(8,128)(2,1)S(1)} %get-tuple-element.8), channel_id=1, source_target_pairs={{0,2},{1,3},{2,0},{3,1},{4,6},{5,7},{6,4},{7,5},{8,10},{9,11},{10,... | collective-permute-start | bytes 786440 | tf_op jit(solution)/shard_map/ppermute | solution.py:26
  13.0 23.4 %collective-permute-start.2 = (bf16[64,2048]{1,0:T(8,128)(2,1)S(1)}, bf16[64,2048]{1,0:T(8,128)(2,1)S(1)}, u32[]{:S(2)}, u32[]{:S(2)}) collective-permute-start(bf16[64,2048]{1,0:T(8,128)(2,1)S(1)} %get-tuple-element.8), channel_id=1, source_target_pairs={{0,1},{1,2},{2,3},{3,0},{4,5},{5,6},{6,7},{7,4},{8,9},{9,10},{10,1... | collective-permute-start | bytes 786440 | tf_op jit(solution)/shard_map/ppermute | solution.py:26
  36.4 25.3 %collective-permute-start.3 = (bf16[256,2048]{1,0:T(8,128)(2,1)S(1)}, bf16[256,2048]{1,0:T(8,128)(2,1)S(1)}, u32[]{:S(2)}, u32[]{:S(2)}) collective-permute-start(bf16[256,2048]{1,0:T(8,128)(2,1)S(1)} %pad_maximum_fusion), channel_id=1, source_target_pairs={{0,12},{1,13},{2,14},{3,15},{4,0},{5,1},{6,2},{7,3},{8,4},{9,5},{1... | collective-permute-start | bytes 3145736 | tf_op jit(solution)/shard_map/ppermute | solution.py:26
  39.5 26.0 %collective-permute-start.4 = (bf16[256,2048]{1,0:T(8,128)(2,1)S(1)}, bf16[256,2048]{1,0:T(8,128)(2,1)S(1)}, u32[]{:S(2)}, u32[]{:S(2)}) collective-permute-start(bf16[256,2048]{1,0:T(8,128)(2,1)S(1)} %pad_maximum_fusion), channel_id=1, source_target_pairs={{0,4},{1,5},{2,6},{3,7},{4,8},{5,9},{6,10},{7,11},{8,12},{9,13},{1... | collective-permute-start | bytes 3145736 | tf_op jit(solution)/shard_map/ppermute | solution.py:26
  61.8 13.9 %collective-permute-start.6 = (bf16[256,1024]{1,0:T(8,128)(2,1)S(1)}, bf16[256,1024]{1,0:T(8,128)(2,1)S(1)}, u32[]{:S(2)}, u32[]{:S(2)}) collective-permute-start(bf16[256,1024]{1,0:T(8,128)(2,1)S(1)} %slice.123), channel_id=1, source_target_pairs={{0,12},{1,13},{2,14},{3,15},{4,0},{5,1},{6,2},{7,3},{8,4},{9,5},{1... | collective-permute-start | bytes 1572872 | tf_op jit(solution)/shard_map/ppermute | solution.py:26
  65.6 13.6 %collective-permute-start.5 = (bf16[256,1024]{1,0:T(8,128)(2,1)S(1)}, bf16[256,1024]{1,0:T(8,128)(2,1)S(1)}, u32[]{:S(2)}, u32[]{:S(2)}) collective-permute-start(bf16[256,1024]{1,0:T(8,128)(2,1)S(1)} %slice.122), channel_id=1, source_target_pairs={{0,4},{1,5},{2,6},{3,7},{4,8},{5,9},{6,10},{7,11},{8,12},{9,13},{1... | collective-permute-start | bytes 1572872 | tf_op jit(solution)/shard_map/ppermute | solution.py:26
  113.1 15.3 %collective-permute-start.9 = (bf16[256,1024]{1,0:T(8,128)(2,1)S(1)}, bf16[256,1024]{1,0:T(8,128)(2,1)S(1)}, u32[]{:S(2)}, u32[]{:S(2)}) collective-permute-start(bf16[256,1024]{1,0:T(8,128)(2,1)S(1)} %get-tuple-element.17), channel_id=1, source_target_pairs={{0,4},{1,5},{2,6},{3,7},{4,8},{5,9},{6,10},{7,11},{8,12},{9,13},{1... | collective-permute-start | bytes 1572872 | tf_op jit(solution)/shard_map/ppermute | solution.py:26
  113.2 15.2 %collective-permute-start.11 = (bf16[256,1024]{1,0:T(8,128)(2,1)S(1)}, bf16[256,1024]{1,0:T(8,128)(2,1)S(1)}, u32[]{:S(2)}, u32[]{:S(2)}) collective-permute-start(bf16[256,1024]{1,0:T(8,128)(2,1)S(1)} %get-tuple-element.18), channel_id=1, source_target_pairs={{0,12},{1,13},{2,14},{3,15},{4,0},{5,1},{6,2},{7,3},{8,4},{9,5},{1... | collective-permute-start | bytes 1572872 | tf_op jit(solution)/shard_map/ppermute | solution.py:26
  128.8 24.6 %collective-permute-start.12 = (bf16[256,2048]{1,0:T(8,128)(2,1)S(1)}, bf16[256,2048]{1,0:T(8,128)(2,1)S(1)}, u32[]{:S(2)}, u32[]{:S(2)}) collective-permute-start(bf16[256,2048]{1,0:T(8,128)(2,1)S(1)} %pad_maximum_fusion.2), channel_id=1, source_target_pairs={{0,12},{1,13},{2,14},{3,15},{4,0},{5,1},{6,2},{7,3},{8,4},{9,5},{1... | collective-permute-start | bytes 3145736 | tf_op jit(solution)/shard_map/ppermute | solution.py:26
  132.0 25.1 %collective-permute-start.10 = (bf16[256,2048]{1,0:T(8,128)(2,1)S(1)}, bf16[256,2048]{1,0:T(8,128)(2,1)S(1)}, u32[]{:S(2)}, u32[]{:S(2)}) collective-permute-start(bf16[256,2048]{1,0:T(8,128)(2,1)S(1)} %pad_maximum_fusion.1), channel_id=1, source_target_pairs={{0,4},{1,5},{2,6},{3,7},{4,8},{5,9},{6,10},{7,11},{8,12},{9,13},{1... | collective-permute-start | bytes 3145736 | tf_op jit(solution)/shard_map/ppermute | solution.py:26
  157.6 13.3 %collective-permute-start.15 = (bf16[64,2048]{1,0:T(8,128)(2,1)S(1)}, bf16[64,2048]{1,0:T(8,128)(2,1)S(1)}, u32[]{:S(2)}, u32[]{:S(2)}) collective-permute-start(bf16[64,2048]{1,0:T(8,128)(2,1)S(1)} %get-tuple-element.25), channel_id=1, source_target_pairs={{0,3},{1,0},{2,1},{3,2},{4,7},{5,4},{6,5},{7,6},{8,11},{9,8},{10,9... | collective-permute-start | bytes 786440 | tf_op jit(solution)/shard_map/ppermute | solution.py:26
  162.2 18.6 %collective-permute-start.14 = (bf16[64,2048]{1,0:T(8,128)(2,1)S(1)}, bf16[64,2048]{1,0:T(8,128)(2,1)S(1)}, u32[]{:S(2)}, u32[]{:S(2)}) collective-permute-start(bf16[64,2048]{1,0:T(8,128)(2,1)S(1)} %get-tuple-element.26), channel_id=1, source_target_pairs={{0,2},{1,3},{2,0},{3,1},{4,6},{5,7},{6,4},{7,5},{8,10},{9,11},{10,... | collective-permute-start | bytes 786440 | tf_op jit(solution)/shard_map/ppermute | solution.py:26
  164.6 16.8 %collective-permute-start.13 = (bf16[64,2048]{1,0:T(8,128)(2,1)S(1)}, bf16[64,2048]{1,0:T(8,128)(2,1)S(1)}, u32[]{:S(2)}, u32[]{:S(2)}) collective-permute-start(bf16[64,2048]{1,0:T(8,128)(2,1)S(1)} %get-tuple-element.24), channel_id=1, source_target_pairs={{0,1},{1,2},{2,3},{3,0},{4,5},{5,6},{6,7},{7,4},{8,9},{9,10},{10,1... | collective-permute-start | bytes 786440 | tf_op jit(solution)/shard_map/ppermute | solution.py:26
  181.6 15.1 %collective-permute-start.18 = (bf16[64,2048]{1,0:T(8,128)(2,1)S(1)}, bf16[64,2048]{1,0:T(8,128)(2,1)S(1)}, u32[]{:S(2)}, u32[]{:S(2)}) collective-permute-start(bf16[64,2048]{1,0:T(8,128)(2,1)S(1)} %add_convert_fusion.10), channel_id=1, source_target_pairs={{0,96},{16,112},{32,64},{48,80},{64,32},{80,48},{96,0},{112,16},{1... | collective-permute-start | bytes 786440 | tf_op jit(solution)/shard_map/ppermute | solution.py:14
  184.4 12.3 %collective-permute-start.17 = (bf16[64,2048]{1,0:T(8,128)(2,1)S(1)}, bf16[64,2048]{1,0:T(8,128)(2,1)S(1)}, u32[]{:S(2)}, u32[]{:S(2)}) collective-permute-start(bf16[64,2048]{1,0:T(8,128)(2,1)S(1)} %add_convert_fusion.10), channel_id=1, source_target_pairs={{0,64},{16,80},{32,96},{48,112},{64,0},{80,16},{96,32},{112,48},{1... | collective-permute-start | bytes 786440 | tf_op jit(solution)/shard_map/ppermute | solution.py:14
  208.1 15.8 %collective-permute-start.21 = (bf16[64,2048]{1,0:T(8,128)(2,1)S(1)}, bf16[64,2048]{1,0:T(8,128)(2,1)S(1)}, u32[]{:S(2)}, u32[]{:S(2)}) collective-permute-start(bf16[64,2048]{1,0:T(8,128)(2,1)S(1)} %get-tuple-element.6), channel_id=1, source_target_pairs={{0,3},{1,0},{2,1},{3,2},{4,7},{5,4},{6,5},{7,6},{8,11},{9,8},{10,9... | collective-permute-start | bytes 786440 | tf_op jit(solution)/shard_map/ppermute | solution.py:26
  213.6 23.5 %collective-permute-start.22 = (bf16[64,2048]{1,0:T(8,128)(2,1)S(1)}, bf16[64,2048]{1,0:T(8,128)(2,1)S(1)}, u32[]{:S(2)}, u32[]{:S(2)}) collective-permute-start(bf16[64,2048]{1,0:T(8,128)(2,1)S(1)} %get-tuple-element.6), channel_id=1, source_target_pairs={{0,2},{1,3},{2,0},{3,1},{4,6},{5,7},{6,4},{7,5},{8,10},{9,11},{10,... | collective-permute-start | bytes 786440 | tf_op jit(solution)/shard_map/ppermute | solution.py:26
  213.7 23.4 %collective-permute-start.23 = (bf16[64,2048]{1,0:T(8,128)(2,1)S(1)}, bf16[64,2048]{1,0:T(8,128)(2,1)S(1)}, u32[]{:S(2)}, u32[]{:S(2)}) collective-permute-start(bf16[64,2048]{1,0:T(8,128)(2,1)S(1)} %get-tuple-element.6), channel_id=1, source_target_pairs={{0,1},{1,2},{2,3},{3,0},{4,5},{5,6},{6,7},{7,4},{8,9},{9,10},{10,1... | collective-permute-start | bytes 786440 | tf_op jit(solution)/shard_map/ppermute | solution.py:26
  237.2 25.0 %collective-permute-start.24 = (bf16[256,2048]{1,0:T(8,128)(2,1)S(1)}, bf16[256,2048]{1,0:T(8,128)(2,1)S(1)}, u32[]{:S(2)}, u32[]{:S(2)}) collective-permute-start(bf16[256,2048]{1,0:T(8,128)(2,1)S(1)} %pad_maximum_fusion.3), channel_id=1, source_target_pairs={{0,12},{1,13},{2,14},{3,15},{4,0},{5,1},{6,2},{7,3},{8,4},{9,5},{1... | collective-permute-start | bytes 3145736 | tf_op jit(solution)/shard_map/ppermute | solution.py:26
  237.7 26.3 %collective-permute-start.25 = (bf16[256,2048]{1,0:T(8,128)(2,1)S(1)}, bf16[256,2048]{1,0:T(8,128)(2,1)S(1)}, u32[]{:S(2)}, u32[]{:S(2)}) collective-permute-start(bf16[256,2048]{1,0:T(8,128)(2,1)S(1)} %pad_maximum_fusion.3), channel_id=1, source_target_pairs={{0,4},{1,5},{2,6},{3,7},{4,8},{5,9},{6,10},{7,11},{8,12},{9,13},{1... | collective-permute-start | bytes 3145736 | tf_op jit(solution)/shard_map/ppermute | solution.py:26
  262.3 12.9 %collective-permute-start.27 = (bf16[256,1024]{1,0:T(8,128)(2,1)S(1)}, bf16[256,1024]{1,0:T(8,128)(2,1)S(1)}, u32[]{:S(2)}, u32[]{:S(2)}) collective-permute-start(bf16[256,1024]{1,0:T(8,128)(2,1)S(1)} %slice.136), channel_id=1, source_target_pairs={{0,12},{1,13},{2,14},{3,15},{4,0},{5,1},{6,2},{7,3},{8,4},{9,5},{1... | collective-permute-start | bytes 1572872 | tf_op jit(solution)/shard_map/ppermute | solution.py:26
  264.0 13.8 %collective-permute-start.26 = (bf16[256,1024]{1,0:T(8,128)(2,1)S(1)}, bf16[256,1024]{1,0:T(8,128)(2,1)S(1)}, u32[]{:S(2)}, u32[]{:S(2)}) collective-permute-start(bf16[256,1024]{1,0:T(8,128)(2,1)S(1)} %slice.135), channel_id=1, source_target_pairs={{0,4},{1,5},{2,6},{3,7},{4,8},{5,9},{6,10},{7,11},{8,12},{9,13},{1... | collective-permute-start | bytes 1572872 | tf_op jit(solution)/shard_map/ppermute | solution.py:26
  300.5 15.3 %collective-permute-start.30 = (bf16[256,1024]{1,0:T(8,128)(2,1)S(1)}, bf16[256,1024]{1,0:T(8,128)(2,1)S(1)}, u32[]{:S(2)}, u32[]{:S(2)}) collective-permute-start(bf16[256,1024]{1,0:T(8,128)(2,1)S(1)} %get-tuple-element.11), channel_id=1, source_target_pairs={{0,4},{1,5},{2,6},{3,7},{4,8},{5,9},{6,10},{7,11},{8,12},{9,13},{1... | collective-permute-start | bytes 1572872 | tf_op jit(solution)/shard_map/ppermute | solution.py:26
  300.6 15.2 %collective-permute-start.32 = (bf16[256,1024]{1,0:T(8,128)(2,1)S(1)}, bf16[256,1024]{1,0:T(8,128)(2,1)S(1)}, u32[]{:S(2)}, u32[]{:S(2)}) collective-permute-start(bf16[256,1024]{1,0:T(8,128)(2,1)S(1)} %get-tuple-element.12), channel_id=1, source_target_pairs={{0,12},{1,13},{2,14},{3,15},{4,0},{5,1},{6,2},{7,3},{8,4},{9,5},{1... | collective-permute-start | bytes 1572872 | tf_op jit(solution)/shard_map/ppermute | solution.py:26
  316.3 24.6 %collective-permute-start.33 = (bf16[256,2048]{1,0:T(8,128)(2,1)S(1)}, bf16[256,2048]{1,0:T(8,128)(2,1)S(1)}, u32[]{:S(2)}, u32[]{:S(2)}) collective-permute-start(bf16[256,2048]{1,0:T(8,128)(2,1)S(1)} %pad_maximum_fusion.5), channel_id=1, source_target_pairs={{0,12},{1,13},{2,14},{3,15},{4,0},{5,1},{6,2},{7,3},{8,4},{9,5},{1... | collective-permute-start | bytes 3145736 | tf_op jit(solution)/shard_map/ppermute | solution.py:26
  319.4 25.1 %collective-permute-start.31 = (bf16[256,2048]{1,0:T(8,128)(2,1)S(1)}, bf16[256,2048]{1,0:T(8,128)(2,1)S(1)}, u32[]{:S(2)}, u32[]{:S(2)}) collective-permute-start(bf16[256,2048]{1,0:T(8,128)(2,1)S(1)} %pad_maximum_fusion.4), channel_id=1, source_target_pairs={{0,4},{1,5},{2,6},{3,7},{4,8},{5,9},{6,10},{7,11},{8,12},{9,13},{1... | collective-permute-start | bytes 3145736 | tf_op jit(solution)/shard_map/ppermute | solution.py:26
  345.1 17.6 %collective-permute-start.36 = (bf16[64,2048]{1,0:T(8,128)(2,1)S(1)}, bf16[64,2048]{1,0:T(8,128)(2,1)S(1)}, u32[]{:S(2)}, u32[]{:S(2)}) collective-permute-start(bf16[64,2048]{1,0:T(8,128)(2,1)S(1)} %get-tuple-element.22), channel_id=1, source_target_pairs={{0,3},{1,0},{2,1},{3,2},{4,7},{5,4},{6,5},{7,6},{8,11},{9,8},{10,9... | collective-permute-start | bytes 786440 | tf_op jit(solution)/shard_map/ppermute | solution.py:26
  350.6 18.6 %collective-permute-start.35 = (bf16[64,2048]{1,0:T(8,128)(2,1)S(1)}, bf16[64,2048]{1,0:T(8,128)(2,1)S(1)}, u32[]{:S(2)}, u32[]{:S(2)}) collective-permute-start(bf16[64,2048]{1,0:T(8,128)(2,1)S(1)} %get-tuple-element.23), channel_id=1, source_target_pairs={{0,2},{1,3},{2,0},{3,1},{4,6},{5,7},{6,4},{7,5},{8,10},{9,11},{10,... | collective-permute-start | bytes 786440 | tf_op jit(solution)/shard_map/ppermute | solution.py:26
  350.9 18.5 %collective-permute-start.34 = (bf16[64,2048]{1,0:T(8,128)(2,1)S(1)}, bf16[64,2048]{1,0:T(8,128)(2,1)S(1)}, u32[]{:S(2)}, u32[]{:S(2)}) collective-permute-start(bf16[64,2048]{1,0:T(8,128)(2,1)S(1)} %get-tuple-element.21), channel_id=1, source_target_pairs={{0,1},{1,2},{2,3},{3,0},{4,5},{5,6},{6,7},{7,4},{8,9},{9,10},{10,1... | collective-permute-start | bytes 786440 | tf_op jit(solution)/shard_map/ppermute | solution.py:26
  369.5 15.1 %collective-permute-start.39 = (bf16[64,2048]{1,0:T(8,128)(2,1)S(1)}, bf16[64,2048]{1,0:T(8,128)(2,1)S(1)}, u32[]{:S(2)}, u32[]{:S(2)}) collective-permute-start(bf16[64,2048]{1,0:T(8,128)(2,1)S(1)} %add_convert_fusion.8), channel_id=1, source_target_pairs={{0,96},{16,112},{32,64},{48,80},{64,32},{80,48},{96,0},{112,16},{1... | collective-permute-start | bytes 786440 | tf_op jit(solution)/shard_map/ppermute | solution.py:14
  372.4 12.3 %collective-permute-start.38 = (bf16[64,2048]{1,0:T(8,128)(2,1)S(1)}, bf16[64,2048]{1,0:T(8,128)(2,1)S(1)}, u32[]{:S(2)}, u32[]{:S(2)}) collective-permute-start(bf16[64,2048]{1,0:T(8,128)(2,1)S(1)} %add_convert_fusion.8), channel_id=1, source_target_pairs={{0,64},{16,80},{32,96},{48,112},{64,0},{80,16},{96,32},{112,48},{1... | collective-permute-start | bytes 786440 | tf_op jit(solution)/shard_map/ppermute | solution.py:14
  (11 other events, 126.9 us)

commit v2 on v1

--- a/solution.py
+++ b/solution.py
@@ -9,21 +9,13 @@
 epsilon = 1e-05
 
 
-def swapped(value, axis, mask):
-    pairs = [(source, source ^ mask) for source in range(lax.axis_size(axis))]
-    return lax.ppermute(value, axis, pairs)
-
-
-def tp_ring(value, inner, outer, stage, step):
+def permuted(value, sources, mapping):
+    tp_count = lax.axis_size("tp")
     pairs = []
-    for source in range(inner * outer):
-        high, low = divmod(source, inner)
-        if stage == "inner":
-            target = high * inner + (low + step) % inner
-        else:
-            target = ((high + step) % outer) * inner + low
-        pairs.append((source, target))
-    return lax.ppermute(value, "tp", pairs)
+    for section, tp in sources:
+        to_section, to_tp = mapping(section, tp)
+        pairs.append((section * tp_count + tp, to_section * tp_count + to_tp))
+    return lax.ppermute(value, ("section", "tp"), pairs)
 
 
 def ring_gather(block, ring):
@@ -70,11 +62,6 @@
     )
 
 
-def shifted(value, axis, steps):
-    count = lax.axis_size(axis)
-    return lax.ppermute(value, axis, [(source, source + steps) for source in range(count - steps)])
-
-
 def body(tokens, norm_gains, w_gate, w_up, w_down):
     section_count = lax.axis_size("section")
     split = section_count // LAYERS
@@ -90,11 +77,28 @@
     inner = 4
     outer = tp_count // inner
 
-    def inner_ring(value, step):
-        return tp_ring(value, inner, outer, "inner", step)
+    def group(layer):
+        return [(s, t) for s in range(layer * split, (layer + 1) * split) for t in range(tp_count)]
 
-    def outer_ring(value, step):
-        return tp_ring(value, inner, outer, "outer", step)
+    def inner_ring(layer):
+        def ring(value, step):
+            return permuted(
+                value, group(layer), lambda s, t: (s, (t // inner) * inner + (t % inner + step) % inner)
+            )
+        return ring
+
+    def outer_ring(layer):
+        def ring(value, step):
+            return permuted(
+                value, group(layer), lambda s, t: (s, ((t // inner + step) % outer) * inner + t % inner)
+            )
+        return ring
+
+    def swapped(value, layer, mask):
+        return permuted(value, group(layer), lambda s, t: (s ^ mask, t))
+
+    def forwarded(value, layer):
+        return permuted(value, group(layer), lambda s, t: (s + split, t))
 
     micro_count, tok_dev, model_width = tokens.shape
     piece_width = model_width // split
@@ -121,16 +125,16 @@
         rows = tokens.reshape(row_count, model_width).astype(jnp.float32)
         return pick(rows, 1, core), jnp.sum(rows * rows, axis=1, keepdims=True)
 
-    def from_received(received):
+    def from_received(received, layer):
         current = received.astype(jnp.float32)
         own_sq = jnp.sum(current * current, axis=1, keepdims=True)
-        return current, own_sq + swapped(own_sq, "section", 1)
+        return current, own_sq + swapped(own_sq, layer, 1)
 
-    def tick(current, square_sum):
+    def tick(current, square_sum, layer):
         inv_rms = lax.rsqrt(square_sum / model_width + epsilon)
         normed = (current * inv_rms * gain_own).astype(jnp.bfloat16)
-        gathered = ring_gather(direct_gather(normed, inner_ring), outer_ring)
-        gathered_other = swapped(gathered, "section", 1)
+        gathered = ring_gather(ring_gather(normed, inner_ring(layer)), outer_ring(layer))
+        gathered_other = swapped(gathered, layer, 1)
         gate_proj = jnp.dot(gathered, gate_own, preferred_element_type=jnp.float32) + jnp.dot(
             gathered_other, gate_other, preferred_element_type=jnp.float32
         )
@@ -139,12 +143,14 @@
         )
         active = (jax.nn.silu(gate_proj) * up_proj).astype(jnp.bfloat16)
         part_other = jnp.dot(active, down_other, preferred_element_type=jnp.float32).astype(jnp.bfloat16)
-        part_from_other = swapped(part_other, "section", 1)
+        part_from_other = swapped(part_other, layer, 1)
         part_own = jnp.dot(active, down_own, preferred_element_type=jnp.float32).astype(jnp.bfloat16)
         pair = (part_own.astype(jnp.float32) + part_from_other.astype(jnp.float32)).astype(jnp.bfloat16)
-        summed = direct_scatter(ring_scatter(pair, outer_ring).astype(jnp.bfloat16), inner_ring).astype(jnp.bfloat16)
+        summed = ring_scatter(
+            ring_scatter(pair, outer_ring(layer)).astype(jnp.bfloat16), inner_ring(layer)
+        ).astype(jnp.bfloat16)
         summed = summed.astype(jnp.float32) + sum(
-            swapped(summed, "section", 2 * mask).astype(jnp.float32) for mask in range(1, x_count)
+            swapped(summed, layer, 2 * mask).astype(jnp.float32) for mask in range(1, x_count)
         )
         full_half = (current + summed.astype(jnp.float32)).astype(jnp.bfloat16)
         block = lax.dynamic_index_in_dim(
@@ -158,11 +164,11 @@
         if tick_index == 0:
             current, square_sum = from_tokens()
         else:
-            current, square_sum = from_received(received)
-        full_half, block = tick(current, square_sum)
+            current, square_sum = from_received(received, tick_index)
+        full_half, block = tick(current, square_sum, tick_index)
         blocks.append(block)
         if tick_index < LAYERS - 1:
-            received = shifted(full_half, "section", split)
+            received = forwarded(full_half, tick_index)
 
     stacked = jnp.stack(blocks, axis=0)
     mine = lax.dynamic_index_in_dim(stacked, section_layer, 0, keepdims=False)

time: 394 us -> 408 us (1.036); the launches traced: 387 us -> 407 us
  starting transfers between devices: 70.4 us -> 91 us
    ppermute x40 -> x44, starting transfers between devices: 70.4 us -> 91 us  [permuted(): return lax.ppermute(value, ('section', 'tp'), pairs)]
    ppermute x40 -> x44, waiting for transfers between devices: 272 us -> 271 us  [permuted(): return lax.ppermute(value, ('section', 'tp'), pairs)]
  transfers between devices with their start and end apart: 40 -> 44, of which waited for: 33 -> 21; matrix products, arithmetic and copies ran while one was open for 2% -> 2% of each run, Pallas kernels for 0% -> 0%
where the time goes in v2:
time: 408 us; the launch traced here: 407 us
  waiting for transfers between devices  271 us (66%)
  starting transfers between devices  91 us (22%)
  matrix products  23.9 us (6%)
  local copies, waits for them, and re-layouts  13.6 us (3%)
  other arithmetic  7.29 us (2%)
    ppermute x44, waiting for transfers between devices, permuted(): return lax.ppermute(value, ('section', 'tp'), pairs)  271 us
    ppermute x44, starting transfers between devices, permuted(): return lax.ppermute(value, ('section', 'tp'), pairs)  91 us
  transfers between devices with their start and end apart: 44, of which 21 were waited for; matrix products, arithmetic and copies ran while one was open for 2% of the time, Pallas kernels for 0%

profile of v2, /device:TPU:32, one launch (start us, length us, event | category | flops | bytes accessed | tf_op | source)
XLA Modules:
  0.0 407.3 jit_solution(2401679939568287331)
XLA Ops:
  18.0 2.7 collective-permute-start.8
  23.8 3.4 fusion.10
  27.2 3.5 convolution_add_fusion.3
  30.7 3.4 fusion.11
  34.1 3.4 multiply_convert_fusion.1
  52.1 163.5 %collective-permute-done.21 = bf16[64,2048]{1,0:T(8,128)(2,1)S(1)} collective-permute-done((bf16[64,2048]{1,0:T(8,128)(2,1)S(1)}, bf16[64,2048]{1,0:T(8,128)(2,1)S(1)}, u32[]{:S(2)}, u32[]{:S(2)}) %collective-permute-start.21) | collective-permute-done | bytes 262176 | tf_op jit(solution)/shard_map/ppermute | solution.py:18
  220.9 6.0 %collective-permute-start.23 = (bf16[64,2048]{1,0:T(8,128)(2,1)S(1)}, bf16[64,2048]{1,0:T(8,128)(2,1)S(1)}, u32[]{:S(2)}, u32[]{:S(2)}) collective-permute-start(bf16[64,2048]{1,0:T(8,128)(2,1)S(1)} %get-tuple-element.6), channel_id=1, source_target_pairs={{128,131},{129,128},{130,129},{131,130},{132,135},{133,132},{134,1... | collective-permute-start | bytes 786440 | tf_op jit(solution)/shard_map/ppermute | solution.py:18
  226.9 4.4 %collective-permute-done.24 = bf16[64,2048]{1,0:T(8,128)(2,1)S(1)} collective-permute-done((bf16[64,2048]{1,0:T(8,128)(2,1)S(1)}, bf16[64,2048]{1,0:T(8,128)(2,1)S(1)}, u32[]{:S(2)}, u32[]{:S(2)}) %collective-permute-start.24) | collective-permute-done | bytes 262176 | tf_op jit(solution)/shard_map/ppermute | solution.py:18
  233.3 6.0 %collective-permute-start.26 = (bf16[64,1024]{1,0:T(8,128)(2,1)S(1)}, bf16[64,1024]{1,0:T(8,128)(2,1)S(1)}, u32[]{:S(2)}, u32[]{:S(2)}) collective-permute-start(bf16[64,1024]{1,0:T(8,128)(2,1)S(1)} %slice.199), channel_id=1, source_target_pairs={{128,131},{129,128},{130,129},{131,130},{132,135},{133,132},{134,1... | collective-permute-start | bytes 393224 | tf_op jit(solution)/shard_map/ppermute | solution.py:18
  243.9 3.9 collective-permute-start.28
  247.9 19.5 %collective-permute-done.27 = bf16[256,2048]{1,0:T(8,128)(2,1)S(1)} collective-permute-done((bf16[256,2048]{1,0:T(8,128)(2,1)S(1)}, bf16[256,2048]{1,0:T(8,128)(2,1)S(1)}, u32[]{:S(2)}, u32[]{:S(2)}) %collective-permute-start.27) | collective-permute-done | bytes 1048608 | tf_op jit(solution)/shard_map/ppermute | solution.py:18
  267.4 3.4 collective-permute-start.30
  270.9 2.4 collective-permute-start.29
  273.4 7.3 %collective-permute-done.30 = bf16[256,1024]{1,0:T(8,128)(2,1)S(1)} collective-permute-done((bf16[256,1024]{1,0:T(8,128)(2,1)S(1)}, bf16[256,1024]{1,0:T(8,128)(2,1)S(1)}, u32[]{:S(2)}, u32[]{:S(2)}) %collective-permute-start.30) | collective-permute-done | bytes 524320 | tf_op jit(solution)/shard_map/ppermute | solution.py:18
  280.7 4.7 %collective-permute-done.29 = bf16[256,1024]{1,0:T(8,128)(2,1)S(1)} collective-permute-done((bf16[256,1024]{1,0:T(8,128)(2,1)S(1)}, bf16[256,1024]{1,0:T(8,128)(2,1)S(1)}, u32[]{:S(2)}, u32[]{:S(2)}) %collective-permute-start.29) | collective-permute-done | bytes 524320 | tf_op jit(solution)/shard_map/ppermute | solution.py:18
  287.8 6.9 %collective-permute-done.31 = bf16[1024,2048]{1,0:T(8,128)(2,1)S(1)} collective-permute-done((bf16[1024,2048]{1,0:T(8,128)(2,1)S(1)}, bf16[1024,2048]{1,0:T(8,128)(2,1)S(1)}, u32[]{:S(2)}, u32[]{:S(2)}) %collective-permute-start.31) | collective-permute-done | bytes 4194336 | tf_op jit(solution)/shard_map/ppermute | solution.py:18
  303.1 7.0 %collective-permute-done.32 = bf16[1024,2048]{1,0:T(8,128)(2,1)S(1)} collective-permute-done((bf16[1024,2048]{1,0:T(8,128)(2,1)S(1)}, bf16[1024,2048]{1,0:T(8,128)(2,1)S(1)}, u32[]{:S(2)}, u32[]{:S(2)}) %collective-permute-start.32) | collective-permute-done | bytes 4194336 | tf_op jit(solution)/shard_map/ppermute | solution.py:18
  313.5 5.1 %collective-permute-start.35 = (bf16[256,1024]{1,0:T(8,128)(2,1)S(1)}, bf16[256,1024]{1,0:T(8,128)(2,1)S(1)}, u32[]{:S(2)}, u32[]{:S(2)}) collective-permute-start(bf16[256,1024]{1,0:T(8,128)(2,1)S(1)} %get-tuple-element.12), channel_id=1, source_target_pairs={{128,140},{129,141},{130,142},{131,143},{132,128},{133,129},{134,1... | collective-permute-start | bytes 1572872 | tf_op jit(solution)/shard_map/ppermute | solution.py:18
  318.7 10.0 %collective-permute-done.33 = bf16[256,1024]{1,0:T(8,128)(2,1)S(1)} collective-permute-done((bf16[256,1024]{1,0:T(8,128)(2,1)S(1)}, bf16[256,1024]{1,0:T(8,128)(2,1)S(1)}, u32[]{:S(2)}, u32[]{:S(2)}) %collective-permute-start.33) | collective-permute-done | bytes 524320 | tf_op jit(solution)/shard_map/ppermute | solution.py:18
  330.3 5.6 %collective-permute-start.36 = (bf16[256,2048]{1,0:T(8,128)(2,1)S(1)}, bf16[256,2048]{1,0:T(8,128)(2,1)S(1)}, u32[]{:S(2)}, u32[]{:S(2)}) collective-permute-start(bf16[256,2048]{1,0:T(8,128)(2,1)S(1)} %pad_maximum_fusion.5), channel_id=1, source_target_pairs={{128,140},{129,141},{130,142},{131,143},{132,128},{133,129},{134,1... | collective-permute-start | bytes 3145736 | tf_op jit(solution)/shard_map/ppermute | solution.py:18
  337.9 19.5 %collective-permute-done.36 = bf16[256,2048]{1,0:T(8,128)(2,1)S(1)} collective-permute-done((bf16[256,2048]{1,0:T(8,128)(2,1)S(1)}, bf16[256,2048]{1,0:T(8,128)(2,1)S(1)}, u32[]{:S(2)}, u32[]{:S(2)}) %collective-permute-start.36) | collective-permute-done | bytes 1048608 | tf_op jit(solution)/shard_map/ppermute | solution.py:18
  357.5 5.4 %collective-permute-done.34 = bf16[256,2048]{1,0:T(8,128)(2,1)S(1)} collective-permute-done((bf16[256,2048]{1,0:T(8,128)(2,1)S(1)}, bf16[256,2048]{1,0:T(8,128)(2,1)S(1)}, u32[]{:S(2)}, u32[]{:S(2)}) %collective-permute-start.34) | collective-permute-done | bytes 1048608 | tf_op jit(solution)/shard_map/ppermute | solution.py:18
  363.5 4.9 %collective-permute-start.37 = (bf16[64,1024]{1,0:T(8,128)(2,1)S(1)}, bf16[64,1024]{1,0:T(8,128)(2,1)S(1)}, u32[]{:S(2)}, u32[]{:S(2)}) collective-permute-start(bf16[64,1024]{1,0:T(8,128)(2,1)S(1)} %get-tuple-element.23), channel_id=1, source_target_pairs={{128,129},{129,130},{130,131},{131,128},{132,133},{133,134},{134,1... | collective-permute-start | bytes 393224 | tf_op jit(solution)/shard_map/ppermute | solution.py:18
  368.4 3.1 collective-permute-start.39
  372.5 3.7 collective-permute-done.39
  376.2 4.3 %collective-permute-start.40 = (bf16[64,2048]{1,0:T(8,128)(2,1)S(1)}, bf16[64,2048]{1,0:T(8,128)(2,1)S(1)}, u32[]{:S(2)}, u32[]{:S(2)}) collective-permute-start(bf16[64,2048]{1,0:T(8,128)(2,1)S(1)} %pad_maximum_fusion.9), channel_id=1, source_target_pairs={{128,131},{129,128},{130,129},{131,130},{132,135},{133,132},{134,1... | collective-permute-start | bytes 786440 | tf_op jit(solution)/shard_map/ppermute | solution.py:18
  380.6 2.5 collective-permute-start.38
  385.4 5.5 %collective-permute-done.38 = bf16[64,2048]{1,0:T(8,128)(2,1)S(1)} collective-permute-done((bf16[64,2048]{1,0:T(8,128)(2,1)S(1)}, bf16[64,2048]{1,0:T(8,128)(2,1)S(1)}, u32[]{:S(2)}, u32[]{:S(2)}) %collective-permute-start.38) | collective-permute-done | bytes 262176 | tf_op jit(solution)/shard_map/ppermute | solution.py:18
  391.0 4.1 collective-permute-start.43
  395.1 2.7 collective-permute-start.42
  397.8 3.0 collective-permute-start.41
  401.4 3.4 collective-permute-done.42
  (143 shorter events, 71.9 us)
Async XLA Ops:
  9.0 2.9 collective-permute-start.4
  9.8 2.9 collective-permute-start.5
  12.0 3.9 collective-permute-start.7
  12.7 3.2 collective-permute-start.6
  18.0 5.8 %collective-permute-start.8 = (bf16[1024,2048]{1,0:T(8,128)(2,1)}, bf16[1024,2048]{1,0:T(8,128)(2,1)}, u32[]{:S(2)}, u32[]{:S(2)}) collective-permute-start(bf16[1024,2048]{1,0:T(8,128)(2,1)} %constant_dynamic-update-slice_fusion), channel_id=1, source_target_pairs={{0,16},{1,17},{2,18},{3,19},{4,20},{5,21},{6,22},{7,23},{8,24},{9,... | collective-permute-start | bytes 12582920 | tf_op jit(solution)/shard_map/ppermute | solution.py:18
  41.4 1.4 collective-permute-start.10
  43.4 1.6 collective-permute-start.13
  47.0 1.4 collective-permute-start.17
  48.5 2.1 collective-permute-start.20
  50.8 164.8 %collective-permute-start.21 = (bf16[64,2048]{1,0:T(8,128)(2,1)S(1)}, bf16[64,2048]{1,0:T(8,128)(2,1)S(1)}, u32[]{:S(2)}, u32[]{:S(2)}) collective-permute-start(bf16[64,2048]{1,0:T(8,128)(2,1)S(1)} %add_convert_fusion.9), channel_id=1, source_target_pairs={{0,128},{1,129},{2,130},{3,131},{4,132},{5,133},{6,134},{7,135},{8... | collective-permute-start | bytes 786440 | tf_op jit(solution)/shard_map/ppermute | solution.py:18
  215.7 3.0 collective-permute-start.22
  218.9 12.4 %collective-permute-start.24 = (bf16[64,2048]{1,0:T(8,128)(2,1)S(1)}, bf16[64,2048]{1,0:T(8,128)(2,1)S(1)}, u32[]{:S(2)}, u32[]{:S(2)}) collective-permute-start(bf16[64,2048]{1,0:T(8,128)(2,1)S(1)} %get-tuple-element.6), channel_id=1, source_target_pairs={{128,129},{129,130},{130,131},{131,128},{132,133},{133,134},{134,1... | collective-permute-start | bytes 786440 | tf_op jit(solution)/shard_map/ppermute | solution.py:18
  220.9 12.4 %collective-permute-start.23 = (bf16[64,2048]{1,0:T(8,128)(2,1)S(1)}, bf16[64,2048]{1,0:T(8,128)(2,1)S(1)}, u32[]{:S(2)}, u32[]{:S(2)}) collective-permute-start(bf16[64,2048]{1,0:T(8,128)(2,1)S(1)} %get-tuple-element.6), channel_id=1, source_target_pairs={{128,131},{129,128},{130,129},{131,130},{132,135},{133,132},{134,1... | collective-permute-start | bytes 786440 | tf_op jit(solution)/shard_map/ppermute | solution.py:18
  231.3 9.0 %collective-permute-start.25 = (bf16[64,1024]{1,0:T(8,128)(2,1)S(1)}, bf16[64,1024]{1,0:T(8,128)(2,1)S(1)}, u32[]{:S(2)}, u32[]{:S(2)}) collective-permute-start(bf16[64,1024]{1,0:T(8,128)(2,1)S(1)} %slice.198), channel_id=1, source_target_pairs={{128,129},{129,130},{130,131},{131,128},{132,133},{133,134},{134,1... | collective-permute-start | bytes 393224 | tf_op jit(solution)/shard_map/ppermute | solution.py:18
  233.3 8.6 %collective-permute-start.26 = (bf16[64,1024]{1,0:T(8,128)(2,1)S(1)}, bf16[64,1024]{1,0:T(8,128)(2,1)S(1)}, u32[]{:S(2)}, u32[]{:S(2)}) collective-permute-start(bf16[64,1024]{1,0:T(8,128)(2,1)S(1)} %slice.199), channel_id=1, source_target_pairs={{128,131},{129,128},{130,129},{131,130},{132,135},{133,132},{134,1... | collective-permute-start | bytes 393224 | tf_op jit(solution)/shard_map/ppermute | solution.py:18
  242.0 25.4 %collective-permute-start.27 = (bf16[256,2048]{1,0:T(8,128)(2,1)S(1)}, bf16[256,2048]{1,0:T(8,128)(2,1)S(1)}, u32[]{:S(2)}, u32[]{:S(2)}) collective-permute-start(bf16[256,2048]{1,0:T(8,128)(2,1)S(1)} %pad_maximum_fusion.3), channel_id=1, source_target_pairs={{128,140},{129,141},{130,142},{131,143},{132,128},{133,129},{134,1... | collective-permute-start | bytes 3145736 | tf_op jit(solution)/shard_map/ppermute | solution.py:18
  243.9 27.0 %collective-permute-start.28 = (bf16[256,2048]{1,0:T(8,128)(2,1)S(1)}, bf16[256,2048]{1,0:T(8,128)(2,1)S(1)}, u32[]{:S(2)}, u32[]{:S(2)}) collective-permute-start(bf16[256,2048]{1,0:T(8,128)(2,1)S(1)} %pad_maximum_fusion.3), channel_id=1, source_target_pairs={{128,132},{129,133},{130,134},{131,135},{132,136},{133,137},{134,1... | collective-permute-start | bytes 3145736 | tf_op jit(solution)/shard_map/ppermute | solution.py:18
  267.4 13.3 %collective-permute-start.30 = (bf16[256,1024]{1,0:T(8,128)(2,1)S(1)}, bf16[256,1024]{1,0:T(8,128)(2,1)S(1)}, u32[]{:S(2)}, u32[]{:S(2)}) collective-permute-start(bf16[256,1024]{1,0:T(8,128)(2,1)S(1)} %slice.201), channel_id=1, source_target_pairs={{128,140},{129,141},{130,142},{131,143},{132,128},{133,129},{134,1... | collective-permute-start | bytes 1572872 | tf_op jit(solution)/shard_map/ppermute | solution.py:18
  270.9 14.5 %collective-permute-start.29 = (bf16[256,1024]{1,0:T(8,128)(2,1)S(1)}, bf16[256,1024]{1,0:T(8,128)(2,1)S(1)}, u32[]{:S(2)}, u32[]{:S(2)}) collective-permute-start(bf16[256,1024]{1,0:T(8,128)(2,1)S(1)} %slice.200), channel_id=1, source_target_pairs={{128,132},{129,133},{130,134},{131,135},{132,136},{133,137},{134,1... | collective-permute-start | bytes 1572872 | tf_op jit(solution)/shard_map/ppermute | solution.py:18
  285.6 9.1 %collective-permute-start.31 = (bf16[1024,2048]{1,0:T(8,128)(2,1)S(1)}, bf16[1024,2048]{1,0:T(8,128)(2,1)S(1)}, u32[]{:S(2)}, u32[]{:S(2)}) collective-permute-start(bf16[1024,2048]{1,0:T(8,128)(2,1)S(1)} %constant_dynamic-update-slice_fusion.6), channel_id=1, source_target_pairs={{128,144},{129,145},{130,146},{131,147},{132,148},{133,149},{134,1... | collective-permute-start | bytes 12582920 | tf_op jit(solution)/shard_map/ppermute | solution.py:18
  301.1 9.1 %collective-permute-start.32 = (bf16[1024,2048]{1,0:T(8,128)(2,1)S(1)}, bf16[1024,2048]{1,0:T(8,128)(2,1)S(1)}, u32[]{:S(2)}, u32[]{:S(2)}) collective-permute-start(bf16[1024,2048]{1,0:T(8,128)(2,1)S(1)} %convolution_convert_fusion), channel_id=1, source_target_pairs={{128,144},{129,145},{130,146},{131,147},{132,148},{133,149},{134,1... | collective-permute-start | bytes 12582920 | tf_op jit(solution)/shard_map/ppermute | solution.py:18
  311.6 17.1 %collective-permute-start.33 = (bf16[256,1024]{1,0:T(8,128)(2,1)S(1)}, bf16[256,1024]{1,0:T(8,128)(2,1)S(1)}, u32[]{:S(2)}, u32[]{:S(2)}) collective-permute-start(bf16[256,1024]{1,0:T(8,128)(2,1)S(1)} %get-tuple-element.11), channel_id=1, source_target_pairs={{128,132},{129,133},{130,134},{131,135},{132,136},{133,137},{134,1... | collective-permute-start | bytes 1572872 | tf_op jit(solution)/shard_map/ppermute | solution.py:18
  313.5 16.3 %collective-permute-start.35 = (bf16[256,1024]{1,0:T(8,128)(2,1)S(1)}, bf16[256,1024]{1,0:T(8,128)(2,1)S(1)}, u32[]{:S(2)}, u32[]{:S(2)}) collective-permute-start(bf16[256,1024]{1,0:T(8,128)(2,1)S(1)} %get-tuple-element.12), channel_id=1, source_target_pairs={{128,140},{129,141},{130,142},{131,143},{132,128},{133,129},{134,1... | collective-permute-start | bytes 1572872 | tf_op jit(solution)/shard_map/ppermute | solution.py:18
  330.3 27.2 %collective-permute-start.36 = (bf16[256,2048]{1,0:T(8,128)(2,1)S(1)}, bf16[256,2048]{1,0:T(8,128)(2,1)S(1)}, u32[]{:S(2)}, u32[]{:S(2)}) collective-permute-start(bf16[256,2048]{1,0:T(8,128)(2,1)S(1)} %pad_maximum_fusion.5), channel_id=1, source_target_pairs={{128,140},{129,141},{130,142},{131,143},{132,128},{133,129},{134,1... | collective-permute-start | bytes 3145736 | tf_op jit(solution)/shard_map/ppermute | solution.py:18
  336.0 26.9 %collective-permute-start.34 = (bf16[256,2048]{1,0:T(8,128)(2,1)S(1)}, bf16[256,2048]{1,0:T(8,128)(2,1)S(1)}, u32[]{:S(2)}, u32[]{:S(2)}) collective-permute-start(bf16[256,2048]{1,0:T(8,128)(2,1)S(1)} %pad_maximum_fusion.4), channel_id=1, source_target_pairs={{128,132},{129,133},{130,134},{131,135},{132,136},{133,137},{134,1... | collective-permute-start | bytes 3145736 | tf_op jit(solution)/shard_map/ppermute | solution.py:18
  363.5 9.0 %collective-permute-start.37 = (bf16[64,1024]{1,0:T(8,128)(2,1)S(1)}, bf16[64,1024]{1,0:T(8,128)(2,1)S(1)}, u32[]{:S(2)}, u32[]{:S(2)}) collective-permute-start(bf16[64,1024]{1,0:T(8,128)(2,1)S(1)} %get-tuple-element.23), channel_id=1, source_target_pairs={{128,129},{129,130},{130,131},{131,128},{132,133},{133,134},{134,1... | collective-permute-start | bytes 393224 | tf_op jit(solution)/shard_map/ppermute | solution.py:18
  368.4 7.8 %collective-permute-start.39 = (bf16[64,1024]{1,0:T(8,128)(2,1)S(1)}, bf16[64,1024]{1,0:T(8,128)(2,1)S(1)}, u32[]{:S(2)}, u32[]{:S(2)}) collective-permute-start(bf16[64,1024]{1,0:T(8,128)(2,1)S(1)} %get-tuple-element.24), channel_id=1, source_target_pairs={{128,131},{129,128},{130,129},{131,130},{132,135},{133,132},{134,1... | collective-permute-start | bytes 393224 | tf_op jit(solution)/shard_map/ppermute | solution.py:18
  376.2 9.2 %collective-permute-start.40 = (bf16[64,2048]{1,0:T(8,128)(2,1)S(1)}, bf16[64,2048]{1,0:T(8,128)(2,1)S(1)}, u32[]{:S(2)}, u32[]{:S(2)}) collective-permute-start(bf16[64,2048]{1,0:T(8,128)(2,1)S(1)} %pad_maximum_fusion.9), channel_id=1, source_target_pairs={{128,131},{129,128},{130,129},{131,130},{132,135},{133,132},{134,1... | collective-permute-start | bytes 786440 | tf_op jit(solution)/shard_map/ppermute | solution.py:18
  380.6 10.4 %collective-permute-start.38 = (bf16[64,2048]{1,0:T(8,128)(2,1)S(1)}, bf16[64,2048]{1,0:T(8,128)(2,1)S(1)}, u32[]{:S(2)}, u32[]{:S(2)}) collective-permute-start(bf16[64,2048]{1,0:T(8,128)(2,1)S(1)} %pad_maximum_fusion.8), channel_id=1, source_target_pairs={{128,129},{129,130},{130,131},{131,128},{132,133},{133,134},{134,1... | collective-permute-start | bytes 786440 | tf_op jit(solution)/shard_map/ppermute | solution.py:18
  391.0 10.4 %collective-permute-start.43 = (bf16[64,2048]{1,0:T(8,128)(2,1)S(1)}, bf16[64,2048]{1,0:T(8,128)(2,1)S(1)}, u32[]{:S(2)}, u32[]{:S(2)}) collective-permute-start(bf16[64,2048]{1,0:T(8,128)(2,1)S(1)} %add_convert_fusion.8), channel_id=1, source_target_pairs={{128,224},{129,225},{130,226},{131,227},{132,228},{133,229},{134,2... | collective-permute-start | bytes 786440 | tf_op jit(solution)/shard_map/ppermute | solution.py:18
  395.1 9.8 %collective-permute-start.42 = (bf16[64,2048]{1,0:T(8,128)(2,1)S(1)}, bf16[64,2048]{1,0:T(8,128)(2,1)S(1)}, u32[]{:S(2)}, u32[]{:S(2)}) collective-permute-start(bf16[64,2048]{1,0:T(8,128)(2,1)S(1)} %add_convert_fusion.8), channel_id=1, source_target_pairs={{128,192},{129,193},{130,194},{131,195},{132,196},{133,197},{134,1... | collective-permute-start | bytes 786440 | tf_op jit(solution)/shard_map/ppermute | solution.py:18
  397.8 8.3 %collective-permute-start.41 = (bf16[64,2048]{1,0:T(8,128)(2,1)S(1)}, bf16[64,2048]{1,0:T(8,128)(2,1)S(1)}, u32[]{:S(2)}, u32[]{:S(2)}) collective-permute-start(bf16[64,2048]{1,0:T(8,128)(2,1)S(1)} %add_convert_fusion.8), channel_id=1, source_target_pairs={{128,160},{129,161},{130,162},{131,163},{132,164},{133,165},{134,1... | collective-permute-start | bytes 786440 | tf_op jit(solution)/shard_map/ppermute | solution.py:18
  (15 other events, 68.3 us)

commit v3 on v0

--- a/solution.py
+++ b/solution.py
@@ -125,8 +125,10 @@
         rows = tokens[micro_index, part * row_count:(part + 1) * row_count].astype(jnp.float32)
         return pick(rows, 1, core), jnp.sum(rows * rows, axis=1, keepdims=True)
 
-    def from_received(received):
-        current = received.astype(jnp.float32)
+    def from_received(partials, piece_index):
+        base, _ = from_tokens(piece_index)
+        total = base + sum(part.astype(jnp.float32) for part in partials)
+        current = total.astype(jnp.bfloat16).astype(jnp.float32)
         own_sq = jnp.sum(current * current, axis=1, keepdims=True)
         return current, own_sq + swapped(own_sq, "section", 1)
 
@@ -146,15 +148,17 @@
         part_from_other = swapped(part_other, "section", 1)
         part_own = jnp.dot(active, down_own, preferred_element_type=jnp.float32).astype(jnp.bfloat16)
         pair = (part_own.astype(jnp.float32) + part_from_other.astype(jnp.float32)).astype(jnp.bfloat16)
-        summed = direct_scatter(ring_scatter(pair, outer_ring).astype(jnp.bfloat16), inner_ring).astype(jnp.bfloat16)
-        summed = summed.astype(jnp.float32) + sum(
-            swapped(summed, "section", 2 * mask).astype(jnp.float32) for mask in range(1, x_count)
+        reduced = direct_scatter(ring_scatter(pair, outer_ring).astype(jnp.bfloat16), inner_ring).astype(jnp.bfloat16)
+        pieces = reduced.reshape(row_count, x_count, piece_width)
+        own_piece = lax.dynamic_index_in_dim(pieces, xpos, 1, keepdims=False).astype(jnp.float32)
+        for mask in range(1, x_count):
+            sent = lax.dynamic_index_in_dim(pieces, xpos ^ mask, 1, keepdims=False)
+            own_piece = own_piece + swapped(sent, "section", 2 * mask).astype(jnp.float32)
+        current_piece = lax.dynamic_index_in_dim(
+            current.reshape(row_count, x_count, piece_width), xpos, 1, keepdims=False
         )
-        full_half = (current + summed.astype(jnp.float32)).astype(jnp.bfloat16)
-        block = lax.dynamic_index_in_dim(
-            full_half.reshape(row_count, x_count, piece_width), xpos, 1, keepdims=False
-        )
-        return full_half, block
+        block = (current_piece + own_piece).astype(jnp.bfloat16)
+        return reduced, block
 
     blocks = []
     received = None
@@ -162,17 +166,24 @@
         if tick_index == 0:
             current, square_sum = from_tokens(0)
         elif tick_index >= piece_count:
-            current, square_sum = from_received(received)
+            current, square_sum = from_received(received, tick_index - 1)
         else:
             first_current, first_sum = from_tokens(tick_index)
-            later_current, later_sum = from_received(received)
+            later_current, later_sum = from_received(received, tick_index - 1)
             is_first = section_layer == 0
             current = jnp.where(is_first, first_current, later_current)
             square_sum = jnp.where(is_first, first_sum, later_sum)
-        full_half, block = tick(current, square_sum)
+        reduced, block = tick(current, square_sum)
         blocks.append(block)
         if tick_index < tick_count - 1:
-            received = shifted(full_half, "section", split)
+            received = [
+                lax.ppermute(
+                    reduced,
+                    "section",
+                    [(source, (source + split) ^ (2 * mask)) for source in range(section_count - split)],
+                )
+                for mask in range(x_count)
+            ]
 
     stacked = jnp.stack(blocks, axis=0)
     outputs = []

time: 358 us -> 364 us (1.017)
  waiting for transfers between devices: 216 us -> 185 us
  starting transfers between devices: 97 us -> 123 us
  local copies, waits for them, and re-layouts: 14.2 us -> 19.3 us
  other arithmetic: 7.23 us -> 12.3 us
    ppermute x42, waiting for transfers between devices: 167 us -> 143 us  [tp_ring(): return lax.ppermute(value, 'tp', pairs)]
    ppermute x42, starting transfers between devices: 79.9 us -> 95.1 us  [tp_ring(): return lax.ppermute(value, 'tp', pairs)]
    ppermute x17, waiting for transfers between devices: 37.4 us -> 26.1 us  [swapped(): return lax.ppermute(value, axis, pairs)]
    ppermute x2 -> x8, starting transfers between devices: 2.58 us -> 10.3 us  [body(): lax.ppermute(reduced, 'section', [(source, source + split ^ 2 * mask) for...]
    ppermute x2 -> x8, waiting for transfers between devices: 11.1 us -> 16.5 us  [body(): lax.ppermute(reduced, 'section', [(source, source + split ^ 2 * mask) for...]
    unnamed x40 -> x60, local copies, waits for them, and re-layouts: 6.06 us -> 7.45 us
  transfers between devices with their start and end apart: 61 -> 67, of which waited for: 50 -> 45; matrix products, arithmetic and copies ran while one was open for 3% -> 5% of each run, Pallas kernels for 0% -> 0%
where the time goes in v3:
time: 364 us; the launch traced here: 357 us
  waiting for transfers between devices  185 us (51%)
  starting transfers between devices  123 us (34%)
  local copies, waits for them, and re-layouts  19.3 us (5%)
  matrix products  16 us (4%)
  other arithmetic  12.3 us (3%)
    ppermute x42, waiting for transfers between devices, tp_ring(): return lax.ppermute(value, 'tp', pairs)  143 us
    ppermute x42, starting transfers between devices, tp_ring(): return lax.ppermute(value, 'tp', pairs)  95.1 us
    ppermute x17, waiting for transfers between devices, swapped(): return lax.ppermute(value, axis, pairs)  26.1 us
    ppermute x17, starting transfers between devices, swapped(): return lax.ppermute(value, axis, pairs)  17.1 us
    ppermute x8, waiting for transfers between devices, body(): lax.ppermute(reduced, 'section', [(source, source + split ^ 2 * mask) for...  16.5 us
    ppermute x8, starting transfers between devices, body(): lax.ppermute(reduced, 'section', [(source, source + split ^ 2 * mask) for...  10.3 us
    unnamed x60, local copies, waits for them, and re-layouts  7.45 us
  transfers between devices with their start and end apart: 67, of which 45 were waited for; matrix products, arithmetic and copies ran while one was open for 5% of the time, Pallas kernels for 0%

profile of v3, /device:TPU:32, one launch (start us, length us, event | category | flops | bytes accessed | tf_op | source)
XLA Modules:
  0.0 357.1 jit_solution(7090011468048638321)
XLA Ops:
  9.7 4.5 %collective-permute-start.1 = (bf16[32,2048]{1,0:T(8,128)(2,1)S(1)}, bf16[32,2048]{1,0:T(8,128)(2,1)S(1)}, u32[]{:S(2)}, u32[]{:S(2)}) collective-permute-start(bf16[32,2048]{1,0:T(8,128)(2,1)S(1)} %get-tuple-element.17), channel_id=1, source_target_pairs={{0,2},{1,3},{2,0},{3,1},{4,6},{5,7},{6,4},{7,5},{8,10},{9,11},{10,... | collective-permute-start | bytes 393224 | tf_op jit(solution)/shard_map/ppermute | solution.py:27
  28.7 9.1 %collective-permute-done.4 = bf16[128,2048]{1,0:T(8,128)(2,1)S(1)} collective-permute-done((bf16[128,2048]{1,0:T(8,128)(2,1)S(1)}, bf16[128,2048]{1,0:T(8,128)(2,1)S(1)}, u32[]{:S(2)}, u32[]{:S(2)}) %collective-permute-start.4) | collective-permute-done | bytes 524320 | tf_op jit(solution)/shard_map/ppermute | solution.py:27
  60.2 3.8 %collective-permute-done.8 = bf16[512,2048]{1,0:T(8,128)(2,1)S(1)} collective-permute-done((bf16[512,2048]{1,0:T(8,128)(2,1)S(1)}, bf16[512,2048]{1,0:T(8,128)(2,1)S(1)}, u32[]{:S(2)}, u32[]{:S(2)}) %collective-permute-start.8) | collective-permute-done | bytes 2097184 | tf_op jit(solution)/shard_map/ppermute | solution.py:15
  68.3 6.8 %collective-permute-done.9 = bf16[128,1024]{1,0:T(8,128)(2,1)S(1)} collective-permute-done((bf16[128,1024]{1,0:T(8,128)(2,1)S(1)}, bf16[128,1024]{1,0:T(8,128)(2,1)S(1)}, u32[]{:S(2)}, u32[]{:S(2)}) %collective-permute-start.9) | collective-permute-done | bytes 262176 | tf_op jit(solution)/shard_map/ppermute | solution.py:27
  78.6 10.7 %collective-permute-done.12 = bf16[128,2048]{1,0:T(8,128)(2,1)S(1)} collective-permute-done((bf16[128,2048]{1,0:T(8,128)(2,1)S(1)}, bf16[128,2048]{1,0:T(8,128)(2,1)S(1)}, u32[]{:S(2)}, u32[]{:S(2)}) %collective-permute-start.12) | collective-permute-done | bytes 524320 | tf_op jit(solution)/shard_map/ppermute | solution.py:27
  89.3 3.5 collective-permute-done.10
  97.5 4.4 %collective-permute-start.14 = (bf16[32,2048]{1,0:T(8,128)(2,1)S(1)}, bf16[32,2048]{1,0:T(8,128)(2,1)S(1)}, u32[]{:S(2)}, u32[]{:S(2)}) collective-permute-start(bf16[32,2048]{1,0:T(8,128)(2,1)S(1)} %get-tuple-element.50), channel_id=1, source_target_pairs={{0,2},{1,3},{2,0},{3,1},{4,6},{5,7},{6,4},{7,5},{8,10},{9,11},{10,... | collective-permute-start | bytes 393224 | tf_op jit(solution)/shard_map/ppermute | solution.py:27
  101.9 9.9 %collective-permute-done.14 = bf16[32,2048]{1,0:T(8,128)(2,1)S(1)} collective-permute-done((bf16[32,2048]{1,0:T(8,128)(2,1)S(1)}, bf16[32,2048]{1,0:T(8,128)(2,1)S(1)}, u32[]{:S(2)}, u32[]{:S(2)}) %collective-permute-start.14) | collective-permute-done | bytes 131104 | tf_op jit(solution)/shard_map/ppermute | solution.py:27
  117.1 5.0 %collective-permute-done.22 = bf16[32,2048]{1,0:T(8,128)(2,1)S(1)} collective-permute-done((bf16[32,2048]{1,0:T(8,128)(2,1)S(1)}, bf16[32,2048]{1,0:T(8,128)(2,1)S(1)}, u32[]{:S(2)}, u32[]{:S(2)}) %collective-permute-start.22) | collective-permute-done | bytes 131104 | tf_op jit(solution)/shard_map/ppermute | solution.py:180
  129.1 5.9 %collective-permute-start.25 = (bf16[32,2048]{1,0:T(8,128)(2,1)S(1)}, bf16[32,2048]{1,0:T(8,128)(2,1)S(1)}, u32[]{:S(2)}, u32[]{:S(2)}) collective-permute-start(bf16[32,2048]{1,0:T(8,128)(2,1)S(1)} %get-tuple-element.12), channel_id=1, source_target_pairs={{0,2},{1,3},{2,0},{3,1},{4,6},{5,7},{6,4},{7,5},{8,10},{9,11},{10,... | collective-permute-start | bytes 393224 | tf_op jit(solution)/shard_map/ppermute | solution.py:27
  135.0 4.0 %collective-permute-start.24 = (bf16[32,2048]{1,0:T(8,128)(2,1)S(1)}, bf16[32,2048]{1,0:T(8,128)(2,1)S(1)}, u32[]{:S(2)}, u32[]{:S(2)}) collective-permute-start(bf16[32,2048]{1,0:T(8,128)(2,1)S(1)} %get-tuple-element.12), channel_id=1, source_target_pairs={{0,3},{1,0},{2,1},{3,2},{4,7},{5,4},{6,5},{7,6},{8,11},{9,8},{10,9... | collective-permute-start | bytes 393224 | tf_op jit(solution)/shard_map/ppermute | solution.py:27
  139.0 8.3 %collective-permute-done.24 = bf16[32,2048]{1,0:T(8,128)(2,1)S(1)} collective-permute-done((bf16[32,2048]{1,0:T(8,128)(2,1)S(1)}, bf16[32,2048]{1,0:T(8,128)(2,1)S(1)}, u32[]{:S(2)}, u32[]{:S(2)}) %collective-permute-start.24) | collective-permute-done | bytes 131104 | tf_op jit(solution)/shard_map/ppermute | solution.py:27
  150.7 11.8 %collective-permute-done.28 = bf16[128,2048]{1,0:T(8,128)(2,1)S(1)} collective-permute-done((bf16[128,2048]{1,0:T(8,128)(2,1)S(1)}, bf16[128,2048]{1,0:T(8,128)(2,1)S(1)}, u32[]{:S(2)}, u32[]{:S(2)}) %collective-permute-start.28) | collective-permute-done | bytes 524320 | tf_op jit(solution)/shard_map/ppermute | solution.py:27
  166.0 5.2 %collective-permute-done.29 = bf16[128,1024]{1,0:T(8,128)(2,1)S(1)} collective-permute-done((bf16[128,1024]{1,0:T(8,128)(2,1)S(1)}, bf16[128,1024]{1,0:T(8,128)(2,1)S(1)}, u32[]{:S(2)}, u32[]{:S(2)}) %collective-permute-start.29) | collective-permute-done | bytes 262176 | tf_op jit(solution)/shard_map/ppermute | solution.py:27
  171.4 4.1 %collective-permute-done.31 = bf16[512,2048]{1,0:T(8,128)(2,1)S(1)} collective-permute-done((bf16[512,2048]{1,0:T(8,128)(2,1)S(1)}, bf16[512,2048]{1,0:T(8,128)(2,1)S(1)}, u32[]{:S(2)}, u32[]{:S(2)}) %collective-permute-start.31) | collective-permute-done | bytes 2097184 | tf_op jit(solution)/shard_map/ppermute | solution.py:15
  180.0 4.0 %collective-permute-done.32 = bf16[512,2048]{1,0:T(8,128)(2,1)S(1)} collective-permute-done((bf16[512,2048]{1,0:T(8,128)(2,1)S(1)}, bf16[512,2048]{1,0:T(8,128)(2,1)S(1)}, u32[]{:S(2)}, u32[]{:S(2)}) %collective-permute-start.32) | collective-permute-done | bytes 2097184 | tf_op jit(solution)/shard_map/ppermute | solution.py:15
  188.1 6.4 %collective-permute-done.33 = bf16[128,1024]{1,0:T(8,128)(2,1)S(1)} collective-permute-done((bf16[128,1024]{1,0:T(8,128)(2,1)S(1)}, bf16[128,1024]{1,0:T(8,128)(2,1)S(1)}, u32[]{:S(2)}, u32[]{:S(2)}) %collective-permute-start.33) | collective-permute-done | bytes 262176 | tf_op jit(solution)/shard_map/ppermute | solution.py:27
  198.2 10.4 %collective-permute-done.36 = bf16[128,2048]{1,0:T(8,128)(2,1)S(1)} collective-permute-done((bf16[128,2048]{1,0:T(8,128)(2,1)S(1)}, bf16[128,2048]{1,0:T(8,128)(2,1)S(1)}, u32[]{:S(2)}, u32[]{:S(2)}) %collective-permute-start.36) | collective-permute-done | bytes 524320 | tf_op jit(solution)/shard_map/ppermute | solution.py:27
  216.7 5.4 %collective-permute-start.38 = (bf16[32,2048]{1,0:T(8,128)(2,1)S(1)}, bf16[32,2048]{1,0:T(8,128)(2,1)S(1)}, u32[]{:S(2)}, u32[]{:S(2)}) collective-permute-start(bf16[32,2048]{1,0:T(8,128)(2,1)S(1)} %get-tuple-element.47), channel_id=1, source_target_pairs={{0,2},{1,3},{2,0},{3,1},{4,6},{5,7},{6,4},{7,5},{8,10},{9,11},{10,... | collective-permute-start | bytes 393224 | tf_op jit(solution)/shard_map/ppermute | solution.py:27
  222.7 7.2 %collective-permute-done.38 = bf16[32,2048]{1,0:T(8,128)(2,1)S(1)} collective-permute-done((bf16[32,2048]{1,0:T(8,128)(2,1)S(1)}, bf16[32,2048]{1,0:T(8,128)(2,1)S(1)}, u32[]{:S(2)}, u32[]{:S(2)}) %collective-permute-start.38) | collective-permute-done | bytes 131104 | tf_op jit(solution)/shard_map/ppermute | solution.py:27
  235.3 5.2 %collective-permute-done.46 = bf16[32,2048]{1,0:T(8,128)(2,1)S(1)} collective-permute-done((bf16[32,2048]{1,0:T(8,128)(2,1)S(1)}, bf16[32,2048]{1,0:T(8,128)(2,1)S(1)}, u32[]{:S(2)}, u32[]{:S(2)}) %collective-permute-start.46) | collective-permute-done | bytes 131104 | tf_op jit(solution)/shard_map/ppermute | solution.py:180
  247.9 4.0 %collective-permute-start.48 = (bf16[32,2048]{1,0:T(8,128)(2,1)S(1)}, bf16[32,2048]{1,0:T(8,128)(2,1)S(1)}, u32[]{:S(2)}, u32[]{:S(2)}) collective-permute-start(bf16[32,2048]{1,0:T(8,128)(2,1)S(1)} %get-tuple-element.8), channel_id=1, source_target_pairs={{0,3},{1,0},{2,1},{3,2},{4,7},{5,4},{6,5},{7,6},{8,11},{9,8},{10,9... | collective-permute-start | bytes 393224 | tf_op jit(solution)/shard_map/ppermute | solution.py:27
  251.9 4.5 %collective-permute-done.50 = bf16[32,2048]{1,0:T(8,128)(2,1)S(1)} collective-permute-done((bf16[32,2048]{1,0:T(8,128)(2,1)S(1)}, bf16[32,2048]{1,0:T(8,128)(2,1)S(1)}, u32[]{:S(2)}, u32[]{:S(2)}) %collective-permute-start.50) | collective-permute-done | bytes 131104 | tf_op jit(solution)/shard_map/ppermute | solution.py:27
  265.5 11.0 %collective-permute-done.52 = bf16[128,2048]{1,0:T(8,128)(2,1)S(1)} collective-permute-done((bf16[128,2048]{1,0:T(8,128)(2,1)S(1)}, bf16[128,2048]{1,0:T(8,128)(2,1)S(1)}, u32[]{:S(2)}, u32[]{:S(2)}) %collective-permute-start.52) | collective-permute-done | bytes 524320 | tf_op jit(solution)/shard_map/ppermute | solution.py:27
  280.0 4.4 %collective-permute-done.53 = bf16[128,1024]{1,0:T(8,128)(2,1)S(1)} collective-permute-done((bf16[128,1024]{1,0:T(8,128)(2,1)S(1)}, bf16[128,1024]{1,0:T(8,128)(2,1)S(1)}, u32[]{:S(2)}, u32[]{:S(2)}) %collective-permute-start.53) | collective-permute-done | bytes 262176 | tf_op jit(solution)/shard_map/ppermute | solution.py:27
  284.8 4.1 %collective-permute-done.55 = bf16[512,2048]{1,0:T(8,128)(2,1)S(1)} collective-permute-done((bf16[512,2048]{1,0:T(8,128)(2,1)S(1)}, bf16[512,2048]{1,0:T(8,128)(2,1)S(1)}, u32[]{:S(2)}, u32[]{:S(2)}) %collective-permute-start.55) | collective-permute-done | bytes 2097184 | tf_op jit(solution)/shard_map/ppermute | solution.py:15
  292.8 4.0 %collective-permute-done.56 = bf16[512,2048]{1,0:T(8,128)(2,1)S(1)} collective-permute-done((bf16[512,2048]{1,0:T(8,128)(2,1)S(1)}, bf16[512,2048]{1,0:T(8,128)(2,1)S(1)}, u32[]{:S(2)}, u32[]{:S(2)}) %collective-permute-start.56) | collective-permute-done | bytes 2097184 | tf_op jit(solution)/shard_map/ppermute | solution.py:15
  302.7 3.6 %collective-permute-start.18 = (bf16[32,512]{1,0:T(8,128)(2,1)}, bf16[32,512]{1,0:T(8,128)(2,1)}, u32[]{:S(2)}, u32[]{:S(2)}) collective-permute-start(bf16[32,512]{1,0:T(8,128)(2,1)} %bitcast.129), channel_id=1, source_target_pairs={{0,96},{16,112},{32,64},{48,80},{64,32},{80,48},{96,0},{112,16},{1... | collective-permute-start | bytes 98312 | tf_op jit(solution)/shard_map/ppermute | solution.py:15
  317.8 3.7 %collective-permute-start.42 = (bf16[32,512]{1,0:T(8,128)(2,1)S(1)}, bf16[32,512]{1,0:T(8,128)(2,1)S(1)}, u32[]{:S(2)}, u32[]{:S(2)}) collective-permute-start(bf16[32,512]{1,0:T(8,128)(2,1)S(1)} %bitcast.166), channel_id=1, source_target_pairs={{0,96},{16,112},{32,64},{48,80},{64,32},{80,48},{96,0},{112,16},{1... | collective-permute-start | bytes 98312 | tf_op jit(solution)/shard_map/ppermute | solution.py:15
  324.8 3.7 %collective-permute-done.58 = bf16[128,2048]{1,0:T(8,128)(2,1)S(1)} collective-permute-done((bf16[128,2048]{1,0:T(8,128)(2,1)}, bf16[128,2048]{1,0:T(8,128)(2,1)S(1)}, u32[]{:S(2)}, u32[]{:S(2)}) %collective-permute-start.58) | collective-permute-done | bytes 524320 | tf_op jit(solution)/shard_map/ppermute | solution.py:27
  334.0 4.8 %collective-permute-start.62 = (bf16[32,2048]{1,0:T(8,128)(2,1)S(1)}, bf16[32,2048]{1,0:T(8,128)(2,1)S(1)}, u32[]{:S(2)}, u32[]{:S(2)}) collective-permute-start(bf16[32,2048]{1,0:T(8,128)(2,1)S(1)} %get-tuple-element.44), channel_id=1, source_target_pairs={{0,2},{1,3},{2,0},{3,1},{4,6},{5,7},{6,4},{7,5},{8,10},{9,11},{10,... | collective-permute-start | bytes 393224 | tf_op jit(solution)/shard_map/ppermute | solution.py:27
  340.2 6.5 %collective-permute-done.62 = bf16[32,2048]{1,0:T(8,128)(2,1)S(1)} collective-permute-done((bf16[32,2048]{1,0:T(8,128)(2,1)S(1)}, bf16[32,2048]{1,0:T(8,128)(2,1)S(1)}, u32[]{:S(2)}, u32[]{:S(2)}) %collective-permute-start.62) | collective-permute-done | bytes 131104 | tf_op jit(solution)/shard_map/ppermute | solution.py:27
  (251 shorter events, 165.3 us)
Async XLA Ops:
  6.4 12.4 %collective-permute-start.2 = (bf16[32,2048]{1,0:T(8,128)(2,1)S(1)}, bf16[32,2048]{1,0:T(8,128)(2,1)S(1)}, u32[]{:S(2)}, u32[]{:S(2)}) collective-permute-start(bf16[32,2048]{1,0:T(8,128)(2,1)S(1)} %get-tuple-element.17), channel_id=1, source_target_pairs={{0,1},{1,2},{2,3},{3,0},{4,5},{5,6},{6,7},{7,4},{8,9},{9,10},{10,1... | collective-permute-start | bytes 393224 | tf_op jit(solution)/shard_map/ppermute | solution.py:27
  9.7 11.8 %collective-permute-start.1 = (bf16[32,2048]{1,0:T(8,128)(2,1)S(1)}, bf16[32,2048]{1,0:T(8,128)(2,1)S(1)}, u32[]{:S(2)}, u32[]{:S(2)}) collective-permute-start(bf16[32,2048]{1,0:T(8,128)(2,1)S(1)} %get-tuple-element.17), channel_id=1, source_target_pairs={{0,2},{1,3},{2,0},{3,1},{4,6},{5,7},{6,4},{7,5},{8,10},{9,11},{10,... | collective-permute-start | bytes 393224 | tf_op jit(solution)/shard_map/ppermute | solution.py:27
  24.1 13.7 %collective-permute-start.4 = (bf16[128,2048]{1,0:T(8,128)(2,1)S(1)}, bf16[128,2048]{1,0:T(8,128)(2,1)S(1)}, u32[]{:S(2)}, u32[]{:S(2)}) collective-permute-start(bf16[128,2048]{1,0:T(8,128)(2,1)S(1)} %pad_maximum_fusion), channel_id=1, source_target_pairs={{0,4},{1,5},{2,6},{3,7},{4,8},{5,9},{6,10},{7,11},{8,12},{9,13},{1... | collective-permute-start | bytes 1572872 | tf_op jit(solution)/shard_map/ppermute | solution.py:27
  25.8 12.5 %collective-permute-start.3 = (bf16[128,2048]{1,0:T(8,128)(2,1)S(1)}, bf16[128,2048]{1,0:T(8,128)(2,1)S(1)}, u32[]{:S(2)}, u32[]{:S(2)}) collective-permute-start(bf16[128,2048]{1,0:T(8,128)(2,1)S(1)} %pad_maximum_fusion), channel_id=1, source_target_pairs={{0,12},{1,13},{2,14},{3,15},{4,0},{5,1},{6,2},{7,3},{8,4},{9,5},{1... | collective-permute-start | bytes 1572872 | tf_op jit(solution)/shard_map/ppermute | solution.py:27
  64.8 10.2 %collective-permute-start.9 = (bf16[128,1024]{1,0:T(8,128)(2,1)S(1)}, bf16[128,1024]{1,0:T(8,128)(2,1)S(1)}, u32[]{:S(2)}, u32[]{:S(2)}) collective-permute-start(bf16[128,1024]{1,0:T(8,128)(2,1)S(1)} %get-tuple-element.32), channel_id=1, source_target_pairs={{0,4},{1,5},{2,6},{3,7},{4,8},{5,9},{6,10},{7,11},{8,12},{9,13},{1... | collective-permute-start | bytes 786440 | tf_op jit(solution)/shard_map/ppermute | solution.py:27
  75.3 14.0 %collective-permute-start.12 = (bf16[128,2048]{1,0:T(8,128)(2,1)S(1)}, bf16[128,2048]{1,0:T(8,128)(2,1)S(1)}, u32[]{:S(2)}, u32[]{:S(2)}) collective-permute-start(bf16[128,2048]{1,0:T(8,128)(2,1)S(1)} %pad_maximum_fusion.2), channel_id=1, source_target_pairs={{0,12},{1,13},{2,14},{3,15},{4,0},{5,1},{6,2},{7,3},{8,4},{9,5},{1... | collective-permute-start | bytes 1572872 | tf_op jit(solution)/shard_map/ppermute | solution.py:27
  78.5 14.4 %collective-permute-start.10 = (bf16[128,2048]{1,0:T(8,128)(2,1)S(1)}, bf16[128,2048]{1,0:T(8,128)(2,1)S(1)}, u32[]{:S(2)}, u32[]{:S(2)}) collective-permute-start(bf16[128,2048]{1,0:T(8,128)(2,1)S(1)} %pad_maximum_fusion.1), channel_id=1, source_target_pairs={{0,4},{1,5},{2,6},{3,7},{4,8},{5,9},{6,10},{7,11},{8,12},{9,13},{1... | collective-permute-start | bytes 1572872 | tf_op jit(solution)/shard_map/ppermute | solution.py:27
  97.5 14.3 %collective-permute-start.14 = (bf16[32,2048]{1,0:T(8,128)(2,1)S(1)}, bf16[32,2048]{1,0:T(8,128)(2,1)S(1)}, u32[]{:S(2)}, u32[]{:S(2)}) collective-permute-start(bf16[32,2048]{1,0:T(8,128)(2,1)S(1)} %get-tuple-element.50), channel_id=1, source_target_pairs={{0,2},{1,3},{2,0},{3,1},{4,6},{5,7},{6,4},{7,5},{8,10},{9,11},{10,... | collective-permute-start | bytes 393224 | tf_op jit(solution)/shard_map/ppermute | solution.py:27
  111.9 10.2 %collective-permute-start.22 = (bf16[32,2048]{1,0:T(8,128)(2,1)S(1)}, bf16[32,2048]{1,0:T(8,128)(2,1)S(1)}, u32[]{:S(2)}, u32[]{:S(2)}) collective-permute-start(bf16[32,2048]{1,0:T(8,128)(2,1)S(1)} %add_convert_fusion.16), channel_id=1, source_target_pairs={{0,224},{16,240},{32,192},{48,208},{64,160},{80,176},{96,128},{112... | collective-permute-start | bytes 393224 | tf_op jit(solution)/shard_map/ppermute | solution.py:180
  113.2 10.6 %collective-permute-start.21 = (bf16[32,2048]{1,0:T(8,128)(2,1)S(1)}, bf16[32,2048]{1,0:T(8,128)(2,1)S(1)}, u32[]{:S(2)}, u32[]{:S(2)}) collective-permute-start(bf16[32,2048]{1,0:T(8,128)(2,1)S(1)} %add_convert_fusion.16), channel_id=1, source_target_pairs={{0,192},{16,208},{32,224},{48,240},{64,128},{80,144},{96,160},{112... | collective-permute-start | bytes 393224 | tf_op jit(solution)/shard_map/ppermute | solution.py:180
  127.6 11.4 %collective-permute-start.26 = (bf16[32,2048]{1,0:T(8,128)(2,1)S(1)}, bf16[32,2048]{1,0:T(8,128)(2,1)S(1)}, u32[]{:S(2)}, u32[]{:S(2)}) collective-permute-start(bf16[32,2048]{1,0:T(8,128)(2,1)S(1)} %get-tuple-element.12), channel_id=1, source_target_pairs={{0,1},{1,2},{2,3},{3,0},{4,5},{5,6},{6,7},{7,4},{8,9},{9,10},{10,1... | collective-permute-start | bytes 393224 | tf_op jit(solution)/shard_map/ppermute | solution.py:27
  135.0 12.3 %collective-permute-start.24 = (bf16[32,2048]{1,0:T(8,128)(2,1)S(1)}, bf16[32,2048]{1,0:T(8,128)(2,1)S(1)}, u32[]{:S(2)}, u32[]{:S(2)}) collective-permute-start(bf16[32,2048]{1,0:T(8,128)(2,1)S(1)} %get-tuple-element.12), channel_id=1, source_target_pairs={{0,3},{1,0},{2,1},{3,2},{4,7},{5,4},{6,5},{7,6},{8,11},{9,8},{10,9... | collective-permute-start | bytes 393224 | tf_op jit(solution)/shard_map/ppermute | solution.py:27
  147.3 15.2 %collective-permute-start.28 = (bf16[128,2048]{1,0:T(8,128)(2,1)S(1)}, bf16[128,2048]{1,0:T(8,128)(2,1)S(1)}, u32[]{:S(2)}, u32[]{:S(2)}) collective-permute-start(bf16[128,2048]{1,0:T(8,128)(2,1)S(1)} %pad_maximum_fusion.3), channel_id=1, source_target_pairs={{0,4},{1,5},{2,6},{3,7},{4,8},{5,9},{6,10},{7,11},{8,12},{9,13},{1... | collective-permute-start | bytes 1572872 | tf_op jit(solution)/shard_map/ppermute | solution.py:27
  147.4 15.2 %collective-permute-start.27 = (bf16[128,2048]{1,0:T(8,128)(2,1)S(1)}, bf16[128,2048]{1,0:T(8,128)(2,1)S(1)}, u32[]{:S(2)}, u32[]{:S(2)}) collective-permute-start(bf16[128,2048]{1,0:T(8,128)(2,1)S(1)} %pad_maximum_fusion.3), channel_id=1, source_target_pairs={{0,12},{1,13},{2,14},{3,15},{4,0},{5,1},{6,2},{7,3},{8,4},{9,5},{1... | collective-permute-start | bytes 1572872 | tf_op jit(solution)/shard_map/ppermute | solution.py:27
  194.8 13.8 %collective-permute-start.36 = (bf16[128,2048]{1,0:T(8,128)(2,1)S(1)}, bf16[128,2048]{1,0:T(8,128)(2,1)S(1)}, u32[]{:S(2)}, u32[]{:S(2)}) collective-permute-start(bf16[128,2048]{1,0:T(8,128)(2,1)S(1)} %pad_maximum_fusion.5), channel_id=1, source_target_pairs={{0,12},{1,13},{2,14},{3,15},{4,0},{5,1},{6,2},{7,3},{8,4},{9,5},{1... | collective-permute-start | bytes 1572872 | tf_op jit(solution)/shard_map/ppermute | solution.py:27
  198.1 14.0 %collective-permute-start.34 = (bf16[128,2048]{1,0:T(8,128)(2,1)S(1)}, bf16[128,2048]{1,0:T(8,128)(2,1)S(1)}, u32[]{:S(2)}, u32[]{:S(2)}) collective-permute-start(bf16[128,2048]{1,0:T(8,128)(2,1)S(1)} %pad_maximum_fusion.4), channel_id=1, source_target_pairs={{0,4},{1,5},{2,6},{3,7},{4,8},{5,9},{6,10},{7,11},{8,12},{9,13},{1... | collective-permute-start | bytes 1572872 | tf_op jit(solution)/shard_map/ppermute | solution.py:27
  216.7 13.3 %collective-permute-start.38 = (bf16[32,2048]{1,0:T(8,128)(2,1)S(1)}, bf16[32,2048]{1,0:T(8,128)(2,1)S(1)}, u32[]{:S(2)}, u32[]{:S(2)}) collective-permute-start(bf16[32,2048]{1,0:T(8,128)(2,1)S(1)} %get-tuple-element.47), channel_id=1, source_target_pairs={{0,2},{1,3},{2,0},{3,1},{4,6},{5,7},{6,4},{7,5},{8,10},{9,11},{10,... | collective-permute-start | bytes 393224 | tf_op jit(solution)/shard_map/ppermute | solution.py:27
  230.1 10.4 %collective-permute-start.46 = (bf16[32,2048]{1,0:T(8,128)(2,1)S(1)}, bf16[32,2048]{1,0:T(8,128)(2,1)S(1)}, u32[]{:S(2)}, u32[]{:S(2)}) collective-permute-start(bf16[32,2048]{1,0:T(8,128)(2,1)S(1)} %add_convert_fusion.14), channel_id=1, source_target_pairs={{0,224},{16,240},{32,192},{48,208},{64,160},{80,176},{96,128},{112... | collective-permute-start | bytes 393224 | tf_op jit(solution)/shard_map/ppermute | solution.py:180
  231.4 11.0 %collective-permute-start.45 = (bf16[32,2048]{1,0:T(8,128)(2,1)S(1)}, bf16[32,2048]{1,0:T(8,128)(2,1)S(1)}, u32[]{:S(2)}, u32[]{:S(2)}) collective-permute-start(bf16[32,2048]{1,0:T(8,128)(2,1)S(1)} %add_convert_fusion.14), channel_id=1, source_target_pairs={{0,192},{16,208},{32,224},{48,240},{64,128},{80,144},{96,160},{112... | collective-permute-start | bytes 393224 | tf_op jit(solution)/shard_map/ppermute | solution.py:180
  245.1 11.3 %collective-permute-start.50 = (bf16[32,2048]{1,0:T(8,128)(2,1)S(1)}, bf16[32,2048]{1,0:T(8,128)(2,1)S(1)}, u32[]{:S(2)}, u32[]{:S(2)}) collective-permute-start(bf16[32,2048]{1,0:T(8,128)(2,1)S(1)} %get-tuple-element.8), channel_id=1, source_target_pairs={{0,1},{1,2},{2,3},{3,0},{4,5},{5,6},{6,7},{7,4},{8,9},{9,10},{10,1... | collective-permute-start | bytes 393224 | tf_op jit(solution)/shard_map/ppermute | solution.py:27
  245.2 14.4 %collective-permute-start.49 = (bf16[32,2048]{1,0:T(8,128)(2,1)S(1)}, bf16[32,2048]{1,0:T(8,128)(2,1)S(1)}, u32[]{:S(2)}, u32[]{:S(2)}) collective-permute-start(bf16[32,2048]{1,0:T(8,128)(2,1)S(1)} %get-tuple-element.8), channel_id=1, source_target_pairs={{0,2},{1,3},{2,0},{3,1},{4,6},{5,7},{6,4},{7,5},{8,10},{9,11},{10,... | collective-permute-start | bytes 393224 | tf_op jit(solution)/shard_map/ppermute | solution.py:27
  247.9 14.2 %collective-permute-start.48 = (bf16[32,2048]{1,0:T(8,128)(2,1)S(1)}, bf16[32,2048]{1,0:T(8,128)(2,1)S(1)}, u32[]{:S(2)}, u32[]{:S(2)}) collective-permute-start(bf16[32,2048]{1,0:T(8,128)(2,1)S(1)} %get-tuple-element.8), channel_id=1, source_target_pairs={{0,3},{1,0},{2,1},{3,2},{4,7},{5,4},{6,5},{7,6},{8,11},{9,8},{10,9... | collective-permute-start | bytes 393224 | tf_op jit(solution)/shard_map/ppermute | solution.py:27
  262.1 14.4 %collective-permute-start.52 = (bf16[128,2048]{1,0:T(8,128)(2,1)S(1)}, bf16[128,2048]{1,0:T(8,128)(2,1)S(1)}, u32[]{:S(2)}, u32[]{:S(2)}) collective-permute-start(bf16[128,2048]{1,0:T(8,128)(2,1)S(1)} %pad_maximum_fusion.6), channel_id=1, source_target_pairs={{0,4},{1,5},{2,6},{3,7},{4,8},{5,9},{6,10},{7,11},{8,12},{9,13},{1... | collective-permute-start | bytes 1572872 | tf_op jit(solution)/shard_map/ppermute | solution.py:27
  262.2 14.4 %collective-permute-start.51 = (bf16[128,2048]{1,0:T(8,128)(2,1)S(1)}, bf16[128,2048]{1,0:T(8,128)(2,1)S(1)}, u32[]{:S(2)}, u32[]{:S(2)}) collective-permute-start(bf16[128,2048]{1,0:T(8,128)(2,1)S(1)} %pad_maximum_fusion.6), channel_id=1, source_target_pairs={{0,12},{1,13},{2,14},{3,15},{4,0},{5,1},{6,2},{7,3},{8,4},{9,5},{1... | collective-permute-start | bytes 1572872 | tf_op jit(solution)/shard_map/ppermute | solution.py:27
  298.5 10.6 %collective-permute-start.59 = (bf16[128,1024]{1,0:T(8,128)(2,1)}, bf16[128,1024]{1,0:T(8,128)(2,1)}, u32[]{:S(2)}, u32[]{:S(2)}) collective-permute-start(bf16[128,1024]{1,0:T(8,128)(2,1)} %get-tuple-element.21), channel_id=1, source_target_pairs={{0,12},{1,13},{2,14},{3,15},{4,0},{5,1},{6,2},{7,3},{8,4},{9,5},{1... | collective-permute-start | bytes 786440 | tf_op jit(solution)/shard_map/ppermute | solution.py:27
  302.7 12.6 %collective-permute-start.18 = (bf16[32,512]{1,0:T(8,128)(2,1)}, bf16[32,512]{1,0:T(8,128)(2,1)}, u32[]{:S(2)}, u32[]{:S(2)}) collective-permute-start(bf16[32,512]{1,0:T(8,128)(2,1)} %bitcast.129), channel_id=1, source_target_pairs={{0,96},{16,112},{32,64},{48,80},{64,32},{80,48},{96,0},{112,16},{1... | collective-permute-start | bytes 98312 | tf_op jit(solution)/shard_map/ppermute | solution.py:15
  311.2 13.6 %collective-permute-start.60 = (bf16[128,2048]{1,0:T(8,128)(2,1)}, bf16[128,2048]{1,0:T(8,128)(2,1)}, u32[]{:S(2)}, u32[]{:S(2)}) collective-permute-start(bf16[128,2048]{1,0:T(8,128)(2,1)} %pad_maximum_fusion.8), channel_id=1, source_target_pairs={{0,12},{1,13},{2,14},{3,15},{4,0},{5,1},{6,2},{7,3},{8,4},{9,5},{1... | collective-permute-start | bytes 1572872 | tf_op jit(solution)/shard_map/ppermute | solution.py:27
  314.4 14.1 %collective-permute-start.58 = (bf16[128,2048]{1,0:T(8,128)(2,1)}, bf16[128,2048]{1,0:T(8,128)(2,1)S(1)}, u32[]{:S(2)}, u32[]{:S(2)}) collective-permute-start(bf16[128,2048]{1,0:T(8,128)(2,1)} %pad_maximum_fusion.7), channel_id=1, source_target_pairs={{0,4},{1,5},{2,6},{3,7},{4,8},{5,9},{6,10},{7,11},{8,12},{9,13},{1... | collective-permute-start | bytes 1572872 | tf_op jit(solution)/shard_map/ppermute | solution.py:27
  317.8 16.3 %collective-permute-start.42 = (bf16[32,512]{1,0:T(8,128)(2,1)S(1)}, bf16[32,512]{1,0:T(8,128)(2,1)S(1)}, u32[]{:S(2)}, u32[]{:S(2)}) collective-permute-start(bf16[32,512]{1,0:T(8,128)(2,1)S(1)} %bitcast.166), channel_id=1, source_target_pairs={{0,96},{16,112},{32,64},{48,80},{64,32},{80,48},{96,0},{112,16},{1... | collective-permute-start | bytes 98312 | tf_op jit(solution)/shard_map/ppermute | solution.py:15
  321.4 17.4 %collective-permute-start.40 = (bf16[32,512]{1,0:T(8,128)(2,1)S(1)}, bf16[32,512]{1,0:T(8,128)(2,1)S(1)}, u32[]{:S(2)}, u32[]{:S(2)}) collective-permute-start(bf16[32,512]{1,0:T(8,128)(2,1)S(1)} %bitcast.165), channel_id=1, source_target_pairs={{0,32},{16,48},{32,0},{48,16},{64,96},{80,112},{96,64},{112,80},{1... | collective-permute-start | bytes 98312 | tf_op jit(solution)/shard_map/ppermute | solution.py:15
  321.4 17.4 %collective-permute-start.41 = (bf16[32,512]{1,0:T(8,128)(2,1)S(1)}, bf16[32,512]{1,0:T(8,128)(2,1)S(1)}, u32[]{:S(2)}, u32[]{:S(2)}) collective-permute-start(bf16[32,512]{1,0:T(8,128)(2,1)S(1)} %bitcast.164), channel_id=1, source_target_pairs={{0,64},{16,80},{32,96},{48,112},{64,0},{80,16},{96,32},{112,48},{1... | collective-permute-start | bytes 98312 | tf_op jit(solution)/shard_map/ppermute | solution.py:15
  334.0 12.7 %collective-permute-start.62 = (bf16[32,2048]{1,0:T(8,128)(2,1)S(1)}, bf16[32,2048]{1,0:T(8,128)(2,1)S(1)}, u32[]{:S(2)}, u32[]{:S(2)}) collective-permute-start(bf16[32,2048]{1,0:T(8,128)(2,1)S(1)} %get-tuple-element.44), channel_id=1, source_target_pairs={{0,2},{1,3},{2,0},{3,1},{4,6},{5,7},{6,4},{7,5},{8,10},{9,11},{10,... | collective-permute-start | bytes 393224 | tf_op jit(solution)/shard_map/ppermute | solution.py:27
  (53 other events, 520.9 us)

commit v4 on v3

--- a/solution.py
+++ b/solution.py
@@ -149,16 +149,10 @@
         part_own = jnp.dot(active, down_own, preferred_element_type=jnp.float32).astype(jnp.bfloat16)
         pair = (part_own.astype(jnp.float32) + part_from_other.astype(jnp.float32)).astype(jnp.bfloat16)
         reduced = direct_scatter(ring_scatter(pair, outer_ring).astype(jnp.bfloat16), inner_ring).astype(jnp.bfloat16)
-        pieces = reduced.reshape(row_count, x_count, piece_width)
-        own_piece = lax.dynamic_index_in_dim(pieces, xpos, 1, keepdims=False).astype(jnp.float32)
-        for mask in range(1, x_count):
-            sent = lax.dynamic_index_in_dim(pieces, xpos ^ mask, 1, keepdims=False)
-            own_piece = own_piece + swapped(sent, "section", 2 * mask).astype(jnp.float32)
         current_piece = lax.dynamic_index_in_dim(
             current.reshape(row_count, x_count, piece_width), xpos, 1, keepdims=False
         )
-        block = (current_piece + own_piece).astype(jnp.bfloat16)
-        return reduced, block
+        return reduced, current_piece
 
     blocks = []
     received = None
@@ -173,8 +167,8 @@
             is_first = section_layer == 0
             current = jnp.where(is_first, first_current, later_current)
             square_sum = jnp.where(is_first, first_sum, later_sum)
-        reduced, block = tick(current, square_sum)
-        blocks.append(block)
+        reduced, current_piece = tick(current, square_sum)
+        blocks.append((reduced, current_piece))
         if tick_index < tick_count - 1:
             received = [
                 lax.ppermute(
@@ -185,15 +179,17 @@
                 for mask in range(x_count)
             ]
 
-    stacked = jnp.stack(blocks, axis=0)
-    outputs = []
-    for micro_index in range(micro_count):
-        parts = [
-            lax.dynamic_index_in_dim(stacked, micro_index * PIECES + part + section_layer, 0, keepdims=False)
-            for part in range(PIECES)
-        ]
-        outputs.append(jnp.concatenate(parts, axis=0))
-    return jnp.stack(outputs, axis=0)[None]
+    reduced_all = jnp.stack([reduced for reduced, _ in blocks], axis=0)
+    current_all = jnp.stack([piece for _, piece in blocks], axis=0)
+    mine = lax.dynamic_slice_in_dim(reduced_all, section_layer, piece_count, 0)
+    pieces = mine.reshape(piece_count, row_count, x_count, piece_width)
+    total = lax.dynamic_index_in_dim(pieces, xpos, 2, keepdims=False).astype(jnp.float32)
+    for mask in range(1, x_count):
+        sent = lax.dynamic_index_in_dim(pieces, xpos ^ mask, 2, keepdims=False)
+        total = total + swapped(sent, "section", 2 * mask).astype(jnp.float32)
+    base = lax.dynamic_slice_in_dim(current_all, section_layer, piece_count, 0)
+    result = (base + total).astype(jnp.bfloat16)
+    return result.reshape(1, micro_count, tok_dev, piece_width)
 
 
 def solution(mesh):

time: 364 us -> 364 us (level)
  waiting for transfers between devices: 185 us -> 200 us
  starting transfers between devices: 123 us -> 113 us
  local copies, waits for them, and re-layouts: 19.3 us -> 15.5 us
    ppermute x42, waiting for transfers between devices: 143 us -> 156 us  [tp_ring(): return lax.ppermute(value, 'tp', pairs)]
    ppermute x17 -> x11, starting transfers between devices: 17.1 us -> 6.86 us  [swapped(): return lax.ppermute(value, axis, pairs)]
    unnamed x60 -> x55, local copies, waits for them, and re-layouts: 7.45 us -> 6.16 us
    ppermute x17 -> x11, waiting for transfers between devices: 26.1 us -> 27.2 us  [swapped(): return lax.ppermute(value, axis, pairs)]
  transfers between devices with their start and end apart: 67 -> 61, of which waited for: 45 -> 43; matrix products, arithmetic and copies ran while one was open for 5% -> 3% of each run, Pallas kernels for 0% -> 0%
where the time goes in v4:
time: 364 us; the launch traced here: 357 us
  waiting for transfers between devices  200 us (55%)
  starting transfers between devices  113 us (31%)
  matrix products  16 us (4%)
  local copies, waits for them, and re-layouts  15.5 us (4%)
  other arithmetic  11.2 us (3%)
    ppermute x42, waiting for transfers between devices, tp_ring(): return lax.ppermute(value, 'tp', pairs)  156 us
    ppermute x42, starting transfers between devices, tp_ring(): return lax.ppermute(value, 'tp', pairs)  95.6 us
    ppermute x11, waiting for transfers between devices, swapped(): return lax.ppermute(value, axis, pairs)  27.2 us
    ppermute x8, waiting for transfers between devices, body(): lax.ppermute(reduced, 'section', [(source, source + split ^ 2 * mask) for...  16.5 us
    ppermute x8, starting transfers between devices, body(): lax.ppermute(reduced, 'section', [(source, source + split ^ 2 * mask) for...  10.3 us
  transfers between devices with their start and end apart: 61, of which 43 were waited for; matrix products, arithmetic and copies ran while one was open for 3% of the time, Pallas kernels for 0%

profile of v4, /device:TPU:32, one launch (start us, length us, event | category | flops | bytes accessed | tf_op | source)
XLA Modules:
  0.0 357.1 jit_solution(10785829826282307567)
XLA Ops:
  9.8 4.5 %collective-permute-start.1 = (bf16[32,2048]{1,0:T(8,128)(2,1)S(1)}, bf16[32,2048]{1,0:T(8,128)(2,1)S(1)}, u32[]{:S(2)}, u32[]{:S(2)}) collective-permute-start(bf16[32,2048]{1,0:T(8,128)(2,1)S(1)} %get-tuple-element.17), channel_id=1, source_target_pairs={{0,2},{1,3},{2,0},{3,1},{4,6},{5,7},{6,4},{7,5},{8,10},{9,11},{10,... | collective-permute-start | bytes 393224 | tf_op jit(solution)/shard_map/ppermute | solution.py:27
  28.8 9.1 %collective-permute-done.4 = bf16[128,2048]{1,0:T(8,128)(2,1)S(1)} collective-permute-done((bf16[128,2048]{1,0:T(8,128)(2,1)S(1)}, bf16[128,2048]{1,0:T(8,128)(2,1)S(1)}, u32[]{:S(2)}, u32[]{:S(2)}) %collective-permute-start.4) | collective-permute-done | bytes 524320 | tf_op jit(solution)/shard_map/ppermute | solution.py:27
  60.6 3.8 %collective-permute-done.8 = bf16[512,2048]{1,0:T(8,128)(2,1)S(1)} collective-permute-done((bf16[512,2048]{1,0:T(8,128)(2,1)S(1)}, bf16[512,2048]{1,0:T(8,128)(2,1)S(1)}, u32[]{:S(2)}, u32[]{:S(2)}) %collective-permute-start.8) | collective-permute-done | bytes 2097184 | tf_op jit(solution)/shard_map/ppermute | solution.py:15
  68.7 6.8 %collective-permute-done.9 = bf16[128,1024]{1,0:T(8,128)(2,1)S(1)} collective-permute-done((bf16[128,1024]{1,0:T(8,128)(2,1)S(1)}, bf16[128,1024]{1,0:T(8,128)(2,1)S(1)}, u32[]{:S(2)}, u32[]{:S(2)}) %collective-permute-start.9) | collective-permute-done | bytes 262176 | tf_op jit(solution)/shard_map/ppermute | solution.py:27
  79.0 10.7 %collective-permute-done.12 = bf16[128,2048]{1,0:T(8,128)(2,1)S(1)} collective-permute-done((bf16[128,2048]{1,0:T(8,128)(2,1)S(1)}, bf16[128,2048]{1,0:T(8,128)(2,1)S(1)}, u32[]{:S(2)}, u32[]{:S(2)}) %collective-permute-start.12) | collective-permute-done | bytes 524320 | tf_op jit(solution)/shard_map/ppermute | solution.py:27
  89.7 3.5 collective-permute-done.10
  97.9 4.5 %collective-permute-start.14 = (bf16[32,2048]{1,0:T(8,128)(2,1)S(1)}, bf16[32,2048]{1,0:T(8,128)(2,1)S(1)}, u32[]{:S(2)}, u32[]{:S(2)}) collective-permute-start(bf16[32,2048]{1,0:T(8,128)(2,1)S(1)} %get-tuple-element.52), channel_id=1, source_target_pairs={{0,2},{1,3},{2,0},{3,1},{4,6},{5,7},{6,4},{7,5},{8,10},{9,11},{10,... | collective-permute-start | bytes 393224 | tf_op jit(solution)/shard_map/ppermute | solution.py:27
  102.3 9.9 %collective-permute-done.14 = bf16[32,2048]{1,0:T(8,128)(2,1)S(1)} collective-permute-done((bf16[32,2048]{1,0:T(8,128)(2,1)S(1)}, bf16[32,2048]{1,0:T(8,128)(2,1)S(1)}, u32[]{:S(2)}, u32[]{:S(2)}) %collective-permute-start.14) | collective-permute-done | bytes 131104 | tf_op jit(solution)/shard_map/ppermute | solution.py:27
  117.5 5.0 %collective-permute-done.19 = bf16[32,2048]{1,0:T(8,128)(2,1)S(1)} collective-permute-done((bf16[32,2048]{1,0:T(8,128)(2,1)S(1)}, bf16[32,2048]{1,0:T(8,128)(2,1)S(1)}, u32[]{:S(2)}, u32[]{:S(2)}) %collective-permute-start.19) | collective-permute-done | bytes 131104 | tf_op jit(solution)/shard_map/ppermute | solution.py:174
  129.2 5.9 %collective-permute-start.22 = (bf16[32,2048]{1,0:T(8,128)(2,1)S(1)}, bf16[32,2048]{1,0:T(8,128)(2,1)S(1)}, u32[]{:S(2)}, u32[]{:S(2)}) collective-permute-start(bf16[32,2048]{1,0:T(8,128)(2,1)S(1)} %get-tuple-element.12), channel_id=1, source_target_pairs={{0,2},{1,3},{2,0},{3,1},{4,6},{5,7},{6,4},{7,5},{8,10},{9,11},{10,... | collective-permute-start | bytes 393224 | tf_op jit(solution)/shard_map/ppermute | solution.py:27
  135.1 4.0 %collective-permute-start.21 = (bf16[32,2048]{1,0:T(8,128)(2,1)S(1)}, bf16[32,2048]{1,0:T(8,128)(2,1)S(1)}, u32[]{:S(2)}, u32[]{:S(2)}) collective-permute-start(bf16[32,2048]{1,0:T(8,128)(2,1)S(1)} %get-tuple-element.12), channel_id=1, source_target_pairs={{0,3},{1,0},{2,1},{3,2},{4,7},{5,4},{6,5},{7,6},{8,11},{9,8},{10,9... | collective-permute-start | bytes 393224 | tf_op jit(solution)/shard_map/ppermute | solution.py:27
  139.1 8.3 %collective-permute-done.21 = bf16[32,2048]{1,0:T(8,128)(2,1)S(1)} collective-permute-done((bf16[32,2048]{1,0:T(8,128)(2,1)S(1)}, bf16[32,2048]{1,0:T(8,128)(2,1)S(1)}, u32[]{:S(2)}, u32[]{:S(2)}) %collective-permute-start.21) | collective-permute-done | bytes 131104 | tf_op jit(solution)/shard_map/ppermute | solution.py:27
  150.8 11.8 %collective-permute-done.25 = bf16[128,2048]{1,0:T(8,128)(2,1)S(1)} collective-permute-done((bf16[128,2048]{1,0:T(8,128)(2,1)S(1)}, bf16[128,2048]{1,0:T(8,128)(2,1)S(1)}, u32[]{:S(2)}, u32[]{:S(2)}) %collective-permute-start.25) | collective-permute-done | bytes 524320 | tf_op jit(solution)/shard_map/ppermute | solution.py:27
  166.1 5.2 %collective-permute-done.26 = bf16[128,1024]{1,0:T(8,128)(2,1)S(1)} collective-permute-done((bf16[128,1024]{1,0:T(8,128)(2,1)S(1)}, bf16[128,1024]{1,0:T(8,128)(2,1)S(1)}, u32[]{:S(2)}, u32[]{:S(2)}) %collective-permute-start.26) | collective-permute-done | bytes 262176 | tf_op jit(solution)/shard_map/ppermute | solution.py:27
  171.5 4.1 %collective-permute-done.28 = bf16[512,2048]{1,0:T(8,128)(2,1)S(1)} collective-permute-done((bf16[512,2048]{1,0:T(8,128)(2,1)S(1)}, bf16[512,2048]{1,0:T(8,128)(2,1)S(1)}, u32[]{:S(2)}, u32[]{:S(2)}) %collective-permute-start.28) | collective-permute-done | bytes 2097184 | tf_op jit(solution)/shard_map/ppermute | solution.py:15
  180.1 4.0 %collective-permute-done.29 = bf16[512,2048]{1,0:T(8,128)(2,1)S(1)} collective-permute-done((bf16[512,2048]{1,0:T(8,128)(2,1)S(1)}, bf16[512,2048]{1,0:T(8,128)(2,1)S(1)}, u32[]{:S(2)}, u32[]{:S(2)}) %collective-permute-start.29) | collective-permute-done | bytes 2097184 | tf_op jit(solution)/shard_map/ppermute | solution.py:15
  188.3 6.4 %collective-permute-done.30 = bf16[128,1024]{1,0:T(8,128)(2,1)S(1)} collective-permute-done((bf16[128,1024]{1,0:T(8,128)(2,1)S(1)}, bf16[128,1024]{1,0:T(8,128)(2,1)S(1)}, u32[]{:S(2)}, u32[]{:S(2)}) %collective-permute-start.30) | collective-permute-done | bytes 262176 | tf_op jit(solution)/shard_map/ppermute | solution.py:27
  198.4 10.4 %collective-permute-done.33 = bf16[128,2048]{1,0:T(8,128)(2,1)S(1)} collective-permute-done((bf16[128,2048]{1,0:T(8,128)(2,1)S(1)}, bf16[128,2048]{1,0:T(8,128)(2,1)S(1)}, u32[]{:S(2)}, u32[]{:S(2)}) %collective-permute-start.33) | collective-permute-done | bytes 524320 | tf_op jit(solution)/shard_map/ppermute | solution.py:27
  216.8 5.4 %collective-permute-start.35 = (bf16[32,2048]{1,0:T(8,128)(2,1)S(1)}, bf16[32,2048]{1,0:T(8,128)(2,1)S(1)}, u32[]{:S(2)}, u32[]{:S(2)}) collective-permute-start(bf16[32,2048]{1,0:T(8,128)(2,1)S(1)} %get-tuple-element.47), channel_id=1, source_target_pairs={{0,2},{1,3},{2,0},{3,1},{4,6},{5,7},{6,4},{7,5},{8,10},{9,11},{10,... | collective-permute-start | bytes 393224 | tf_op jit(solution)/shard_map/ppermute | solution.py:27
  222.9 7.2 %collective-permute-done.35 = bf16[32,2048]{1,0:T(8,128)(2,1)S(1)} collective-permute-done((bf16[32,2048]{1,0:T(8,128)(2,1)S(1)}, bf16[32,2048]{1,0:T(8,128)(2,1)S(1)}, u32[]{:S(2)}, u32[]{:S(2)}) %collective-permute-start.35) | collective-permute-done | bytes 131104 | tf_op jit(solution)/shard_map/ppermute | solution.py:27
  235.4 5.2 %collective-permute-done.40 = bf16[32,2048]{1,0:T(8,128)(2,1)S(1)} collective-permute-done((bf16[32,2048]{1,0:T(8,128)(2,1)S(1)}, bf16[32,2048]{1,0:T(8,128)(2,1)S(1)}, u32[]{:S(2)}, u32[]{:S(2)}) %collective-permute-start.40) | collective-permute-done | bytes 131104 | tf_op jit(solution)/shard_map/ppermute | solution.py:174
  248.1 4.0 %collective-permute-start.42 = (bf16[32,2048]{1,0:T(8,128)(2,1)S(1)}, bf16[32,2048]{1,0:T(8,128)(2,1)S(1)}, u32[]{:S(2)}, u32[]{:S(2)}) collective-permute-start(bf16[32,2048]{1,0:T(8,128)(2,1)S(1)} %get-tuple-element.8), channel_id=1, source_target_pairs={{0,3},{1,0},{2,1},{3,2},{4,7},{5,4},{6,5},{7,6},{8,11},{9,8},{10,9... | collective-permute-start | bytes 393224 | tf_op jit(solution)/shard_map/ppermute | solution.py:27
  252.2 4.5 %collective-permute-done.44 = bf16[32,2048]{1,0:T(8,128)(2,1)S(1)} collective-permute-done((bf16[32,2048]{1,0:T(8,128)(2,1)S(1)}, bf16[32,2048]{1,0:T(8,128)(2,1)S(1)}, u32[]{:S(2)}, u32[]{:S(2)}) %collective-permute-start.44) | collective-permute-done | bytes 131104 | tf_op jit(solution)/shard_map/ppermute | solution.py:27
  265.7 11.1 %collective-permute-done.46 = bf16[128,2048]{1,0:T(8,128)(2,1)S(1)} collective-permute-done((bf16[128,2048]{1,0:T(8,128)(2,1)S(1)}, bf16[128,2048]{1,0:T(8,128)(2,1)S(1)}, u32[]{:S(2)}, u32[]{:S(2)}) %collective-permute-start.46) | collective-permute-done | bytes 524320 | tf_op jit(solution)/shard_map/ppermute | solution.py:27
  280.3 4.5 %collective-permute-done.47 = bf16[128,1024]{1,0:T(8,128)(2,1)S(1)} collective-permute-done((bf16[128,1024]{1,0:T(8,128)(2,1)S(1)}, bf16[128,1024]{1,0:T(8,128)(2,1)S(1)}, u32[]{:S(2)}, u32[]{:S(2)}) %collective-permute-start.47) | collective-permute-done | bytes 262176 | tf_op jit(solution)/shard_map/ppermute | solution.py:27
  285.2 4.1 %collective-permute-done.49 = bf16[512,2048]{1,0:T(8,128)(2,1)S(1)} collective-permute-done((bf16[512,2048]{1,0:T(8,128)(2,1)S(1)}, bf16[512,2048]{1,0:T(8,128)(2,1)S(1)}, u32[]{:S(2)}, u32[]{:S(2)}) %collective-permute-start.49) | collective-permute-done | bytes 2097184 | tf_op jit(solution)/shard_map/ppermute | solution.py:15
  293.2 4.0 %collective-permute-done.50 = bf16[512,2048]{1,0:T(8,128)(2,1)S(1)} collective-permute-done((bf16[512,2048]{1,0:T(8,128)(2,1)S(1)}, bf16[512,2048]{1,0:T(8,128)(2,1)S(1)}, u32[]{:S(2)}, u32[]{:S(2)}) %collective-permute-start.50) | collective-permute-done | bytes 2097184 | tf_op jit(solution)/shard_map/ppermute | solution.py:15
  301.4 6.4 %collective-permute-done.51 = bf16[128,1024]{1,0:T(8,128)(2,1)S(1)} collective-permute-done((bf16[128,1024]{1,0:T(8,128)(2,1)S(1)}, bf16[128,1024]{1,0:T(8,128)(2,1)S(1)}, u32[]{:S(2)}, u32[]{:S(2)}) %collective-permute-start.51) | collective-permute-done | bytes 262176 | tf_op jit(solution)/shard_map/ppermute | solution.py:27
  312.7 10.0 %collective-permute-done.54 = bf16[128,2048]{1,0:T(8,128)(2,1)} collective-permute-done((bf16[128,2048]{1,0:T(8,128)(2,1)}, bf16[128,2048]{1,0:T(8,128)(2,1)}, u32[]{:S(2)}, u32[]{:S(2)}) %collective-permute-start.54) | collective-permute-done | bytes 524320 | tf_op jit(solution)/shard_map/ppermute | solution.py:27
  322.7 4.2 %collective-permute-done.52 = bf16[128,2048]{1,0:T(8,128)(2,1)} collective-permute-done((bf16[128,2048]{1,0:T(8,128)(2,1)}, bf16[128,2048]{1,0:T(8,128)(2,1)}, u32[]{:S(2)}, u32[]{:S(2)}) %collective-permute-start.52) | collective-permute-done | bytes 524320 | tf_op jit(solution)/shard_map/ppermute | solution.py:27
  332.7 4.6 %collective-permute-start.56 = (bf16[32,2048]{1,0:T(8,128)(2,1)S(1)}, bf16[32,2048]{1,0:T(8,128)(2,1)S(1)}, u32[]{:S(2)}, u32[]{:S(2)}) collective-permute-start(bf16[32,2048]{1,0:T(8,128)(2,1)S(1)} %get-tuple-element.44), channel_id=1, source_target_pairs={{0,2},{1,3},{2,0},{3,1},{4,6},{5,7},{6,4},{7,5},{8,10},{9,11},{10,... | collective-permute-start | bytes 393224 | tf_op jit(solution)/shard_map/ppermute | solution.py:27
  338.8 6.4 %collective-permute-done.56 = bf16[32,2048]{1,0:T(8,128)(2,1)S(1)} collective-permute-done((bf16[32,2048]{1,0:T(8,128)(2,1)S(1)}, bf16[32,2048]{1,0:T(8,128)(2,1)S(1)}, u32[]{:S(2)}, u32[]{:S(2)}) %collective-permute-start.56) | collective-permute-done | bytes 131104 | tf_op jit(solution)/shard_map/ppermute | solution.py:27
  (226 shorter events, 155.9 us)
Async XLA Ops:
  6.5 12.4 %collective-permute-start.2 = (bf16[32,2048]{1,0:T(8,128)(2,1)S(1)}, bf16[32,2048]{1,0:T(8,128)(2,1)S(1)}, u32[]{:S(2)}, u32[]{:S(2)}) collective-permute-start(bf16[32,2048]{1,0:T(8,128)(2,1)S(1)} %get-tuple-element.17), channel_id=1, source_target_pairs={{0,1},{1,2},{2,3},{3,0},{4,5},{5,6},{6,7},{7,4},{8,9},{9,10},{10,1... | collective-permute-start | bytes 393224 | tf_op jit(solution)/shard_map/ppermute | solution.py:27
  9.8 11.8 %collective-permute-start.1 = (bf16[32,2048]{1,0:T(8,128)(2,1)S(1)}, bf16[32,2048]{1,0:T(8,128)(2,1)S(1)}, u32[]{:S(2)}, u32[]{:S(2)}) collective-permute-start(bf16[32,2048]{1,0:T(8,128)(2,1)S(1)} %get-tuple-element.17), channel_id=1, source_target_pairs={{0,2},{1,3},{2,0},{3,1},{4,6},{5,7},{6,4},{7,5},{8,10},{9,11},{10,... | collective-permute-start | bytes 393224 | tf_op jit(solution)/shard_map/ppermute | solution.py:27
  14.3 9.9 %collective-permute-start = (bf16[32,2048]{1,0:T(8,128)(2,1)S(1)}, bf16[32,2048]{1,0:T(8,128)(2,1)S(1)}, u32[]{:S(2)}, u32[]{:S(2)}) collective-permute-start(bf16[32,2048]{1,0:T(8,128)(2,1)S(1)} %get-tuple-element.17), channel_id=1, source_target_pairs={{0,3},{1,0},{2,1},{3,2},{4,7},{5,4},{6,5},{7,6},{8,11},{9,8},{10,9... | collective-permute-start | bytes 393224 | tf_op jit(solution)/shard_map/ppermute | solution.py:27
  24.2 13.7 %collective-permute-start.4 = (bf16[128,2048]{1,0:T(8,128)(2,1)S(1)}, bf16[128,2048]{1,0:T(8,128)(2,1)S(1)}, u32[]{:S(2)}, u32[]{:S(2)}) collective-permute-start(bf16[128,2048]{1,0:T(8,128)(2,1)S(1)} %pad_maximum_fusion), channel_id=1, source_target_pairs={{0,4},{1,5},{2,6},{3,7},{4,8},{5,9},{6,10},{7,11},{8,12},{9,13},{1... | collective-permute-start | bytes 1572872 | tf_op jit(solution)/shard_map/ppermute | solution.py:27
  25.8 12.5 %collective-permute-start.3 = (bf16[128,2048]{1,0:T(8,128)(2,1)S(1)}, bf16[128,2048]{1,0:T(8,128)(2,1)S(1)}, u32[]{:S(2)}, u32[]{:S(2)}) collective-permute-start(bf16[128,2048]{1,0:T(8,128)(2,1)S(1)} %pad_maximum_fusion), channel_id=1, source_target_pairs={{0,12},{1,13},{2,14},{3,15},{4,0},{5,1},{6,2},{7,3},{8,4},{9,5},{1... | collective-permute-start | bytes 1572872 | tf_op jit(solution)/shard_map/ppermute | solution.py:27
  65.2 10.3 %collective-permute-start.9 = (bf16[128,1024]{1,0:T(8,128)(2,1)S(1)}, bf16[128,1024]{1,0:T(8,128)(2,1)S(1)}, u32[]{:S(2)}, u32[]{:S(2)}) collective-permute-start(bf16[128,1024]{1,0:T(8,128)(2,1)S(1)} %get-tuple-element.32), channel_id=1, source_target_pairs={{0,4},{1,5},{2,6},{3,7},{4,8},{5,9},{6,10},{7,11},{8,12},{9,13},{1... | collective-permute-start | bytes 786440 | tf_op jit(solution)/shard_map/ppermute | solution.py:27
  75.7 14.0 %collective-permute-start.12 = (bf16[128,2048]{1,0:T(8,128)(2,1)S(1)}, bf16[128,2048]{1,0:T(8,128)(2,1)S(1)}, u32[]{:S(2)}, u32[]{:S(2)}) collective-permute-start(bf16[128,2048]{1,0:T(8,128)(2,1)S(1)} %pad_maximum_fusion.2), channel_id=1, source_target_pairs={{0,12},{1,13},{2,14},{3,15},{4,0},{5,1},{6,2},{7,3},{8,4},{9,5},{1... | collective-permute-start | bytes 1572872 | tf_op jit(solution)/shard_map/ppermute | solution.py:27
  78.9 14.4 %collective-permute-start.10 = (bf16[128,2048]{1,0:T(8,128)(2,1)S(1)}, bf16[128,2048]{1,0:T(8,128)(2,1)S(1)}, u32[]{:S(2)}, u32[]{:S(2)}) collective-permute-start(bf16[128,2048]{1,0:T(8,128)(2,1)S(1)} %pad_maximum_fusion.1), channel_id=1, source_target_pairs={{0,4},{1,5},{2,6},{3,7},{4,8},{5,9},{6,10},{7,11},{8,12},{9,13},{1... | collective-permute-start | bytes 1572872 | tf_op jit(solution)/shard_map/ppermute | solution.py:27
  97.9 14.4 %collective-permute-start.14 = (bf16[32,2048]{1,0:T(8,128)(2,1)S(1)}, bf16[32,2048]{1,0:T(8,128)(2,1)S(1)}, u32[]{:S(2)}, u32[]{:S(2)}) collective-permute-start(bf16[32,2048]{1,0:T(8,128)(2,1)S(1)} %get-tuple-element.52), channel_id=1, source_target_pairs={{0,2},{1,3},{2,0},{3,1},{4,6},{5,7},{6,4},{7,5},{8,10},{9,11},{10,... | collective-permute-start | bytes 393224 | tf_op jit(solution)/shard_map/ppermute | solution.py:27
  112.3 10.2 %collective-permute-start.19 = (bf16[32,2048]{1,0:T(8,128)(2,1)S(1)}, bf16[32,2048]{1,0:T(8,128)(2,1)S(1)}, u32[]{:S(2)}, u32[]{:S(2)}) collective-permute-start(bf16[32,2048]{1,0:T(8,128)(2,1)S(1)} %add_convert_fusion.16), channel_id=1, source_target_pairs={{0,224},{16,240},{32,192},{48,208},{64,160},{80,176},{96,128},{112... | collective-permute-start | bytes 393224 | tf_op jit(solution)/shard_map/ppermute | solution.py:174
  113.6 10.6 %collective-permute-start.18 = (bf16[32,2048]{1,0:T(8,128)(2,1)S(1)}, bf16[32,2048]{1,0:T(8,128)(2,1)S(1)}, u32[]{:S(2)}, u32[]{:S(2)}) collective-permute-start(bf16[32,2048]{1,0:T(8,128)(2,1)S(1)} %add_convert_fusion.16), channel_id=1, source_target_pairs={{0,192},{16,208},{32,224},{48,240},{64,128},{80,144},{96,160},{112... | collective-permute-start | bytes 393224 | tf_op jit(solution)/shard_map/ppermute | solution.py:174
  127.9 11.2 %collective-permute-start.23 = (bf16[32,2048]{1,0:T(8,128)(2,1)S(1)}, bf16[32,2048]{1,0:T(8,128)(2,1)S(1)}, u32[]{:S(2)}, u32[]{:S(2)}) collective-permute-start(bf16[32,2048]{1,0:T(8,128)(2,1)S(1)} %get-tuple-element.12), channel_id=1, source_target_pairs={{0,1},{1,2},{2,3},{3,0},{4,5},{5,6},{6,7},{7,4},{8,9},{9,10},{10,1... | collective-permute-start | bytes 393224 | tf_op jit(solution)/shard_map/ppermute | solution.py:27
  129.2 9.9 %collective-permute-start.22 = (bf16[32,2048]{1,0:T(8,128)(2,1)S(1)}, bf16[32,2048]{1,0:T(8,128)(2,1)S(1)}, u32[]{:S(2)}, u32[]{:S(2)}) collective-permute-start(bf16[32,2048]{1,0:T(8,128)(2,1)S(1)} %get-tuple-element.12), channel_id=1, source_target_pairs={{0,2},{1,3},{2,0},{3,1},{4,6},{5,7},{6,4},{7,5},{8,10},{9,11},{10,... | collective-permute-start | bytes 393224 | tf_op jit(solution)/shard_map/ppermute | solution.py:27
  135.1 12.3 %collective-permute-start.21 = (bf16[32,2048]{1,0:T(8,128)(2,1)S(1)}, bf16[32,2048]{1,0:T(8,128)(2,1)S(1)}, u32[]{:S(2)}, u32[]{:S(2)}) collective-permute-start(bf16[32,2048]{1,0:T(8,128)(2,1)S(1)} %get-tuple-element.12), channel_id=1, source_target_pairs={{0,3},{1,0},{2,1},{3,2},{4,7},{5,4},{6,5},{7,6},{8,11},{9,8},{10,9... | collective-permute-start | bytes 393224 | tf_op jit(solution)/shard_map/ppermute | solution.py:27
  147.4 15.2 %collective-permute-start.25 = (bf16[128,2048]{1,0:T(8,128)(2,1)S(1)}, bf16[128,2048]{1,0:T(8,128)(2,1)S(1)}, u32[]{:S(2)}, u32[]{:S(2)}) collective-permute-start(bf16[128,2048]{1,0:T(8,128)(2,1)S(1)} %pad_maximum_fusion.3), channel_id=1, source_target_pairs={{0,4},{1,5},{2,6},{3,7},{4,8},{5,9},{6,10},{7,11},{8,12},{9,13},{1... | collective-permute-start | bytes 1572872 | tf_op jit(solution)/shard_map/ppermute | solution.py:27
  147.5 15.2 %collective-permute-start.24 = (bf16[128,2048]{1,0:T(8,128)(2,1)S(1)}, bf16[128,2048]{1,0:T(8,128)(2,1)S(1)}, u32[]{:S(2)}, u32[]{:S(2)}) collective-permute-start(bf16[128,2048]{1,0:T(8,128)(2,1)S(1)} %pad_maximum_fusion.3), channel_id=1, source_target_pairs={{0,12},{1,13},{2,14},{3,15},{4,0},{5,1},{6,2},{7,3},{8,4},{9,5},{1... | collective-permute-start | bytes 1572872 | tf_op jit(solution)/shard_map/ppermute | solution.py:27
  195.0 13.9 %collective-permute-start.33 = (bf16[128,2048]{1,0:T(8,128)(2,1)S(1)}, bf16[128,2048]{1,0:T(8,128)(2,1)S(1)}, u32[]{:S(2)}, u32[]{:S(2)}) collective-permute-start(bf16[128,2048]{1,0:T(8,128)(2,1)S(1)} %pad_maximum_fusion.5), channel_id=1, source_target_pairs={{0,12},{1,13},{2,14},{3,15},{4,0},{5,1},{6,2},{7,3},{8,4},{9,5},{1... | collective-permute-start | bytes 1572872 | tf_op jit(solution)/shard_map/ppermute | solution.py:27
  198.3 14.0 %collective-permute-start.31 = (bf16[128,2048]{1,0:T(8,128)(2,1)S(1)}, bf16[128,2048]{1,0:T(8,128)(2,1)S(1)}, u32[]{:S(2)}, u32[]{:S(2)}) collective-permute-start(bf16[128,2048]{1,0:T(8,128)(2,1)S(1)} %pad_maximum_fusion.4), channel_id=1, source_target_pairs={{0,4},{1,5},{2,6},{3,7},{4,8},{5,9},{6,10},{7,11},{8,12},{9,13},{1... | collective-permute-start | bytes 1572872 | tf_op jit(solution)/shard_map/ppermute | solution.py:27
  212.6 9.9 %collective-permute-start.34 = (bf16[32,2048]{1,0:T(8,128)(2,1)S(1)}, bf16[32,2048]{1,0:T(8,128)(2,1)S(1)}, u32[]{:S(2)}, u32[]{:S(2)}) collective-permute-start(bf16[32,2048]{1,0:T(8,128)(2,1)S(1)} %get-tuple-element.45), channel_id=1, source_target_pairs={{0,1},{1,2},{2,3},{3,0},{4,5},{5,6},{6,7},{7,4},{8,9},{9,10},{10,1... | collective-permute-start | bytes 393224 | tf_op jit(solution)/shard_map/ppermute | solution.py:27
  216.8 13.3 %collective-permute-start.35 = (bf16[32,2048]{1,0:T(8,128)(2,1)S(1)}, bf16[32,2048]{1,0:T(8,128)(2,1)S(1)}, u32[]{:S(2)}, u32[]{:S(2)}) collective-permute-start(bf16[32,2048]{1,0:T(8,128)(2,1)S(1)} %get-tuple-element.47), channel_id=1, source_target_pairs={{0,2},{1,3},{2,0},{3,1},{4,6},{5,7},{6,4},{7,5},{8,10},{9,11},{10,... | collective-permute-start | bytes 393224 | tf_op jit(solution)/shard_map/ppermute | solution.py:27
  230.2 10.4 %collective-permute-start.40 = (bf16[32,2048]{1,0:T(8,128)(2,1)S(1)}, bf16[32,2048]{1,0:T(8,128)(2,1)S(1)}, u32[]{:S(2)}, u32[]{:S(2)}) collective-permute-start(bf16[32,2048]{1,0:T(8,128)(2,1)S(1)} %add_convert_fusion.14), channel_id=1, source_target_pairs={{0,224},{16,240},{32,192},{48,208},{64,160},{80,176},{96,128},{112... | collective-permute-start | bytes 393224 | tf_op jit(solution)/shard_map/ppermute | solution.py:174
  231.5 11.0 %collective-permute-start.39 = (bf16[32,2048]{1,0:T(8,128)(2,1)S(1)}, bf16[32,2048]{1,0:T(8,128)(2,1)S(1)}, u32[]{:S(2)}, u32[]{:S(2)}) collective-permute-start(bf16[32,2048]{1,0:T(8,128)(2,1)S(1)} %add_convert_fusion.14), channel_id=1, source_target_pairs={{0,192},{16,208},{32,224},{48,240},{64,128},{80,144},{96,160},{112... | collective-permute-start | bytes 393224 | tf_op jit(solution)/shard_map/ppermute | solution.py:174
  245.3 11.4 %collective-permute-start.44 = (bf16[32,2048]{1,0:T(8,128)(2,1)S(1)}, bf16[32,2048]{1,0:T(8,128)(2,1)S(1)}, u32[]{:S(2)}, u32[]{:S(2)}) collective-permute-start(bf16[32,2048]{1,0:T(8,128)(2,1)S(1)} %get-tuple-element.8), channel_id=1, source_target_pairs={{0,1},{1,2},{2,3},{3,0},{4,5},{5,6},{6,7},{7,4},{8,9},{9,10},{10,1... | collective-permute-start | bytes 393224 | tf_op jit(solution)/shard_map/ppermute | solution.py:27
  245.4 14.5 %collective-permute-start.43 = (bf16[32,2048]{1,0:T(8,128)(2,1)S(1)}, bf16[32,2048]{1,0:T(8,128)(2,1)S(1)}, u32[]{:S(2)}, u32[]{:S(2)}) collective-permute-start(bf16[32,2048]{1,0:T(8,128)(2,1)S(1)} %get-tuple-element.8), channel_id=1, source_target_pairs={{0,2},{1,3},{2,0},{3,1},{4,6},{5,7},{6,4},{7,5},{8,10},{9,11},{10,... | collective-permute-start | bytes 393224 | tf_op jit(solution)/shard_map/ppermute | solution.py:27
  248.1 14.2 %collective-permute-start.42 = (bf16[32,2048]{1,0:T(8,128)(2,1)S(1)}, bf16[32,2048]{1,0:T(8,128)(2,1)S(1)}, u32[]{:S(2)}, u32[]{:S(2)}) collective-permute-start(bf16[32,2048]{1,0:T(8,128)(2,1)S(1)} %get-tuple-element.8), channel_id=1, source_target_pairs={{0,3},{1,0},{2,1},{3,2},{4,7},{5,4},{6,5},{7,6},{8,11},{9,8},{10,9... | collective-permute-start | bytes 393224 | tf_op jit(solution)/shard_map/ppermute | solution.py:27
  262.4 14.4 %collective-permute-start.46 = (bf16[128,2048]{1,0:T(8,128)(2,1)S(1)}, bf16[128,2048]{1,0:T(8,128)(2,1)S(1)}, u32[]{:S(2)}, u32[]{:S(2)}) collective-permute-start(bf16[128,2048]{1,0:T(8,128)(2,1)S(1)} %pad_maximum_fusion.6), channel_id=1, source_target_pairs={{0,4},{1,5},{2,6},{3,7},{4,8},{5,9},{6,10},{7,11},{8,12},{9,13},{1... | collective-permute-start | bytes 1572872 | tf_op jit(solution)/shard_map/ppermute | solution.py:27
  262.5 14.5 %collective-permute-start.45 = (bf16[128,2048]{1,0:T(8,128)(2,1)S(1)}, bf16[128,2048]{1,0:T(8,128)(2,1)S(1)}, u32[]{:S(2)}, u32[]{:S(2)}) collective-permute-start(bf16[128,2048]{1,0:T(8,128)(2,1)S(1)} %pad_maximum_fusion.6), channel_id=1, source_target_pairs={{0,12},{1,13},{2,14},{3,15},{4,0},{5,1},{6,2},{7,3},{8,4},{9,5},{1... | collective-permute-start | bytes 1572872 | tf_op jit(solution)/shard_map/ppermute | solution.py:27
  298.0 9.8 %collective-permute-start.51 = (bf16[128,1024]{1,0:T(8,128)(2,1)S(1)}, bf16[128,1024]{1,0:T(8,128)(2,1)S(1)}, u32[]{:S(2)}, u32[]{:S(2)}) collective-permute-start(bf16[128,1024]{1,0:T(8,128)(2,1)S(1)} %get-tuple-element.20), channel_id=1, source_target_pairs={{0,4},{1,5},{2,6},{3,7},{4,8},{5,9},{6,10},{7,11},{8,12},{9,13},{1... | collective-permute-start | bytes 786440 | tf_op jit(solution)/shard_map/ppermute | solution.py:27
  308.8 13.9 %collective-permute-start.54 = (bf16[128,2048]{1,0:T(8,128)(2,1)}, bf16[128,2048]{1,0:T(8,128)(2,1)}, u32[]{:S(2)}, u32[]{:S(2)}) collective-permute-start(bf16[128,2048]{1,0:T(8,128)(2,1)} %pad_maximum_fusion.8), channel_id=1, source_target_pairs={{0,12},{1,13},{2,14},{3,15},{4,0},{5,1},{6,2},{7,3},{8,4},{9,5},{1... | collective-permute-start | bytes 1572872 | tf_op jit(solution)/shard_map/ppermute | solution.py:27
  312.7 14.3 %collective-permute-start.52 = (bf16[128,2048]{1,0:T(8,128)(2,1)}, bf16[128,2048]{1,0:T(8,128)(2,1)}, u32[]{:S(2)}, u32[]{:S(2)}) collective-permute-start(bf16[128,2048]{1,0:T(8,128)(2,1)} %pad_maximum_fusion.7), channel_id=1, source_target_pairs={{0,4},{1,5},{2,6},{3,7},{4,8},{5,9},{6,10},{7,11},{8,12},{9,13},{1... | collective-permute-start | bytes 1572872 | tf_op jit(solution)/shard_map/ppermute | solution.py:27
  328.5 10.3 %collective-permute-start.55 = (bf16[32,2048]{1,0:T(8,128)(2,1)S(1)}, bf16[32,2048]{1,0:T(8,128)(2,1)S(1)}, u32[]{:S(2)}, u32[]{:S(2)}) collective-permute-start(bf16[32,2048]{1,0:T(8,128)(2,1)S(1)} %get-tuple-element.42), channel_id=1, source_target_pairs={{0,1},{1,2},{2,3},{3,0},{4,5},{5,6},{6,7},{7,4},{8,9},{9,10},{10,1... | collective-permute-start | bytes 393224 | tf_op jit(solution)/shard_map/ppermute | solution.py:27
  332.7 12.5 %collective-permute-start.56 = (bf16[32,2048]{1,0:T(8,128)(2,1)S(1)}, bf16[32,2048]{1,0:T(8,128)(2,1)S(1)}, u32[]{:S(2)}, u32[]{:S(2)}) collective-permute-start(bf16[32,2048]{1,0:T(8,128)(2,1)S(1)} %get-tuple-element.44), channel_id=1, source_target_pairs={{0,2},{1,3},{2,0},{3,1},{4,6},{5,7},{6,4},{7,5},{8,10},{9,11},{10,... | collective-permute-start | bytes 393224 | tf_op jit(solution)/shard_map/ppermute | solution.py:27
  (46 other events, 533.7 us)
